TPU v7x, 32 devices: a whole 2x2x4 slice. The times are simulated.
32 devices in a mesh: front: 8 (over z, x), grp: 4 (over y, core).
Axes of the slice: x: 2, y: 2, z: 4, core: 2. Of those that a mesh axis runs over, the one named last changes fastest.
Arguments:
- front_block: float32 [8, 16384, 1408], P('front', 'grp'), as said below
- child_blocks: float32 [8, 4, 4, 16, 1408], P('front', 'grp'), may hold values from -0.5 to 0.5
- child_rows: int32 [8, 4, 4, 16], P('front', 'grp'), may hold values from 0 to 4095
- child_dest: int32 [8, 4, 4, 1], P('front', 'grp'), may hold values from 0 to 7; in each aligned block of 4 rows (0 to 3, 4 to 7, ..., all dimensions but the last counted through in order) at most 2 rows name the same one
- panel_owner: int32 [8], P('front'), may hold values from 0 to 3
Outputs:
- panel_factor: float32 [8, 16384, 512], P('front', 'grp')
- schur_block: float32 [8, 16384, 896], P('front', 'grp')
Inputs may be any that keep to these rules, and one draw needn't show every extreme that they name: `child_dest`: among the 4 blocks of one device no front is named more than 2 times, and in every draw some device names some front exactly 2 times. `front_block`: for every front and row block, the first 512 rows' leading 512 x 512 block has a positive diagonal that dominates; other entries lie within -2.3 to 2.3.
All inputs are finite; a program needn't handle non-finite values.
Results may differ from a plain program's by a relative error of at most 0.0003.
Values sent between devices are 32-bit elements; how exact they have to be, the bound alone decides.
No kernel may reach another device: no remote copies, remote signals or barrier semaphores. Data moves between devices by JAX's collectives and lax.ppermute only.
A program may use at most 128 MiB of HBM per device.

v0:
```python
import jax
import jax.numpy as jnp
from jax import lax
from jax.sharding import PartitionSpec as P

PB = 512
CAP = 2


def spread(array, axis, root):
    mine = lax.axis_index(axis) == root
    return lax.psum(jnp.where(mine, array, jnp.zeros_like(array)), axis)


def right_solve(factor, rows):
    return lax.linalg.triangular_solve(factor, rows, left_side=False, lower=True, transpose_a=True)


def pack_slots(values, slot_index, front_count):
    empty = jnp.zeros((front_count * CAP,) + values.shape[1:], values.dtype)
    filled = empty.at[slot_index].set(values)
    return filled.reshape((front_count, CAP) + values.shape[1:])


def local(front_block, child_blocks, child_rows, child_dest, panel_owner):
    local_rows = front_block[0]
    front_count = lax.axis_size("front")
    blocks = child_blocks[0, 0]
    row_lists = child_rows[0, 0]
    target_front = child_dest[0, 0, :, 0]
    block_count = target_front.shape[0]
    position = jnp.arange(block_count, dtype=jnp.int32)
    same_front = target_front[:, None] == target_front[None, :]
    earlier = position[None, :] < position[:, None]
    slot_index = target_front * CAP + jnp.sum((same_front & earlier).astype(jnp.int32), axis=1)
    send_rows = pack_slots(row_lists, slot_index, front_count)
    panel_cols = PB
    send_panel = pack_slots(blocks[:, :, :panel_cols], slot_index, front_count)
    got_panel, got_rows = (
        lax.all_to_all(send_panel, "front", split_axis=0, concat_axis=0, tiled=True),
        lax.all_to_all(send_rows, "front", split_axis=0, concat_axis=0, tiled=True),
    )
    flat_rows = got_rows.reshape(-1)
    panel_part = local_rows[:, :panel_cols].at[flat_rows].add(got_panel.reshape(-1, panel_cols))
    local_rows = jnp.concatenate([panel_part, local_rows[:, panel_cols:]], axis=1)
    send_trail = pack_slots(blocks[:, :, panel_cols:], slot_index, front_count)
    trailing_rows = lax.all_to_all(send_trail, "front", split_axis=0, concat_axis=0, tiled=True)
    win_cols = local_rows.shape[1] - panel_cols
    owner_index = panel_owner[0]
    is_owner = lax.axis_index("grp") == owner_index
    pivot_block = spread(local_rows[:panel_cols, :panel_cols], "grp", owner_index)
    symmetric = 0.5 * (pivot_block + pivot_block.T)
    pivot_factor = jnp.linalg.cholesky(symmetric)
    solved = right_solve(pivot_factor, local_rows[:, :panel_cols])
    window = spread(solved[panel_cols : panel_cols + win_cols], "grp", owner_index)
    schur_part = local_rows[:, panel_cols:] - jnp.dot(
        solved, window.T, precision=lax.Precision.HIGHEST
    )
    schur_part = schur_part.at[flat_rows].add(trailing_rows.reshape(-1, win_cols))
    top_rows = jnp.where(is_owner, pivot_factor, solved[:panel_cols])
    panel_rows = jnp.concatenate([top_rows, solved[panel_cols:]], axis=0)
    return (panel_rows[None], schur_part[None])


def solution(mesh):
    placed = (
        P("front", "grp", None),
        P("front", "grp", None, None, None),
        P("front", "grp", None, None),
        P("front", "grp", None, None),
        P("front"),
    )
    return jax.shard_map(
        local,
        mesh=mesh,
        in_specs=placed,
        out_specs=(P("front", "grp", None), P("front", "grp", None)),
        check_vma=False,
    )
```

profile of v0, /device:TPU:0, one launch (start us, length us, event | category | flops | bytes accessed | tf_op | source)
XLA Modules:
  0.0 377.0 jit_solution(13516703856548817198)
XLA Ops:
  7.2 0.9 convert_reduce_fusion
  8.1 0.7 fusion.38
  8.8 1.2 scatter_custom_fusion
  9.9 7.3 %all-to-all-start = ((s32[8,2,16]{2,1,0:T(2,128)}), s32[8,2,16]{2,1,0:T(2,128)S(1)}, u32[]{:S(2)}, u32[]{:S(2)}) async-start(s32[8,2,16]{2,1,0:T(2,128)} %bitcast.7), calls=%async_computation | async-start | bytes 16384 | tf_op jit(solution)/shard_map/all_to_all | solution.py:41
  17.2 0.9 slice.147
  18.1 0.9 broadcast_in_dim.31
  18.9 2.0 scatter_fusion
  21.0 2.7 all-to-all-done
  23.7 3.5 all-to-all-start.1
  27.9 7.9 %slice.146 = f32[4096,512]{1,0:T(8,128)} slice(f32[4096,1408]{1,0:T(8,128)} %bitcast.80), slice={[0:4096], [0:512]} | slice | bytes 16777216 | tf_op jit(solution)/shard_map/slice | solution.py:44
  35.9 5.0 %all-to-all-done.1 = f32[8,2,16,512]{3,2,1,0:T(8,128)S(1)} async-done(((f32[8,2,16,512]{3,2,1,0:T(8,128)}), f32[8,2,16,512]{3,2,1,0:T(8,128)S(1)}, u32[]{:S(2)}, u32[]{:S(2)}) %all-to-all-start.1) | async-done | bytes 524320 | tf_op jit(solution)/shard_map/all_to_all | solution.py:40
  40.9 9.0 %scatter_fusion.1 = f32[4096,512]{1,0:T(8,128)} fusion(f32[4096,512]{1,0:T(8,128)} %slice.146, s32[256]{0:T(256)S(1)} %bitcast.85, f32[256,512]{1,0:T(8,128)S(1)} %bitcast.82), kind=kCustom, calls=%fused_computation.2 | custom fusion | flops 131072 | bytes 1573888 | tf_op jit(solution)/shard_map/scatter-add | solution.py:44
  50.0 1.3 slice.148
  51.6 1.1 broadcast_select_fusion
  52.7 1.0 broadcast_in_dim.35
  53.7 2.2 scatter_fusion.2
  55.9 4.2 %all-to-all-start.2 = ((f32[8,2,16,896]{3,2,1,0:T(8,128)}), f32[8,2,16,896]{3,2,1,0:T(8,128)}, u32[]{:S(2)}, u32[]{:S(2)}) async-start(f32[8,2,16,896]{3,2,1,0:T(8,128)} %bitcast.25), calls=%async_computation.2 | async-start | bytes 1835008 | tf_op jit(solution)/shard_map/all_to_all | solution.py:47
  60.4 27.7 %all-reduce.4.cloned.1.call-done = f32[512,512]{0,1:T(8,128)} async-done(((f32[512,512]{0,1:T(8,128)}), f32[512,512]{0,1:T(8,128)}) %all-reduce.4.cloned.1.call-update) | async-done | bytes 1048592 | tf_op jit(solution)/shard_map/psum | solution.py:12
  88.0 1.6 copy.34
  90.5 11.7 %cholesky.103 = f32[128,128]{1,0:T(8,128)S(1)} custom-call(f32[128,128]{1,0:T(8,128)S(1)} %cholesky.263), custom_call_target="Cholesky" | custom-call | tf_op jit(solution)/shard_map/jit(cholesky)/cholesky | solution.py:53
  102.4 9.8 %custom-call.30 = f32[1,128,128]{1,2,0:T(8,128)S(1)} custom-call(f32[1,128,128]{2,1,0:T(8,128)S(1)} %get-tuple-element.43), custom_call_target="InvertDiagBlocksLowerTriangular" | custom-call | tf_op jit(solution)/shard_map/jit(cholesky)/cholesky | solution.py:53
  113.0 11.7 %cholesky.215 = f32[128,128]{1,0:T(8,128)S(1)} custom-call(f32[128,128]{1,0:T(8,128)S(1)} %cholesky.267), custom_call_target="Cholesky" | custom-call | tf_op jit(solution)/shard_map/jit(cholesky)/cholesky | solution.py:53
  124.9 10.1 %custom-call.31 = f32[1,128,128]{1,2,0:T(8,128)S(1)} custom-call(f32[1,128,128]{2,1,0:T(8,128)S(1)} %get-tuple-element.41), custom_call_target="InvertDiagBlocksLowerTriangular" | custom-call | tf_op jit(solution)/shard_map/jit(cholesky)/cholesky | solution.py:53
  135.5 1.5 convolution_subtract_fusion.3
  137.0 11.7 %cholesky.236 = f32[128,128]{1,0:T(8,128)S(1)} custom-call(f32[128,128]{1,0:T(8,128)S(1)} %cholesky.272), custom_call_target="Cholesky" | custom-call | tf_op jit(solution)/shard_map/jit(cholesky)/cholesky | solution.py:53
  148.9 9.8 %custom-call.32 = f32[1,128,128]{1,2,0:T(8,128)S(1)} custom-call(f32[1,128,128]{2,1,0:T(8,128)S(1)} %get-tuple-element.39), custom_call_target="InvertDiagBlocksLowerTriangular" | custom-call | tf_op jit(solution)/shard_map/jit(cholesky)/cholesky | solution.py:53
  159.0 1.3 convolution_subtract_fusion.4
  160.3 11.9 %cholesky.253 = f32[128,128]{1,0:T(8,128)S(1)} custom-call(f32[128,128]{1,0:T(8,128)S(1)} %convolution_subtract_fusion.4), custom_call_target="Cholesky" | custom-call | tf_op jit(solution)/shard_map/jit(cholesky)/cholesky | solution.py:53
  172.3 0.7 compare_reduce_fusion.1
  173.1 0.6 compare_reduce_fusion
  173.7 0.7 compare_reduce_fusion.2
  177.0 11.3 %while.1 = (s32[]{:T(128)}, f32[512,512]{0,1:T(8,128)S(1)}, s32[4,2]{0,1:T(2,128)S(1)}, f32[4,128,128]{2,1,0:T(8,128)}, s32[]{:T(128)}) while((s32[]{:T(128)}, f32[512,512]{0,1:T(8,128)S(1)}, s32[4,2]{0,1:T(2,128)S(1)}, f32[4,128,128]{2,1,0:T(8,128)}, s32[]{:T(128)}) %tuple.33), condition=%wide.while_cond, body=%wide.while_body.sunk | while | flops 2 | bytes 393329 | solution.py:16
  177.1 0.6 fusion.49
  177.7 1.4 dynamic-slice.7
  179.3 0.6 bitcast_dynamic-update-slice_fusion.2
  180.0 0.6 fusion.49
  180.6 1.4 dynamic-slice.7
  182.1 0.6 bitcast_dynamic-update-slice_fusion.2
  183.4 1.4 dynamic-slice.7
  184.9 0.6 bitcast_dynamic-update-slice_fusion.2
  185.6 0.6 fusion.49
  186.2 1.4 dynamic-slice.7
  187.7 0.6 bitcast_dynamic-update-slice_fusion.2
  188.4 1.0 copy-done.9
  189.3 40.1 %custom-call.33 = f32[4,128,128]{1,2,0:T(8,128)S(1)} custom-call(f32[4,128,128]{2,1,0:T(8,128)} %get-tuple-element.9), custom_call_target="InvertDiagBlocksLowerTriangular" | custom-call | tf_op jit(solution)/shard_map/triangular_solve | solution.py:16
  229.5 3.6 fusion.12
  233.1 5.2 %convolution_subtract_fusion.1 = f32[4096,128]{1,0:T(8,128)S(1)} fusion(f32[4096,128]{0,1:T(8,128)S(1)} %fusion.12, f32[4096,512]{1,0:T(8,128)} %scatter_fusion.1, f32[512,512]{0,1:T(8,128)} %copy-done.9), kind=kOutput, calls=%fused_computation.17 | convolution fusion | flops 805830656 | bytes 6356992 | tf_op jit(solution)/shard_map/triangular_solve | solution.py:16
  238.2 2.0 fusion.27
  240.3 10.0 %convolution_subtract_fusion = f32[4096,128]{1,0:T(8,128)S(1)} fusion(f32[4096,128]{0,1:T(8,128)S(1)} %fusion.27, f32[4096,128]{0,1:T(8,128)S(1)} %fusion.12, f32[4096,512]{1,0:T(8,128)} %scatter_fusion.1, f32[512,512]{0,1:T(8,128)} %copy-done.9), kind=kOutput, calls=%fused_computation.16 | convolution fusion | flops 1612185600 | bytes 8519680 | tf_op jit(solution)/shard_map/triangular_solve | solution.py:16
  250.3 2.0 fusion.26
  252.4 12.7 %fusion.6 = f32[4096,128]{1,0:T(8,128)S(1)} fusion(f32[4096,128]{0,1:T(8,128)S(1)} %fusion.26, f32[4096,128]{0,1:T(8,128)S(1)} %fusion.27, f32[4096,128]{0,1:T(8,128)S(1)} %fusion.12, f32[4096,512]{1,0:T(8,128)} %scatter_fusion.1, f32[512,512]{0,1:T(8,128)} %copy-done.9), kind=kOutput, calls=%fused_computation.18 | convolution fusion | flops 2419589120 | bytes 10682368 | tf_op jit(solution)/shard_map/triangular_solve | solution.py:16
  265.1 2.0 fusion.25
  267.2 1.3 copy-done.6
  268.5 1.5 maximum_select_fusion
  270.0 5.9 %pad_maximum_fusion = f32[4096,512]{0,1:T(8,128)} fusion(f32[4096,128]{0,1:T(8,128)} %copy-done.6, f32[4096,128]{0,1:T(8,128)} %copy-done.4, f32[4096,128]{0,1:T(8,128)} %copy-done.2, f32[4096,128]{0,1:T(8,128)S(1)} %fusion.12), kind=kLoop, calls=%fused_computation.8 | loop fusion | flops 6291456 | bytes 16777216 | tf_op jit(solution)/shard_map/triangular_solve | solution.py:16
  276.0 1.6 copy-done.3
  277.5 0.6 copy-done.5
  278.2 0.6 copy-done.7
  279.0 3.1 slice-done
  282.1 3.9 %maximum_bitcast_fusion = f32[1,4096,512]{1,2,0:T(8,128)} fusion(f32[3584,512]{0,1:T(8,128)S(1)} %slice-done, f32[512,512]{0,1:T(8,128)S(1)} %maximum_select_fusion.1), kind=kLoop, calls=%fused_computation.9 | loop fusion | flops 2097152 | bytes 16777216 | tf_op jit(solution)/shard_map/broadcast_in_dim | solution.py:62
  286.0 9.0 %copy.44 = f32[1,4096,512]{2,1,0:T(8,128)} copy(f32[1,4096,512]{1,2,0:T(8,128)} %maximum_bitcast_fusion) | data formatting | bytes 16777216
  295.0 28.4 %all-reduce.6.cloned.1.call-done = f32[896,512]{0,1:T(8,128)} async-done(((f32[896,512]{0,1:T(8,128)}), f32[896,512]{0,1:T(8,128)}) %all-reduce.6.cloned.1.call-update) | async-done | bytes 1835024 | tf_op jit(solution)/shard_map/psum | solution.py:12
  323.4 32.7 %slice_subtract_fusion = f32[4096,896]{1,0:T(8,128)} fusion(f32[4096,1408]{1,0:T(8,128)} %bitcast.81, f32[896,512]{0,1:T(8,128)} %all-reduce.6.cloned.1.call-done, f32[4096,128]{0,1:T(8,128)} %copy-done.6, f32[4096,128]{0,1:T(8,128)} %copy-done.4, f32[4096,128]{0,1:T(8,128)} %copy-done.2, f32[4096,128]{0,1:T(8,128)S(1)} %fusion.12), kind=kOutput, calls=%fused_computation.7 | convolution fusion | flops 22558539776 | bytes 39583744 | tf_op jit(solution)/shard_map/dot_general | solution.py:56
  356.1 13.9 %scatter_fusion.3 = f32[4096,896]{1,0:T(8,128)} fusion(f32[4096,896]{1,0:T(8,128)} %slice_subtract_fusion, s32[256]{0:T(256)S(1)} %bitcast.86, f32[256,896]{1,0:T(8,128)} %bitcast.26), kind=kCustom, calls=%fused_computation.4 | custom fusion | flops 229376 | bytes 2753536 | tf_op jit(solution)/shard_map/scatter-add | solution.py:59
  (67 shorter events, 5.2 us)
Async XLA Ops:
  7.2 1.6 copy-start
  9.9 13.8 %all-to-all-start = ((s32[8,2,16]{2,1,0:T(2,128)}), s32[8,2,16]{2,1,0:T(2,128)S(1)}, u32[]{:S(2)}, u32[]{:S(2)}) async-start(s32[8,2,16]{2,1,0:T(2,128)} %bitcast.7), calls=%async_computation | async-start | bytes 16384 | tf_op jit(solution)/shard_map/all_to_all | solution.py:41
  23.7 17.2 %all-to-all-start.1 = ((f32[8,2,16,512]{3,2,1,0:T(8,128)}), f32[8,2,16,512]{3,2,1,0:T(8,128)S(1)}, u32[]{:S(2)}, u32[]{:S(2)}) async-start(f32[8,2,16,512]{3,2,1,0:T(8,128)} %bitcast.10), calls=%async_computation.1 | async-start | bytes 1048576 | tf_op jit(solution)/shard_map/all_to_all | solution.py:40
  27.2 60.8 %all-reduce.4.cloned.1.call-start = ((), (), s32[]{:S(2)}) async-start(), calls=%async_computation.3 | async-start | bytes 2097152 | tf_op jit(solution)/shard_map/psum | solution.py:12
  51.6 1.1 copy-start.11
  55.9 300.2 %all-to-all-start.2 = ((f32[8,2,16,896]{3,2,1,0:T(8,128)}), f32[8,2,16,896]{3,2,1,0:T(8,128)}, u32[]{:S(2)}, u32[]{:S(2)}) async-start(f32[8,2,16,896]{3,2,1,0:T(8,128)} %bitcast.25), calls=%async_computation.2 | async-start | bytes 1835008 | tf_op jit(solution)/shard_map/all_to_all | solution.py:47
  60.1 263.3 %all-reduce.6.cloned.1.call-start = ((), (), s32[]{:S(2)}) async-start(), calls=%async_computation.4 | async-start | bytes 3670016 | tf_op jit(solution)/shard_map/psum | solution.py:12
  88.0 1.7 copy-start.8
  90.5 34.3 %copy-start.10 = (f32[512,512]{1,0:T(8,128)}, f32[512,512]{1,0:T(8,128)S(1)}, u32[]{:S(2)}) copy-start(f32[512,512]{1,0:T(8,128)S(1)} %fusion.14) | copy-start | bytes 3145732
  188.4 1.0 copy-start.9
  240.3 26.9 %copy-start.2 = (f32[4096,128]{0,1:T(8,128)}, f32[4096,128]{0,1:T(8,128)S(1)}, u32[]{:S(2)}) copy-start(f32[4096,128]{0,1:T(8,128)S(1)} %fusion.27) | copy-start | bytes 6291460
  252.4 14.8 %copy-start.4 = (f32[4096,128]{0,1:T(8,128)}, f32[4096,128]{0,1:T(8,128)S(1)}, u32[]{:S(2)}) copy-start(f32[4096,128]{0,1:T(8,128)S(1)} %fusion.26) | copy-start | bytes 6291460
  267.2 1.4 copy-start.6
  275.9 1.6 copy-start.3
  275.9 2.2 copy-start.5
  276.0 2.8 copy-start.7
  278.8 3.3 slice-start
  356.1 13.9 %copy-start.1 = (s32[1,1,4,16]{3,2,1,0:T(4,128)S(1)}, s32[1,1,4,16]{3,2,1,0:T(4,128)}, u32[]{:S(2)}) copy-start(s32[1,1,4,16]{3,2,1,0:T(4,128)} %param.7) | copy-start | bytes 772
Sparse Core Ops, SparseCore 0:
  52.8 35.1 all-reduce.3
  276.1 47.3 all-reduce.5
where the time goes:
time: 382 us; the launch traced here: 377 us
  other arithmetic  157 us (41%)
  matrix products  74.4 us (19%)
  waiting for transfers between devices  63.9 us (17%)
  local copies, waits for them, and re-layouts  48.9 us (13%)
  between operations  17.9 us (5%)
  starting transfers between devices  15.2 us (4%)
    another operation x14, other arithmetic, local(): pivot_factor = jnp.linalg.cholesky(symmetric)  78.9 us
    psum x2, waiting for transfers between devices, spread(): return lax.psum(jnp.where(mine, array, jnp.zeros_like(array)), axis)  56.1 us
    another operation x4, other arithmetic, right_solve(): lax.linalg.triangular_solve(factor, rows, left_side=False, lower=True, tr...  46.2 us
    another operation x7, matrix products, right_solve(): lax.linalg.triangular_solve(factor, rows, left_side=False, lower=True, tr...  37.6 us
    dot_general x1, matrix products, local(): jnp.dot(solved, window.T, precision=lax.Precision.HIGHEST)  32.7 us
    unnamed x26, local copies, waits for them, and re-layouts  14.5 us
    scatter-add x1, other arithmetic, local(): schur_part.at[flat_rows].add(trailing_rows.reshape(-1, win_cols))  13.9 us
    another operation x20, local copies, waits for them, and re-layouts  11.2 us
  transfers between devices with their start and end apart: 5, of which 4 were waited for; matrix products, arithmetic and copies ran while one was open for 65% of the time, Pallas kernels for 0%

commit v1 on v0

v1 whole, which is shorter than its diff:
```python
import jax
import jax.numpy as jnp
from jax import lax
from jax.sharding import PartitionSpec as P

PB = 512
CAP = 2
BLK = 128
EXACT = lax.Precision.HIGHEST
FAST = lax.Precision.HIGH


def pack_slots(values, slot_index, front_count):
    empty = jnp.zeros((front_count * CAP,) + values.shape[1:], values.dtype)
    filled = empty.at[slot_index].set(values)
    return filled.reshape((front_count, CAP) + values.shape[1:])


def pairs(size, bit):
    return [(d, d ^ bit) for d in range(size)]


def broadcast_from(x, owner, axis):
    size = lax.axis_size(axis)
    me = lax.axis_index(axis)
    got = lax.ppermute(x, axis, pairs(size, 1))
    x = jnp.where(me == owner, x, got)
    half_rows = x.shape[0] // 2
    core = me % 2
    half = jnp.where(core == 0, x[:half_rows], x[half_rows:])
    bit = 2
    while bit < size:
        got = lax.ppermute(half, axis, pairs(size, bit))
        half = jnp.where(me // bit == owner // bit, half, got)
        bit *= 2
    other = lax.ppermute(half, axis, pairs(size, 1))
    return jnp.where(
        core == 0,
        jnp.concatenate([half, other], axis=0),
        jnp.concatenate([other, half], axis=0),
    )


def tri_inverse(factor):
    eye = jnp.eye(factor.shape[0], dtype=factor.dtype)
    return lax.linalg.triangular_solve(factor, eye, left_side=True, lower=True)


def cholesky_and_inverse(sym):
    n = sym.shape[0]
    nb = n // BLK
    blk = [[None] * nb for _ in range(nb)]
    inv_diag = []
    for k in range(nb):
        akk = sym[k * BLK:(k + 1) * BLK, k * BLK:(k + 1) * BLK]
        for j in range(k):
            akk = akk - jnp.dot(blk[k][j], blk[k][j].T, precision=EXACT)
        lkk = jnp.linalg.cholesky(akk)
        ikk = tri_inverse(lkk)
        blk[k][k] = lkk
        inv_diag.append(ikk)
        if k + 1 < nb:
            rest = sym[(k + 1) * BLK:, k * BLK:(k + 1) * BLK]
            for j in range(k):
                below = jnp.concatenate([blk[i][j] for i in range(k + 1, nb)], axis=0)
                rest = rest - jnp.dot(below, blk[k][j].T, precision=EXACT)
            panel = jnp.dot(rest, ikk.T, precision=EXACT)
            for i in range(k + 1, nb):
                blk[i][k] = panel[(i - k - 1) * BLK:(i - k) * BLK]
    inv = [[None] * nb for _ in range(nb)]
    for i in range(nb):
        inv[i][i] = inv_diag[i]
        for j in range(i - 1, -1, -1):
            acc = jnp.dot(blk[i][j], inv[j][j], precision=EXACT)
            for k in range(j + 1, i):
                acc = acc + jnp.dot(blk[i][k], inv[k][j], precision=EXACT)
            inv[i][j] = -jnp.dot(inv_diag[i], acc, precision=EXACT)
    zero = jnp.zeros((BLK, BLK), sym.dtype)

    def join(parts):
        return jnp.concatenate(
            [jnp.concatenate([parts[i][j] if j <= i else zero for j in range(nb)], axis=1) for i in range(nb)],
            axis=0,
        )

    return join(blk), join(inv)


def local(front_block, child_blocks, child_rows, child_dest, panel_owner):
    local_rows = front_block[0]
    front_count = lax.axis_size("front")
    blocks = child_blocks[0, 0]
    row_lists = child_rows[0, 0]
    target_front = child_dest[0, 0, :, 0]
    block_count = target_front.shape[0]
    position = jnp.arange(block_count, dtype=jnp.int32)
    same_front = target_front[:, None] == target_front[None, :]
    earlier = position[None, :] < position[:, None]
    slot_index = target_front * CAP + jnp.sum((same_front & earlier).astype(jnp.int32), axis=1)
    send_rows = pack_slots(row_lists, slot_index, front_count)
    send_panel = pack_slots(blocks[:, :, :PB], slot_index, front_count)
    got_panel = lax.all_to_all(send_panel, "front", split_axis=0, concat_axis=0, tiled=True)
    got_rows = lax.all_to_all(send_rows, "front", split_axis=0, concat_axis=0, tiled=True)
    flat_rows = got_rows.reshape(-1)
    panel_part = local_rows[:, :PB].at[flat_rows].add(got_panel.reshape(-1, PB))
    send_trail = pack_slots(blocks[:, :, PB:], slot_index, front_count)
    trailing_rows = lax.all_to_all(send_trail, "front", split_axis=0, concat_axis=0, tiled=True)
    win_cols = local_rows.shape[1] - PB
    owner_index = panel_owner[0]
    is_owner = lax.axis_index("grp") == owner_index

    pivot_block = broadcast_from(panel_part[:PB], owner_index, "grp")
    window_rows = broadcast_from(panel_part[PB:PB + win_cols], owner_index, "grp")
    symmetric = 0.5 * (pivot_block + pivot_block.T)
    pivot_factor, factor_inverse = cholesky_and_inverse(symmetric)
    solved = jnp.dot(panel_part, factor_inverse.T, precision=FAST)
    window = jnp.dot(window_rows, factor_inverse.T, precision=FAST)
    schur_part = local_rows[:, PB:] - jnp.dot(solved, window.T, precision=FAST)
    schur_part = schur_part.at[flat_rows].add(trailing_rows.reshape(-1, win_cols))
    top_rows = jnp.where(is_owner, pivot_factor, solved[:PB])
    panel_rows = jnp.concatenate([top_rows, solved[PB:]], axis=0)
    return (panel_rows[None], schur_part[None])


def solution(mesh):
    placed = (
        P("front", "grp", None),
        P("front", "grp", None, None, None),
        P("front", "grp", None, None),
        P("front", "grp", None, None),
        P("front"),
    )
    return jax.shard_map(
        local,
        mesh=mesh,
        in_specs=placed,
        out_specs=(P("front", "grp", None), P("front", "grp", None)),
        check_vma=False,
    )
```

time: 382 us -> 241 us (0.63)
  waiting for transfers between devices: 63.9 us -> 13 us
  matrix products: 74.4 us -> 44.5 us
  other arithmetic: 157 us -> 130 us
  local copies, waits for them, and re-layouts: 48.9 us -> 25.1 us
  between operations: 17.9 us -> 2.38 us
  starting transfers between devices: 15.2 us -> 20.8 us
    psum x2 -> x0, waiting for transfers between devices: 56.1 us -> none  [spread(): return lax.psum(jnp.where(mine, array, jnp.zeros_like(array)), axis)]
    another operation x13 -> x4, matrix products: 41.7 us -> 1.08 us  [tri_inverse(): return lax.linalg.triangular_solve(factor, eye, left_side=True, lower=True)]
    another operation x18 -> x20, other arithmetic: 125 us -> 92.4 us  [the longest x12 50 us: cholesky_and_inverse(): lkk = jnp.linalg.cholesky(akk)]
    unnamed x26 -> x14, local copies, waits for them, and re-layouts: 14.5 us -> 2.74 us
    another operation x34 -> x5, local copies, waits for them, and re-layouts: 11.9 us -> 0.29 us  [the longest x3 0.27 us: tri_inverse(): return lax.linalg.triangular_solve(factor, eye, left_side=True, lower=True)]
    dot_general x1 -> x31, matrix products: 32.7 us -> 43.5 us  [the longest x1 17.8 us: local(): schur_part = local_rows[:, PB:] - jnp.dot(solved, window.T, precision=FAST)]
    ppermute x0 -> x6, starting transfers between devices: none -> 5.33 us  [the longest x2 4.35 us: broadcast_from(): got = lax.ppermute(half, axis, pairs(size, bit))]
    ppermute x0 -> x6, waiting for transfers between devices: none -> 4.52 us  [the longest x2 4.51 us: broadcast_from(): got = lax.ppermute(half, axis, pairs(size, bit))]
  transfers between devices with their start and end apart: 5 -> 9, of which waited for: 4 -> 3; matrix products, arithmetic and copies ran while one was open for 65% -> 73% of each run, Pallas kernels for 0% -> 0%
where the time goes in v1:
time: 241 us; the launch traced here: 236 us
  other arithmetic  130 us (54%)
  matrix products  44.5 us (18%)
  local copies, waits for them, and re-layouts  25.1 us (10%)
  starting transfers between devices  20.8 us (9%)
  waiting for transfers between devices  13 us (5%)
    another operation x12, other arithmetic, cholesky_and_inverse(): lkk = jnp.linalg.cholesky(akk)  50 us
    another operation x8, other arithmetic, tri_inverse(): return lax.linalg.triangular_solve(factor, eye, left_side=True, lower=True)  42.4 us
    dot_general x1, matrix products, local(): schur_part = local_rows[:, PB:] - jnp.dot(solved, window.T, precision=FAST)  17.8 us
    scatter-add x1, other arithmetic, local(): schur_part.at[flat_rows].add(trailing_rows.reshape(-1, win_cols))  13.8 us
    dot_general x1, matrix products, local(): solved = jnp.dot(panel_part, factor_inverse.T, precision=FAST)  9.42 us
    scatter-add x1, other arithmetic, local(): panel_part = local_rows[:, :PB].at[flat_rows].add(got_panel.reshape(-1, PB))  9.03 us
    slice x1, local copies, waits for them, and re-layouts, local(): panel_part = local_rows[:, :PB].at[flat_rows].add(got_panel.reshape(-1, PB))  7.92 us
    all_to_all x1, starting transfers between devices, local(): lax.all_to_all(send_rows, 'front', split_axis=0, concat_axis=0, tiled=True)  7.25 us
  transfers between devices with their start and end apart: 9, of which 3 were waited for; matrix products, arithmetic and copies ran while one was open for 73% of the time, Pallas kernels for 0%

profile of v1, /device:TPU:0, one launch (start us, length us, event | category | flops | bytes accessed | tf_op | source)
XLA Modules:
  0.0 236.1 jit_solution(13027901601082787073)
XLA Ops:
  0.6 0.9 convert_reduce_fusion
  1.6 0.7 fusion.38
  2.2 1.2 scatter_custom_fusion
  3.4 7.3 %all-to-all-start = ((s32[8,2,16]{2,1,0:T(2,128)}), s32[8,2,16]{2,1,0:T(2,128)S(1)}, u32[]{:S(2)}, u32[]{:S(2)}) async-start(s32[8,2,16]{2,1,0:T(2,128)} %bitcast.7), calls=%async_computation | async-start | bytes 16384 | tf_op jit(solution)/shard_map/all_to_all | solution.py:103
  10.6 0.9 slice.104
  11.6 0.9 broadcast_in_dim.14
  12.4 2.0 scatter_fusion
  14.4 2.7 %all-to-all-done = s32[8,2,16]{2,1,0:T(2,128)S(1)} async-done(((s32[8,2,16]{2,1,0:T(2,128)}), s32[8,2,16]{2,1,0:T(2,128)S(1)}, u32[]{:S(2)}, u32[]{:S(2)}) %all-to-all-start) | async-done | bytes 1056 | tf_op jit(solution)/shard_map/all_to_all | solution.py:103
  17.2 3.5 %all-to-all-start.1 = ((f32[8,2,16,512]{3,2,1,0:T(8,128)}), f32[8,2,16,512]{3,2,1,0:T(8,128)S(1)}, u32[]{:S(2)}, u32[]{:S(2)}) async-start(f32[8,2,16,512]{3,2,1,0:T(8,128)} %bitcast.10), calls=%async_computation.1 | async-start | bytes 1048576 | tf_op jit(solution)/shard_map/all_to_all | solution.py:102
  20.7 7.9 %slice.103 = f32[4096,512]{1,0:T(8,128)} slice(f32[4096,1408]{1,0:T(8,128)} %bitcast.108), slice={[0:4096], [0:512]} | slice | bytes 16777216 | tf_op jit(solution)/shard_map/slice | solution.py:105
  28.7 5.7 %all-to-all-done.1 = f32[8,2,16,512]{3,2,1,0:T(8,128)S(1)} async-done(((f32[8,2,16,512]{3,2,1,0:T(8,128)}), f32[8,2,16,512]{3,2,1,0:T(8,128)S(1)}, u32[]{:S(2)}, u32[]{:S(2)}) %all-to-all-start.1) | async-done | bytes 524320 | tf_op jit(solution)/shard_map/all_to_all | solution.py:102
  34.4 9.0 %scatter_fusion.1 = f32[4096,512]{1,0:T(8,128)} fusion(f32[4096,512]{1,0:T(8,128)} %slice.103, s32[256]{0:T(256)S(1)} %bitcast.113, f32[256,512]{1,0:T(8,128)S(1)} %bitcast.110), kind=kCustom, calls=%fused_computation.2 | custom fusion | flops 131072 | bytes 1573888 | tf_op jit(solution)/shard_map/scatter-add | solution.py:105
  43.4 1.3 slice.105
  44.8 1.6 slice.123
  46.5 0.6 collective-permute-start.3
  47.7 1.8 broadcast_select_fusion.1
  49.4 0.9 slice_select_fusion.1
  50.3 1.6 collective-permute-start.1
  51.9 1.0 broadcast_in_dim.30
  52.9 2.2 scatter_fusion.2
  55.1 4.7 %all-to-all-start.2 = ((f32[8,2,16,896]{3,2,1,0:T(8,128)}), f32[8,2,16,896]{3,2,1,0:T(8,128)}, u32[]{:S(2)}, u32[]{:S(2)}) async-start(f32[8,2,16,896]{3,2,1,0:T(8,128)} %bitcast.26), calls=%async_computation.2 | async-start | bytes 1835008 | tf_op jit(solution)/shard_map/all_to_all | solution.py:107
  59.8 4.5 %collective-permute-done.1 = f32[256,512]{1,0:T(8,128)} collective-permute-done((f32[256,512]{1,0:T(8,128)}, f32[256,512]{1,0:T(8,128)}, u32[]{:S(2)}, u32[]{:S(2)}) %collective-permute-start.1) | collective-permute-done | bytes 524320 | tf_op jit(solution)/shard_map/ppermute | solution.py:33
  64.6 2.5 %broadcast_select_fusion = f32[896,512]{1,0:T(8,128)S(1)} fusion(f32[896,512]{1,0:T(8,128)} %collective-permute-done.3, pred[]{:T(512)S(6)} %eq.45, f32[4096,512]{1,0:T(8,128)} %scatter_fusion.1), kind=kLoop, calls=%fused_computation.49 | loop fusion | flops 458752 | bytes 5505025 | tf_op jit(solution)/shard_map/jit(_where)/select_n | solution.py:27
  67.1 1.1 slice_select_fusion
  68.2 2.8 %collective-permute-start.4 = (f32[448,512]{1,0:T(8,128)}, f32[448,512]{1,0:T(8,128)}, u32[]{:S(2)}, u32[]{:S(2)}) collective-permute-start(f32[448,512]{1,0:T(8,128)} %slice_select_fusion), channel_id=1, source_target_pairs={{0,2},{1,3},{2,0},{3,1},{4,6},{5,7},{6,4},{7,5},{8,10},{9,11},{10,... | collective-permute-start | bytes 2752520 | tf_op jit(solution)/shard_map/ppermute | solution.py:33
  71.1 1.3 copy.31
  72.4 1.4 fusion.13
  73.7 1.0 copy-done.2
  74.8 0.9 fusion.33
  75.8 11.7 %cholesky.74 = f32[128,128]{1,0:T(8,128)S(1)} custom-call(f32[128,128]{1,0:T(8,128)S(1)} %copy.33), custom_call_target="Cholesky" | custom-call | tf_op jit(solution)/shard_map/jit(cholesky)/cholesky | solution.py:58
  87.5 0.6 compare_reduce_fusion.3
  88.2 0.6 select_bitcast_fusion.3
  88.7 9.8 %custom-call.8 = f32[1,128,128]{1,2,0:T(8,128)S(1)} custom-call(f32[1,128,128]{2,1,0:T(8,128)S(1)} %get-tuple-element.10), custom_call_target="InvertDiagBlocksLowerTriangular" | custom-call | tf_op jit(solution)/shard_map/triangular_solve/custom-call.0 | solution.py:46
  98.8 1.3 fusion.15
  100.2 1.1 convolution_subtract_fusion.8
  101.3 1.1 convolution_subtract_fusion.7
  102.4 0.3 fusion.44
  102.7 1.1 convolution_subtract_fusion.5
  103.9 1.1 convolution_subtract_fusion.3
  105.0 1.3 convolution_subtract_fusion
  106.5 11.9 %cholesky.85 = f32[128,128]{1,0:T(8,128)S(1)} custom-call(f32[128,128]{1,0:T(8,128)S(1)} %copy.36), custom_call_target="Cholesky" | custom-call | tf_op jit(solution)/shard_map/jit(cholesky)/cholesky | solution.py:58
  118.4 0.6 compare_reduce_fusion.2
  119.1 0.7 select_bitcast_fusion.2
  119.7 9.8 %custom-call.9 = f32[1,128,128]{1,2,0:T(8,128)S(1)} custom-call(f32[1,128,128]{2,1,0:T(8,128)S(1)} %get-tuple-element.8), custom_call_target="InvertDiagBlocksLowerTriangular" | custom-call | tf_op jit(solution)/shard_map/triangular_solve/custom-call.0 | solution.py:46
  130.6 0.3 fusion.40
  130.9 0.3 fusion.48
  131.2 0.6 fusion.65
  132.8 11.7 %cholesky.96 = f32[128,128]{1,0:T(8,128)S(1)} custom-call(f32[128,128]{1,0:T(8,128)S(1)} %copy.40), custom_call_target="Cholesky" | custom-call | tf_op jit(solution)/shard_map/jit(cholesky)/cholesky | solution.py:58
  144.6 0.6 compare_reduce_fusion.1
  145.2 0.7 select_bitcast_fusion.1
  145.9 9.8 %custom-call.10 = f32[1,128,128]{1,2,0:T(8,128)S(1)} custom-call(f32[1,128,128]{2,1,0:T(8,128)S(1)} %get-tuple-element.6), custom_call_target="InvertDiagBlocksLowerTriangular" | custom-call | tf_op jit(solution)/shard_map/triangular_solve/custom-call.0 | solution.py:46
  156.0 0.3 fusion.68
  157.1 11.9 %cholesky.107 = f32[128,128]{1,0:T(8,128)S(1)} custom-call(f32[128,128]{1,0:T(8,128)S(1)} %copy.44), custom_call_target="Cholesky" | custom-call | tf_op jit(solution)/shard_map/jit(cholesky)/cholesky | solution.py:58
  169.0 0.7 compare_reduce_fusion
  171.0 1.3 select_bitcast_fusion
  172.3 9.8 %custom-call.11 = f32[1,128,128]{1,2,0:T(8,128)S(1)} custom-call(f32[1,128,128]{2,1,0:T(8,128)S(1)} %get-tuple-element.4), custom_call_target="InvertDiagBlocksLowerTriangular" | custom-call | tf_op jit(solution)/shard_map/triangular_solve/custom-call.0 | solution.py:46
  184.2 0.9 copy.64
  185.1 0.3 convolution_negate_fusion.2
  185.4 9.4 %fusion.63 = f32[4096,512]{1,0:T(8,128)S(1)} fusion(f32[4096,512]{1,0:T(8,128)} %scatter_fusion.1, f32[128,256]{1,0:T(8,128)S(1)} %broadcast.100, f32[128,128]{1,0:T(8,128)S(1)} %cholesky.75, f32[128,128]{1,0:T(8,128)S(1)} %fusion.23, f32[128,128]{1,0:T(8,128)S(1)} %copy.54, f32[128,128]{1,0:T(8,128)S(1)} %convolution_negate_fusion, ...), kind=kOutput, calls=%fused_computation.129 | convolution fusion | flops 6445858816 | bytes 17629184 | tf_op jit(solution)/shard_map/dot_general | solution.py:116
  194.9 0.8 slice.121
  196.4 4.4 %maximum_bitcast_fusion = f32[1,4096,512]{2,1,0:T(8,128)} fusion(f32[3584,512]{1,0:T(8,128)S(1)} %slice.121, f32[512,512]{1,0:T(8,128)S(1)} %fusion.9), kind=kLoop, calls=%fused_computation.6 | loop fusion | flops 2097152 | bytes 16777216 | tf_op jit(solution)/shard_map/broadcast_in_dim | solution.py:122
  200.8 3.1 %fusion = f32[896,512]{1,0:T(8,128)S(1)} fusion(f32[448,512]{1,0:T(8,128)} %collective-permute-done.5, f32[448,512]{1,0:T(8,128)S(1)} %broadcast_select_fusion.2, pred[]{:T(512)S(6)} %eq.46, f32[128,256]{1,0:T(8,128)S(1)} %broadcast.100, f32[128,128]{1,0:T(8,128)S(1)} %cholesky.75, f32[128,128]{1,0:T(8,128)S(1)} %fusion.23, f32[128,128]{1,0:T(8,128)S(1)} %copy.54, ...), kind=kOutput, calls=%fused_computation.8 | convolution fusion | flops 1414070272 | bytes 4521985 | tf_op jit(solution)/shard_map/dot_general | solution.py:117
  203.9 17.8 %slice_subtract_fusion = f32[4096,896]{1,0:T(8,128)} fusion(f32[4096,1408]{1,0:T(8,128)} %bitcast.109, f32[4096,512]{1,0:T(8,128)S(1)} %fusion.63, f32[896,512]{1,0:T(8,128)S(1)} %fusion), kind=kOutput, calls=%fused_computation.5 | convolution fusion | flops 11277959168 | bytes 39583744 | tf_op jit(solution)/shard_map/dot_general | solution.py:118
  221.8 13.8 %scatter_fusion.3 = f32[4096,896]{1,0:T(8,128)} fusion(f32[4096,896]{1,0:T(8,128)} %slice_subtract_fusion, s32[256]{0:T(256)S(1)} %bitcast.114, f32[256,896]{1,0:T(8,128)} %bitcast.27), kind=kCustom, calls=%fused_computation.4 | custom fusion | flops 229376 | bytes 2753536 | tf_op jit(solution)/shard_map/scatter-add | solution.py:119
  (70 shorter events, 8.3 us)
Async XLA Ops:
  0.6 1.6 copy-start
  3.4 13.8 %all-to-all-start = ((s32[8,2,16]{2,1,0:T(2,128)}), s32[8,2,16]{2,1,0:T(2,128)S(1)}, u32[]{:S(2)}, u32[]{:S(2)}) async-start(s32[8,2,16]{2,1,0:T(2,128)} %bitcast.7), calls=%async_computation | async-start | bytes 16384 | tf_op jit(solution)/shard_map/all_to_all | solution.py:103
  17.2 17.2 %all-to-all-start.1 = ((f32[8,2,16,512]{3,2,1,0:T(8,128)}), f32[8,2,16,512]{3,2,1,0:T(8,128)S(1)}, u32[]{:S(2)}, u32[]{:S(2)}) async-start(f32[8,2,16,512]{3,2,1,0:T(8,128)} %bitcast.10), calls=%async_computation.1 | async-start | bytes 1048576 | tf_op jit(solution)/shard_map/all_to_all | solution.py:102
  34.4 17.5 %copy-start.3 = (f32[1,1,4,16,1408]{4,3,2,1,0:T(8,128)S(1)}, f32[1,1,4,16,1408]{4,3,2,1,0:T(8,128)}, u32[]{:S(2)}) copy-start(f32[1,1,4,16,1408]{4,3,2,1,0:T(8,128)} %param.9) | copy-start | bytes 1081348
  44.7 2.9 %collective-permute-start = (f32[512,512]{1,0:T(8,128)S(1)}, f32[512,512]{1,0:T(8,128)}, u32[]{:S(2)}, u32[]{:S(2)}) collective-permute-start(f32[512,512]{1,0:T(8,128)S(1)} %slice.105), channel_id=1, source_target_pairs={{0,1},{1,0},{2,3},{3,2},{4,5},{5,4},{6,7},{7,6},{8,9},{9,8},{10,11... | collective-permute-start | bytes 3145736 | tf_op jit(solution)/shard_map/ppermute | solution.py:26
  46.5 18.1 %collective-permute-start.3 = (f32[896,512]{1,0:T(8,128)S(1)}, f32[896,512]{1,0:T(8,128)}, u32[]{:S(2)}, u32[]{:S(2)}) collective-permute-start(f32[896,512]{1,0:T(8,128)S(1)} %slice.123), channel_id=1, source_target_pairs={{0,1},{1,0},{2,3},{3,2},{4,5},{5,4},{6,7},{7,6},{8,9},{9,8},{10,11... | collective-permute-start | bytes 5505032 | tf_op jit(solution)/shard_map/ppermute | solution.py:26
  50.3 14.0 %collective-permute-start.1 = (f32[256,512]{1,0:T(8,128)}, f32[256,512]{1,0:T(8,128)}, u32[]{:S(2)}, u32[]{:S(2)}) collective-permute-start(f32[256,512]{1,0:T(8,128)} %slice_select_fusion.1), channel_id=1, source_target_pairs={{0,2},{1,3},{2,0},{3,1},{4,6},{5,7},{6,4},{7,5},{8,10},{9,11},{10,... | collective-permute-start | bytes 1572872 | tf_op jit(solution)/shard_map/ppermute | solution.py:33
  55.1 166.7 %all-to-all-start.2 = ((f32[8,2,16,896]{3,2,1,0:T(8,128)}), f32[8,2,16,896]{3,2,1,0:T(8,128)}, u32[]{:S(2)}, u32[]{:S(2)}) async-start(f32[8,2,16,896]{3,2,1,0:T(8,128)} %bitcast.26), calls=%async_computation.2 | async-start | bytes 1835008 | tf_op jit(solution)/shard_map/all_to_all | solution.py:107
  64.5 6.5 %collective-permute-start.2 = (f32[256,512]{1,0:T(8,128)S(1)}, f32[256,512]{1,0:T(8,128)S(1)}, u32[]{:S(2)}, u32[]{:S(2)}) collective-permute-start(f32[256,512]{1,0:T(8,128)S(1)} %broadcast_select_fusion.3), channel_id=1, source_target_pairs={{0,1},{1,0},{2,3},{3,2},{4,5},{5,4},{6,7},{7,6},{8,9},{9,8},{10,11... | collective-permute-start | bytes 1572872 | tf_op jit(solution)/shard_map/ppermute | solution.py:36
  68.2 127.6 %collective-permute-start.4 = (f32[448,512]{1,0:T(8,128)}, f32[448,512]{1,0:T(8,128)}, u32[]{:S(2)}, u32[]{:S(2)}) collective-permute-start(f32[448,512]{1,0:T(8,128)} %slice_select_fusion), channel_id=1, source_target_pairs={{0,2},{1,3},{2,0},{3,1},{4,6},{5,7},{6,4},{7,5},{8,10},{9,11},{10,... | collective-permute-start | bytes 2752520 | tf_op jit(solution)/shard_map/ppermute | solution.py:33
  73.7 1.0 copy-start.2
  194.9 1.4 copy-start.4
  196.0 4.8 %collective-permute-start.5 = (f32[448,512]{1,0:T(8,128)S(1)}, f32[448,512]{1,0:T(8,128)}, u32[]{:S(2)}, u32[]{:S(2)}) collective-permute-start(f32[448,512]{1,0:T(8,128)S(1)} %broadcast_select_fusion.2), channel_id=1, source_target_pairs={{0,1},{1,0},{2,3},{3,2},{4,5},{5,4},{6,7},{7,6},{8,9},{9,8},{10,11... | collective-permute-start | bytes 2752520 | tf_op jit(solution)/shard_map/ppermute | solution.py:36
  203.9 31.7 %copy-start.1 = (s32[1,1,4,16]{3,2,1,0:T(4,128)S(1)}, s32[1,1,4,16]{3,2,1,0:T(4,128)}, u32[]{:S(2)}) copy-start(s32[1,1,4,16]{3,2,1,0:T(4,128)} %param.10) | copy-start | bytes 772

commit v2 on v1

--- a/solution.py
+++ b/solution.py
@@ -1,6 +1,8 @@
 import jax
 import jax.numpy as jnp
 from jax import lax
+from jax.experimental import pallas as pl
+from jax.experimental.pallas import tpu as pltpu
 from jax.sharding import PartitionSpec as P
 
 PB = 512
@@ -41,49 +43,71 @@
     )
 
 
-def tri_inverse(factor):
-    eye = jnp.eye(factor.shape[0], dtype=factor.dtype)
-    return lax.linalg.triangular_solve(factor, eye, left_side=True, lower=True)
+def _mm(a, b):
+    return jnp.dot(a, b, precision=EXACT, preferred_element_type=jnp.float32)
 
 
-def cholesky_and_inverse(sym):
-    n = sym.shape[0]
+def _mm_t(a, b):
+    return lax.dot_general(a, b, (((1,), (1,)), ((), ())), precision=EXACT, preferred_element_type=jnp.float32)
+
+
+def _factor_kernel(s_ref, l_ref, inv_ref, w_ref, d_ref, dt_ref, di_ref):
+    n = s_ref.shape[0]
     nb = n // BLK
-    blk = [[None] * nb for _ in range(nb)]
+    w_ref[...] = s_ref[...]
+    l_ref[...] = jnp.zeros_like(l_ref)
+    inv_ref[...] = jnp.zeros_like(inv_ref)
+    sub = lax.broadcasted_iota(jnp.int32, (BLK, BLK), 0)
+    lane = lax.broadcasted_iota(jnp.int32, (BLK, BLK), 1)
+    lane1 = lax.broadcasted_iota(jnp.int32, (1, BLK), 1)
+    sub1 = lax.broadcasted_iota(jnp.int32, (BLK, 1), 0)
+    eye = jnp.where(sub == lane, 1.0, 0.0).astype(jnp.float32)
+
+    def step(j, carry):
+        row = d_ref[pl.ds(j, 1), :]
+        d = jnp.sum(jnp.where(lane1 == j, row, 0.0), axis=1, keepdims=True)
+        s = lax.rsqrt(d)
+        c = jnp.where(lane1 >= j, row * s, 0.0)
+        wv = d_ref[...]
+        col = jnp.sum(jnp.where(lane == j, wv, 0.0), axis=1, keepdims=True)
+        ccol = jnp.where(sub1 >= j, col * s, 0.0)
+        d_ref[...] = wv - ccol * c
+        dt_ref[pl.ds(j, 1), :] = c
+        xrow = di_ref[pl.ds(j, 1), :] * s
+        di_ref[...] = di_ref[...] - jnp.where(sub1 > j, ccol, 0.0) * xrow
+        di_ref[pl.ds(j, 1), :] = xrow
+        return carry
+
     inv_diag = []
     for k in range(nb):
-        akk = sym[k * BLK:(k + 1) * BLK, k * BLK:(k + 1) * BLK]
-        for j in range(k):
-            akk = akk - jnp.dot(blk[k][j], blk[k][j].T, precision=EXACT)
-        lkk = jnp.linalg.cholesky(akk)
-        ikk = tri_inverse(lkk)
-        blk[k][k] = lkk
+        lo, hi = k * BLK, (k + 1) * BLK
+        d_ref[...] = w_ref[lo:hi, lo:hi]
+        di_ref[...] = eye
+        lax.fori_loop(0, BLK, step, 0)
+        lkk = dt_ref[...].T
+        ikk = di_ref[...]
+        l_ref[lo:hi, lo:hi] = lkk
+        inv_ref[lo:hi, lo:hi] = ikk
         inv_diag.append(ikk)
         if k + 1 < nb:
-            rest = sym[(k + 1) * BLK:, k * BLK:(k + 1) * BLK]
-            for j in range(k):
-                below = jnp.concatenate([blk[i][j] for i in range(k + 1, nb)], axis=0)
-                rest = rest - jnp.dot(below, blk[k][j].T, precision=EXACT)
-            panel = jnp.dot(rest, ikk.T, precision=EXACT)
-            for i in range(k + 1, nb):
-                blk[i][k] = panel[(i - k - 1) * BLK:(i - k) * BLK]
-    inv = [[None] * nb for _ in range(nb)]
+            panel = _mm_t(w_ref[hi:, lo:hi], ikk)
+            l_ref[hi:, lo:hi] = panel
+            w_ref[hi:, hi:] = w_ref[hi:, hi:] - _mm_t(panel, panel)
     for i in range(nb):
-        inv[i][i] = inv_diag[i]
         for j in range(i - 1, -1, -1):
-            acc = jnp.dot(blk[i][j], inv[j][j], precision=EXACT)
-            for k in range(j + 1, i):
-                acc = acc + jnp.dot(blk[i][k], inv[k][j], precision=EXACT)
-            inv[i][j] = -jnp.dot(inv_diag[i], acc, precision=EXACT)
-    zero = jnp.zeros((BLK, BLK), sym.dtype)
+            acc = _mm(l_ref[i * BLK:(i + 1) * BLK, j * BLK:i * BLK], inv_ref[j * BLK:i * BLK, j * BLK:(j + 1) * BLK])
+            inv_ref[i * BLK:(i + 1) * BLK, j * BLK:(j + 1) * BLK] = -_mm(inv_diag[i], acc)
 
-    def join(parts):
-        return jnp.concatenate(
-            [jnp.concatenate([parts[i][j] if j <= i else zero for j in range(nb)], axis=1) for i in range(nb)],
-            axis=0,
-        )
 
-    return join(blk), join(inv)
+def factor_and_inverse(sym):
+    n = sym.shape[0]
+    return pl.pallas_call(
+        _factor_kernel,
+        out_shape=(jax.ShapeDtypeStruct((n, n), jnp.float32), jax.ShapeDtypeStruct((n, n), jnp.float32)),
+        in_specs=[pl.BlockSpec(memory_space=pltpu.VMEM)],
+        out_specs=(pl.BlockSpec(memory_space=pltpu.VMEM), pl.BlockSpec(memory_space=pltpu.VMEM)),
+        scratch_shapes=[pltpu.VMEM((n, n), jnp.float32)] + [pltpu.VMEM((BLK, BLK), jnp.float32)] * 3,
+    )(sym)
 
 
 def local(front_block, child_blocks, child_rows, child_dest, panel_owner):
@@ -112,7 +136,7 @@
     pivot_block = broadcast_from(panel_part[:PB], owner_index, "grp")
     window_rows = broadcast_from(panel_part[PB:PB + win_cols], owner_index, "grp")
     symmetric = 0.5 * (pivot_block + pivot_block.T)
-    pivot_factor, factor_inverse = cholesky_and_inverse(symmetric)
+    pivot_factor, factor_inverse = factor_and_inverse(symmetric)
     solved = jnp.dot(panel_part, factor_inverse.T, precision=FAST)
     window = jnp.dot(window_rows, factor_inverse.T, precision=FAST)
     schur_part = local_rows[:, PB:] - jnp.dot(solved, window.T, precision=FAST)

time: 241 us -> 210 us (0.87); the launches traced: 236 us -> 208 us
  other arithmetic: 130 us -> 42.5 us
  Pallas kernels: 0 us -> 63.2 us
  matrix products: 44.5 us -> 34.1 us
  local copies, waits for them, and re-layouts: 25.1 us -> 35 us
    another operation x20 -> x0, other arithmetic: 92.4 us -> none  [the longest x12 50 us: cholesky_and_inverse(): lkk = jnp.linalg.cholesky(akk)]
    pallas_call x0 -> x1, Pallas kernels: none -> 63.2 us  [factor_and_inverse(): pl.pallas_call(_factor_kernel, out_shape=(jax.ShapeDtypeStruct((n, n), jn...]
    dot_general x28 -> x0, matrix products: 13.1 us -> none  [the longest x6 4.2 us: cholesky_and_inverse(): akk = akk - jnp.dot(blk[k][j], blk[k][j].T, precision=EXACT)]
    broadcast_in_dim x1, other arithmetic: 4.41 us -> 7.65 us  [local(): return (panel_rows[None], schur_part[None])]
    slice x1, local copies, waits for them, and re-layouts: 0.85 us -> 3.89 us  [local(): panel_rows = jnp.concatenate([top_rows, solved[PB:]], axis=0)]
    unnamed x14 -> x12, local copies, waits for them, and re-layouts: 2.74 us -> 5.28 us
  transfers between devices with their start and end apart: 9 -> 9, of which waited for: 3 -> 3; matrix products, arithmetic and copies ran while one was open for 73% -> 39% of each run, Pallas kernels for 0% -> 30%
where the time goes in v2:
time: 210 us; the launch traced here: 208 us
  Pallas kernels  63.2 us (30%)
  other arithmetic  42.5 us (20%)
  local copies, waits for them, and re-layouts  35 us (17%)
  matrix products  34.1 us (16%)
  starting transfers between devices  18.8 us (9%)
  waiting for transfers between devices  13.3 us (6%)
    pallas_call x1, Pallas kernels, factor_and_inverse(): pl.pallas_call(_factor_kernel, out_shape=(jax.ShapeDtypeStruct((n, n), jn...  63.2 us
    dot_general x1, matrix products, local(): schur_part = local_rows[:, PB:] - jnp.dot(solved, window.T, precision=FAST)  20.2 us
    scatter-add x1, other arithmetic, local(): schur_part.at[flat_rows].add(trailing_rows.reshape(-1, win_cols))  13.8 us
    dot_general x1, matrix products, local(): solved = jnp.dot(panel_part, factor_inverse.T, precision=FAST)  10.1 us
    scatter-add x1, other arithmetic, local(): panel_part = local_rows[:, :PB].at[flat_rows].add(got_panel.reshape(-1, PB))  9.06 us
    slice x1, local copies, waits for them, and re-layouts, local(): panel_part = local_rows[:, :PB].at[flat_rows].add(got_panel.reshape(-1, PB))  7.92 us
    broadcast_in_dim x1, other arithmetic, local(): return (panel_rows[None], schur_part[None])  7.65 us
    all_to_all x1, starting transfers between devices, local(): lax.all_to_all(send_rows, 'front', split_axis=0, concat_axis=0, tiled=True)  7.25 us
  transfers between devices with their start and end apart: 9, of which 3 were waited for; matrix products, arithmetic and copies ran while one was open for 39% of the time, Pallas kernels for 30%

profile of v2, /device:TPU:0, one launch (start us, length us, event | category | flops | bytes accessed | tf_op | source)
XLA Modules:
  0.0 208.4 jit_solution(13831044828161664804)
XLA Ops:
  0.6 0.0 copy-start
  0.6 0.9 convert_reduce_fusion
  1.6 0.7 fusion.12
  2.2 0.0 copy-done
  2.2 1.2 scatter_custom_fusion
  3.4 7.3 %all-to-all-start = ((s32[8,2,16]{2,1,0:T(2,128)}), s32[8,2,16]{2,1,0:T(2,128)S(1)}, u32[]{:S(2)}, u32[]{:S(2)}) async-start(s32[8,2,16]{2,1,0:T(2,128)} %bitcast.7), calls=%async_computation | async-start | bytes 16384 | tf_op jit(solution)/shard_map/all_to_all | solution.py:127
  10.6 0.9 slice.49
  11.6 0.9 broadcast_in_dim.11
  12.4 2.0 scatter_fusion
  14.4 2.7 %all-to-all-done = s32[8,2,16]{2,1,0:T(2,128)S(1)} async-done(((s32[8,2,16]{2,1,0:T(2,128)}), s32[8,2,16]{2,1,0:T(2,128)S(1)}, u32[]{:S(2)}, u32[]{:S(2)}) %all-to-all-start) | async-done | bytes 1056 | tf_op jit(solution)/shard_map/all_to_all | solution.py:127
  17.2 3.5 %all-to-all-start.1 = ((f32[8,2,16,512]{3,2,1,0:T(8,128)}), f32[8,2,16,512]{3,2,1,0:T(8,128)S(1)}, u32[]{:S(2)}, u32[]{:S(2)}) async-start(f32[8,2,16,512]{3,2,1,0:T(8,128)} %bitcast.10), calls=%async_computation.1 | async-start | bytes 1048576 | tf_op jit(solution)/shard_map/all_to_all | solution.py:126
  20.7 7.9 %slice.48 = f32[4096,512]{1,0:T(8,128)} slice(f32[4096,1408]{1,0:T(8,128)} %bitcast.42), slice={[0:4096], [0:512]} | slice | bytes 16777216 | tf_op jit(solution)/shard_map/slice | solution.py:129
  28.6 0.1 reshape.81
  28.7 5.7 %all-to-all-done.1 = f32[8,2,16,512]{3,2,1,0:T(8,128)S(1)} async-done(((f32[8,2,16,512]{3,2,1,0:T(8,128)}), f32[8,2,16,512]{3,2,1,0:T(8,128)S(1)}, u32[]{:S(2)}, u32[]{:S(2)}) %all-to-all-start.1) | async-done | bytes 524320 | tf_op jit(solution)/shard_map/all_to_all | solution.py:126
  34.4 9.1 %scatter_fusion.1 = f32[4096,512]{1,0:T(8,128)} fusion(f32[4096,512]{1,0:T(8,128)} %slice.48, s32[256]{0:T(256)S(1)} %bitcast.47, f32[256,512]{1,0:T(8,128)S(1)} %bitcast.44), kind=kCustom, calls=%fused_computation.2 | custom fusion | flops 131072 | bytes 1573888 | tf_op jit(solution)/shard_map/scatter-add | solution.py:129
  43.5 0.0 copy-start.4
  43.5 1.3 slice.50
  44.8 0.3 copy.24
  45.1 0.1 collective-permute-start
  45.2 2.9 %slice.56 = f32[896,512]{1,0:T(8,128)} slice(f32[4096,512]{1,0:T(8,128)} %scatter_fusion.1), slice={[512:1408], [0:512]} | slice | bytes 3670016 | tf_op jit(solution)/shard_map/slice | solution.py:137
  48.1 0.5 collective-permute-start.3
  49.2 0.0 collective-permute-done
  49.3 0.2 broadcast_select_fusion.2
  49.5 0.1 slice_select_fusion.1
  49.5 1.5 collective-permute-start.1
  51.0 0.0 copy-done.4
  51.0 1.0 broadcast_in_dim.25
  52.0 2.2 %scatter_fusion.2 = f32[16,16,896]{2,1,0:T(8,128)} fusion(f32[16,16,896]{2,1,0:T(8,128)} %broadcast_in_dim.25, s32[4]{0:T(128)S(1)} %fusion.12, f32[4,16,896]{2,1,0:T(8,128)S(1)} %slice.59), kind=kCustom, calls=%fused_computation.3 | custom fusion | bytes 688144 | tf_op jit(solution)/shard_map/scatter | solution.py:17
  54.2 4.4 %all-to-all-start.2 = ((f32[8,2,16,896]{3,2,1,0:T(8,128)}), f32[8,2,16,896]{3,2,1,0:T(8,128)}, u32[]{:S(2)}, u32[]{:S(2)}) async-start(f32[8,2,16,896]{3,2,1,0:T(8,128)} %bitcast.14), calls=%async_computation.2 | async-start | bytes 1835008 | tf_op jit(solution)/shard_map/all_to_all | solution.py:131
  58.6 4.8 %collective-permute-done.1 = f32[256,512]{0,1:T(8,128)S(1)} collective-permute-done((f32[256,512]{0,1:T(8,128)S(1)}, f32[256,512]{0,1:T(8,128)S(1)}, u32[]{:S(2)}, u32[]{:S(2)}) %collective-permute-start.1) | collective-permute-done | bytes 524320 | tf_op jit(solution)/shard_map/ppermute | solution.py:35
  63.5 0.1 broadcast_select_fusion.4
  63.6 0.1 collective-permute-start.2
  63.6 0.0 collective-permute-done.3
  63.7 2.5 %broadcast_select_fusion = f32[896,512]{1,0:T(8,128)S(1)} fusion(f32[896,512]{1,0:T(8,128)} %collective-permute-done.3, pred[]{:T(512)S(6)} %eq.17, f32[4096,512]{1,0:T(8,128)} %scatter_fusion.1), kind=kLoop, calls=%fused_computation.18 | loop fusion | flops 458752 | bytes 5505025 | tf_op jit(solution)/shard_map/jit(_where)/select_n | solution.py:29
  66.1 1.1 slice_select_fusion
  67.3 1.4 collective-permute-start.4
  68.7 0.0 collective-permute-done.2
  68.7 0.2 maximum_select_fusion.2
  68.8 1.3 copy.20
  70.2 2.4 %fusion.6.s_ref = f32[512,512]{1,0:T(8,128)} fusion(f32[512,512]{1,0:T(8,128)} %copy.20, f32[512,512]{0,1:T(8,128)S(1)} %maximum_select_fusion.2), kind=kLoop, calls=%fused_computation.16 | loop fusion | flops 524288 | bytes 3145728 | tf_op jit(solution)/shard_map/mul | solution.py:138
  72.6 63.2 %shard_map.68 = (f32[512,512]{1,0:T(8,128)}, f32[512,512]{1,0:T(8,128)}) custom-call(f32[512,512]{1,0:T(8,128)} %fusion.6.s_ref), custom_call_target="tpu_custom_call" | custom-call | tf_op jit(solution)/shard_map/pallas_call | solution.py:104
  135.8 10.1 %fusion.14 = f32[4096,512]{1,0:T(8,128)S(1)} fusion(f32[4096,512]{1,0:T(8,128)} %scatter_fusion.1, f32[512,512]{1,0:T(8,128)} %get-tuple-element.5), kind=kOutput, calls=%fused_computation.36 | convolution fusion | flops 6442450944 | bytes 17825792 | tf_op jit(solution)/shard_map/dot_general | solution.py:140
  145.9 0.0 copy-start.2
  145.9 1.1 slice.53
  147.0 2.4 %copy-done.2 = f32[4096,512]{1,0:T(8,128)} copy-done((f32[4096,512]{1,0:T(8,128)}, f32[4096,512]{1,0:T(8,128)S(1)}, u32[]{:S(2)}) %copy-start.2) | copy-done | bytes 8388632
  149.4 3.9 %slice.54 = f32[3584,512]{1,0:T(8,128)} slice(f32[4096,512]{1,0:T(8,128)S(1)} %fusion.14), slice={[512:4096], [0:512]} | slice | bytes 14680064 | tf_op jit(solution)/shard_map/slice | solution.py:145
  153.3 1.6 copy.22
  154.9 2.5 %copy.25 = f32[512,512]{0,1:T(8,128)} copy(f32[512,512]{1,0:T(8,128)} %slice.53) | data formatting | bytes 2097152
  157.4 0.0 collective-permute-done.4
  157.4 1.3 broadcast_select_fusion.3
  158.7 0.2 collective-permute-start.5
  158.9 2.4 %broadcast_select_fusion.1 = f32[512,512]{0,1:T(8,128)} fusion(f32[512,512]{0,1:T(8,128)S(1)} %copy.22, f32[512,512]{0,1:T(8,128)} %copy.25, pred[]{:T(512)S(6)} %eq.17), kind=kLoop, calls=%fused_computation.21 | loop fusion | flops 262144 | bytes 3145729 | tf_op jit(solution)/shard_map/jit(_where)/select_n | solution.py:144
  161.3 1.6 copy.23
  162.9 0.0 copy-start.3
  162.9 7.6 %maximum_bitcast_fusion = f32[1,4096,512]{2,1,0:T(8,128)} fusion(f32[3584,512]{1,0:T(8,128)} %slice.54, f32[512,512]{1,0:T(8,128)S(1)} %copy.23), kind=kLoop, calls=%fused_computation.6 | loop fusion | flops 2097152 | bytes 16777216 | tf_op jit(solution)/shard_map/broadcast_in_dim | solution.py:146
  170.5 0.0 collective-permute-done.5
  170.5 0.0 copy-done.3
  170.5 3.8 %fusion = f32[896,512]{1,0:T(8,128)S(1)} fusion(f32[512,512]{1,0:T(8,128)S(1)} %copy-done.3, f32[448,512]{1,0:T(8,128)} %collective-permute-done.5, f32[448,512]{1,0:T(8,128)} %broadcast_select_fusion.3, pred[]{:T(512)S(6)} %eq.34), kind=kOutput, calls=%fused_computation.8 | convolution fusion | flops 1410662400 | bytes 4718593 | tf_op jit(solution)/shard_map/dot_general | solution.py:141
  174.3 0.0 copy-start.1
  174.4 20.2 %slice_subtract_fusion = f32[4096,896]{1,0:T(8,128)} fusion(f32[4096,1408]{1,0:T(8,128)} %bitcast.43, f32[4096,512]{1,0:T(8,128)} %copy-done.2, f32[896,512]{1,0:T(8,128)S(1)} %fusion), kind=kOutput, calls=%fused_computation.5 | convolution fusion | flops 11277959168 | bytes 39583744 | tf_op jit(solution)/shard_map/dot_general | solution.py:142
  194.6 0.0 all-to-all-done.2
  194.6 13.8 %scatter_fusion.3 = f32[4096,896]{1,0:T(8,128)} fusion(f32[4096,896]{1,0:T(8,128)} %slice_subtract_fusion, s32[256]{0:T(256)S(1)} %bitcast.48, f32[256,896]{1,0:T(8,128)} %bitcast.15), kind=kCustom, calls=%fused_computation.4 | custom fusion | flops 229376 | bytes 2753536 | tf_op jit(solution)/shard_map/scatter-add | solution.py:143
  208.4 0.0 copy-done.1
  (2 shorter events, 0.0 us)
Async XLA Ops:
  0.6 1.6 copy-start
  3.4 13.8 %all-to-all-start = ((s32[8,2,16]{2,1,0:T(2,128)}), s32[8,2,16]{2,1,0:T(2,128)S(1)}, u32[]{:S(2)}, u32[]{:S(2)}) async-start(s32[8,2,16]{2,1,0:T(2,128)} %bitcast.7), calls=%async_computation | async-start | bytes 16384 | tf_op jit(solution)/shard_map/all_to_all | solution.py:127
  17.2 17.2 %all-to-all-start.1 = ((f32[8,2,16,512]{3,2,1,0:T(8,128)}), f32[8,2,16,512]{3,2,1,0:T(8,128)S(1)}, u32[]{:S(2)}, u32[]{:S(2)}) async-start(f32[8,2,16,512]{3,2,1,0:T(8,128)} %bitcast.10), calls=%async_computation.1 | async-start | bytes 1048576 | tf_op jit(solution)/shard_map/all_to_all | solution.py:126
  43.5 7.5 %copy-start.4 = (f32[1,1,4,16,1408]{4,3,2,1,0:T(8,128)S(1)}, f32[1,1,4,16,1408]{4,3,2,1,0:T(8,128)}, u32[]{:S(2)}) copy-start(f32[1,1,4,16,1408]{4,3,2,1,0:T(8,128)} %param.6) | copy-start | bytes 1081348
  45.1 4.1 %collective-permute-start = (f32[512,512]{0,1:T(8,128)S(1)}, f32[512,512]{0,1:T(8,128)S(1)}, u32[]{:S(2)}, u32[]{:S(2)}) collective-permute-start(f32[512,512]{0,1:T(8,128)S(1)} %copy.24), channel_id=1, source_target_pairs={{0,1},{1,0},{2,3},{3,2},{4,5},{5,4},{6,7},{7,6},{8,9},{9,8},{10,11... | collective-permute-start | bytes 3145736 | tf_op jit(solution)/shard_map/ppermute | solution.py:28
  48.1 15.5 %collective-permute-start.3 = (f32[896,512]{1,0:T(8,128)}, f32[896,512]{1,0:T(8,128)}, u32[]{:S(2)}, u32[]{:S(2)}) collective-permute-start(f32[896,512]{1,0:T(8,128)} %slice.56), channel_id=1, source_target_pairs={{0,1},{1,0},{2,3},{3,2},{4,5},{5,4},{6,7},{7,6},{8,9},{9,8},{10,11... | collective-permute-start | bytes 5505032 | tf_op jit(solution)/shard_map/ppermute | solution.py:28
  49.5 13.9 %collective-permute-start.1 = (f32[256,512]{0,1:T(8,128)S(1)}, f32[256,512]{0,1:T(8,128)S(1)}, u32[]{:S(2)}, u32[]{:S(2)}) collective-permute-start(f32[256,512]{0,1:T(8,128)S(1)} %slice_select_fusion.1), channel_id=1, source_target_pairs={{0,2},{1,3},{2,0},{3,1},{4,6},{5,7},{6,4},{7,5},{8,10},{9,11},{10,... | collective-permute-start | bytes 1572872 | tf_op jit(solution)/shard_map/ppermute | solution.py:35
  54.2 140.4 %all-to-all-start.2 = ((f32[8,2,16,896]{3,2,1,0:T(8,128)}), f32[8,2,16,896]{3,2,1,0:T(8,128)}, u32[]{:S(2)}, u32[]{:S(2)}) async-start(f32[8,2,16,896]{3,2,1,0:T(8,128)} %bitcast.14), calls=%async_computation.2 | async-start | bytes 1835008 | tf_op jit(solution)/shard_map/all_to_all | solution.py:131
  63.6 5.1 %collective-permute-start.2 = (f32[256,512]{0,1:T(8,128)S(1)}, f32[256,512]{0,1:T(8,128)S(1)}, u32[]{:S(2)}, u32[]{:S(2)}) collective-permute-start(f32[256,512]{0,1:T(8,128)S(1)} %broadcast_select_fusion.4), channel_id=1, source_target_pairs={{0,1},{1,0},{2,3},{3,2},{4,5},{5,4},{6,7},{7,6},{8,9},{9,8},{10,11... | collective-permute-start | bytes 1572872 | tf_op jit(solution)/shard_map/ppermute | solution.py:38
  67.3 90.1 %collective-permute-start.4 = (f32[448,512]{1,0:T(8,128)}, f32[448,512]{1,0:T(8,128)}, u32[]{:S(2)}, u32[]{:S(2)}) collective-permute-start(f32[448,512]{1,0:T(8,128)} %slice_select_fusion), channel_id=1, source_target_pairs={{0,2},{1,3},{2,0},{3,1},{4,6},{5,7},{6,4},{7,5},{8,10},{9,11},{10,... | collective-permute-start | bytes 2752520 | tf_op jit(solution)/shard_map/ppermute | solution.py:35
  145.9 3.5 %copy-start.2 = (f32[4096,512]{1,0:T(8,128)}, f32[4096,512]{1,0:T(8,128)S(1)}, u32[]{:S(2)}) copy-start(f32[4096,512]{1,0:T(8,128)S(1)} %fusion.14) | copy-start | bytes 25165828
  158.7 11.9 %collective-permute-start.5 = (f32[448,512]{1,0:T(8,128)}, f32[448,512]{1,0:T(8,128)}, u32[]{:S(2)}, u32[]{:S(2)}) collective-permute-start(f32[448,512]{1,0:T(8,128)} %broadcast_select_fusion.3), channel_id=1, source_target_pairs={{0,1},{1,0},{2,3},{3,2},{4,5},{5,4},{6,7},{7,6},{8,9},{9,8},{10,11... | collective-permute-start | bytes 2752520 | tf_op jit(solution)/shard_map/ppermute | solution.py:38
  162.9 7.7 %copy-start.3 = (f32[512,512]{1,0:T(8,128)S(1)}, f32[512,512]{1,0:T(8,128)}, u32[]{:S(2)}) copy-start(f32[512,512]{1,0:T(8,128)} %get-tuple-element.5) | copy-start | bytes 3145732
  174.3 34.1 %copy-start.1 = (s32[1,1,4,16]{3,2,1,0:T(4,128)S(1)}, s32[1,1,4,16]{3,2,1,0:T(4,128)}, u32[]{:S(2)}) copy-start(s32[1,1,4,16]{3,2,1,0:T(4,128)} %param.7) | copy-start | bytes 772

commit v3 on v2

--- a/solution.py
+++ b/solution.py
@@ -112,6 +112,8 @@
 
 def local(front_block, child_blocks, child_rows, child_dest, panel_owner):
     local_rows = front_block[0]
+    row_count, col_count = local_rows.shape
+    win_cols = col_count - PB
     front_count = lax.axis_size("front")
     blocks = child_blocks[0, 0]
     row_lists = child_rows[0, 0]
@@ -122,27 +124,35 @@
     earlier = position[None, :] < position[:, None]
     slot_index = target_front * CAP + jnp.sum((same_front & earlier).astype(jnp.int32), axis=1)
     send_rows = pack_slots(row_lists, slot_index, front_count)
-    send_panel = pack_slots(blocks[:, :, :PB], slot_index, front_count)
-    got_panel = lax.all_to_all(send_panel, "front", split_axis=0, concat_axis=0, tiled=True)
+    send_blocks = pack_slots(blocks, slot_index, front_count)
     got_rows = lax.all_to_all(send_rows, "front", split_axis=0, concat_axis=0, tiled=True)
+    got_blocks = lax.all_to_all(send_blocks, "front", split_axis=0, concat_axis=0, tiled=True)
     flat_rows = got_rows.reshape(-1)
-    panel_part = local_rows[:, :PB].at[flat_rows].add(got_panel.reshape(-1, PB))
-    send_trail = pack_slots(blocks[:, :, PB:], slot_index, front_count)
-    trailing_rows = lax.all_to_all(send_trail, "front", split_axis=0, concat_axis=0, tiled=True)
-    win_cols = local_rows.shape[1] - PB
+    got_blocks = got_blocks.reshape(-1, col_count)
+    got_panel = got_blocks[:, :PB]
+    got_trail = got_blocks[:, PB:]
     owner_index = panel_owner[0]
     is_owner = lax.axis_index("grp") == owner_index
 
-    pivot_block = broadcast_from(panel_part[:PB], owner_index, "grp")
-    window_rows = broadcast_from(panel_part[PB:PB + win_cols], owner_index, "grp")
+    top_count = PB + win_cols
+    top_hits = (jnp.arange(top_count, dtype=jnp.int32)[:, None] == flat_rows[None, :]).astype(jnp.float32)
+    top_rows = local_rows[:top_count, :PB] + jnp.dot(top_hits, got_panel, precision=EXACT)
+    pivot_block = broadcast_from(top_rows[:PB], owner_index, "grp")
+    window_rows = broadcast_from(top_rows[PB:], owner_index, "grp")
     symmetric = 0.5 * (pivot_block + pivot_block.T)
     pivot_factor, factor_inverse = factor_and_inverse(symmetric)
-    solved = jnp.dot(panel_part, factor_inverse.T, precision=FAST)
+
+    hits = (jnp.arange(row_count, dtype=jnp.int32)[:, None] == flat_rows[None, :]).astype(jnp.float32)
+    child_solved = jnp.dot(got_panel, factor_inverse.T, precision=EXACT)
+    solved = jnp.dot(local_rows[:, :PB], factor_inverse.T, precision=FAST) + jnp.dot(hits, child_solved, precision=FAST)
     window = jnp.dot(window_rows, factor_inverse.T, precision=FAST)
-    schur_part = local_rows[:, PB:] - jnp.dot(solved, window.T, precision=FAST)
-    schur_part = schur_part.at[flat_rows].add(trailing_rows.reshape(-1, win_cols))
-    top_rows = jnp.where(is_owner, pivot_factor, solved[:PB])
-    panel_rows = jnp.concatenate([top_rows, solved[PB:]], axis=0)
+    schur_part = (
+        local_rows[:, PB:]
+        - jnp.dot(solved, window.T, precision=FAST)
+        + jnp.dot(hits, got_trail, precision=FAST)
+    )
+    head = jnp.where(is_owner, pivot_factor, solved[:PB])
+    panel_rows = lax.dynamic_update_slice(solved, head, (0, 0))
     return (panel_rows[None], schur_part[None])
 
 

time: 210 us -> 258 us (1.23)
  local copies, waits for them, and re-layouts: 35 us -> 75.8 us
  other arithmetic: 42.5 us -> 10.1 us
  matrix products: 34.1 us -> 61.6 us
  waiting for transfers between devices: 13.3 us -> 25.9 us
    unnamed x12 -> x24, local copies, waits for them, and re-layouts: 5.28 us -> 57.6 us
    dot_general x2 -> x6, matrix products: 30.3 us -> 56.3 us  [the longest x1 17.4 us: local(): jnp.dot(solved, window.T, precision=FAST)]
    scatter-add x2 -> x0, other arithmetic: 22.9 us -> none  [the longest x1 13.8 us: local(): schur_part.at[flat_rows].add(trailing_rows.reshape(-1, win_cols))]
    slice x7 -> x2, local copies, waits for them, and re-layouts: 18.1 us -> 2.46 us  [the longest x1 1.35 us: local(): window_rows = broadcast_from(top_rows[PB:], owner_index, 'grp')]
    ppermute x2, waiting for transfers between devices: 4.83 us -> 12.6 us  [broadcast_from(): got = lax.ppermute(half, axis, pairs(size, bit))]
    broadcast_in_dim x1 -> x0, other arithmetic: 7.65 us -> none  [local(): return (panel_rows[None], schur_part[None])]
    ppermute x0 -> x2, local copies, waits for them, and re-layouts: none -> 5.12 us  [the longest x1 2.63 us: broadcast_from(): got = lax.ppermute(half, axis, pairs(size, bit))]
    all_to_all x2 -> x1, starting transfers between devices: 7.91 us -> 3.58 us  [local(): lax.all_to_all(send_blocks, 'front', split_axis=0, concat_axis=0, tiled=T...]
  transfers between devices with their start and end apart: 9 -> 8, of which waited for: 3 -> 4; matrix products, arithmetic and copies ran while one was open for 39% -> 27% of each run, Pallas kernels for 30% -> 25%
where the time goes in v3:
time: 258 us; the launch traced here: 256 us
  local copies, waits for them, and re-layouts  75.8 us (29%)
  Pallas kernels  63.3 us (25%)
  matrix products  61.6 us (24%)
  waiting for transfers between devices  25.9 us (10%)
  starting transfers between devices  17.6 us (7%)
  other arithmetic  10.1 us (4%)
    pallas_call x1, Pallas kernels, factor_and_inverse(): pl.pallas_call(_factor_kernel, out_shape=(jax.ShapeDtypeStruct((n, n), jn...  63.3 us
    unnamed x24, local copies, waits for them, and re-layouts  57.6 us
    dot_general x1, matrix products, local(): jnp.dot(solved, window.T, precision=FAST)  17.4 us
    dot_general x1, matrix products, local(): jnp.dot(hits, got_trail, precision=FAST)  16.5 us
    ppermute x2, waiting for transfers between devices, broadcast_from(): got = lax.ppermute(half, axis, pairs(size, bit))  12.6 us
    dot_general x1, matrix products, local(): jnp.dot(local_rows[:, :PB], factor_inverse.T, precision=FAST)  10.6 us
    all_to_all x1, waiting for transfers between devices, local(): lax.all_to_all(send_blocks, 'front', split_axis=0, concat_axis=0, tiled=T...  10 us
    all_to_all x1, starting transfers between devices, local(): lax.all_to_all(send_rows, 'front', split_axis=0, concat_axis=0, tiled=True)  7.25 us
  transfers between devices with their start and end apart: 8, of which 4 were waited for; matrix products, arithmetic and copies ran while one was open for 27% of the time, Pallas kernels for 25%

profile of v3, /device:TPU:0, one launch (start us, length us, event | category | flops | bytes accessed | tf_op | source)
XLA Modules:
  0.0 255.8 jit_solution(2609033197766742886)
XLA Ops:
  0.6 0.0 copy-start
  0.6 0.9 convert_reduce_fusion
  1.6 0.7 fusion.28
  2.2 0.0 copy-done
  2.2 1.2 scatter_custom_fusion
  3.4 7.3 %all-to-all-start = ((s32[8,2,16]{2,1,0:T(2,128)}), s32[8,2,16]{2,1,0:T(2,128)S(1)}, u32[]{:S(2)}, u32[]{:S(2)}) async-start(s32[8,2,16]{2,1,0:T(2,128)} %bitcast.7), calls=%async_computation | async-start | bytes 16384 | tf_op jit(solution)/shard_map/all_to_all | solution.py:128
  10.6 1.2 broadcast_in_dim.21
  11.8 2.5 scatter_fusion
  14.3 2.9 %all-to-all-done = s32[8,2,16]{2,1,0:T(2,128)S(1)} async-done(((s32[8,2,16]{2,1,0:T(2,128)}), s32[8,2,16]{2,1,0:T(2,128)S(1)}, u32[]{:S(2)}, u32[]{:S(2)}) %all-to-all-start) | async-done | bytes 1056 | tf_op jit(solution)/shard_map/all_to_all | solution.py:128
  17.2 3.6 %all-to-all-start.1 = ((f32[8,2,16,1408]{3,2,1,0:T(8,128)}), f32[8,2,16,1408]{3,2,1,0:T(8,128)S(1)}, u32[]{:S(2)}, u32[]{:S(2)}) async-start(f32[8,2,16,1408]{3,2,1,0:T(8,128)} %bitcast.9), calls=%async_computation.1 | async-start | bytes 2883584 | tf_op jit(solution)/shard_map/all_to_all | solution.py:129
  20.7 23.3 %copy.30 = f32[1,4096,1408]{1,2,0:T(8,128)} copy(f32[1,4096,1408]{2,1,0:T(8,128)} %param.5) | data formatting | bytes 46137344 | tf_op args[0]
  44.1 0.1 eq.69
  44.2 10.0 %all-to-all-done.1 = f32[8,2,16,1408]{3,2,1,0:T(8,128)S(1)} async-done(((f32[8,2,16,1408]{3,2,1,0:T(8,128)}), f32[8,2,16,1408]{3,2,1,0:T(8,128)S(1)}, u32[]{:S(2)}, u32[]{:S(2)}) %all-to-all-start.1) | async-done | bytes 1441824 | tf_op jit(solution)/shard_map/all_to_all | solution.py:129
  54.2 1.1 copy-done.8
  55.3 3.5 %convolution_add_fusion = f32[1408,512]{0,1:T(8,128)S(1)} fusion(f32[4096,1408]{0,1:T(8,128)} %bitcast.43, s32[256]{0:T(256)S(1)} %eq.69, f32[256,1408]{1,0:T(8,128)} %bitcast.46), kind=kOutput, calls=%fused_computation.10 | convolution fusion | flops 2215673856 | bytes 6292480 | tf_op jit(solution)/shard_map/dot_general | solution.py:139
  58.8 1.1 slice.50
  59.9 0.0 collective-permute-start
  60.0 1.3 slice.56
  61.3 0.5 collective-permute-start.3
  62.5 0.5 collective-permute-done
  63.0 0.2 broadcast_select_fusion.2
  63.1 0.0 copy-start.7
  63.1 1.0 copy-done.7
  64.1 0.1 slice_select_fusion.2
  64.2 2.8 %collective-permute-start.1 = (f32[256,512]{0,1:T(8,128)S(1)}, f32[256,512]{0,1:T(8,128)}, u32[]{:S(2)}, u32[]{:S(2)}) collective-permute-start(f32[256,512]{0,1:T(8,128)S(1)} %slice_select_fusion.2), channel_id=1, source_target_pairs={{0,2},{1,3},{2,0},{3,1},{4,6},{5,7},{6,4},{7,5},{8,10},{9,11},{10,... | collective-permute-start | bytes 1572872 | tf_op jit(solution)/shard_map/ppermute | solution.py:35
  67.0 12.6 %collective-permute-done.1 = f32[256,512]{0,1:T(8,128)} collective-permute-done((f32[256,512]{0,1:T(8,128)S(1)}, f32[256,512]{0,1:T(8,128)}, u32[]{:S(2)}, u32[]{:S(2)}) %collective-permute-start.1) | collective-permute-done | bytes 524320 | tf_op jit(solution)/shard_map/ppermute | solution.py:35
  79.5 1.3 broadcast_select_fusion.3
  80.8 0.1 collective-permute-start.2
  80.9 0.0 collective-permute-done.3
  80.9 0.3 broadcast_select_fusion
  81.2 0.0 copy-start.3
  81.2 1.2 copy-done.3
  82.5 0.3 slice_select_fusion
  82.8 1.3 copy.35
  84.1 3.2 %collective-permute-start.4 = (f32[448,512]{1,0:T(8,128)}, f32[448,512]{1,0:T(8,128)}, u32[]{:S(2)}, u32[]{:S(2)}) collective-permute-start(f32[448,512]{1,0:T(8,128)} %copy.35), channel_id=1, source_target_pairs={{0,2},{1,3},{2,0},{3,1},{4,6},{5,7},{6,4},{7,5},{8,10},{9,11},{10,... | collective-permute-start | bytes 2752520 | tf_op jit(solution)/shard_map/ppermute | solution.py:35
  87.3 0.0 collective-permute-done.2
  87.3 1.4 maximum_select_fusion.2
  88.7 0.3 copy.32
  89.1 1.2 fusion.17.s_ref
  90.3 63.3 %shard_map.68 = (f32[512,512]{1,0:T(8,128)}, f32[512,512]{1,0:T(8,128)}) custom-call(f32[512,512]{1,0:T(8,128)} %fusion.17.s_ref), custom_call_target="tpu_custom_call" | custom-call | tf_op jit(solution)/shard_map/pallas_call | solution.py:104
  153.6 2.4 fusion.21
  156.0 5.8 %fusion.6 = f32[4096,512]{0,1:T(8,128)} fusion(f32[256,512]{1,0:T(8,128)S(1)} %fusion.21, s32[256]{0:T(256)S(1)} %eq.69), kind=kOutput, calls=%fused_computation.9 | convolution fusion | flops 3222274048 | bytes 8913920 | tf_op jit(solution)/shard_map/dot_general | solution.py:147
  161.8 0.0 collective-permute-done.4
  161.8 2.6 %copy.36 = f32[448,512]{0,1:T(8,128)} copy(f32[448,512]{1,0:T(8,128)} %collective-permute-done.4) | data formatting | bytes 1835008 | tf_op jit(solution)/shard_map/ppermute | solution.py:35
  164.4 0.0 copy-done.4
  164.5 1.4 broadcast_select_fusion.1
  165.8 2.5 copy.37
  168.3 0.2 collective-permute-start.5
  168.5 0.0 copy-done.5
  168.5 10.6 %bitcast_add_fusion = f32[4096,512]{0,1:T(8,128)S(1)} fusion(f32[4096,512]{0,1:T(8,128)} %fusion.6, f32[512,512]{1,0:T(8,128)S(1)} %copy-done.5, f32[4096,1408]{0,1:T(8,128)} %bitcast.44), kind=kOutput, calls=%fused_computation.7 | convolution fusion | flops 6444548096 | bytes 26214400 | tf_op jit(solution)/shard_map/dot_general | solution.py:147
  179.1 0.0 copy-start.2
  179.2 3.4 %copy.49 = f32[1,4096,512]{1,2,0:T(8,128)} copy(f32[1,4096,512]{1,2,0:T(8,128)S(1)} %bitcast.42) | data formatting | bytes 16777216
  182.6 2.4 copy-done.2
  185.0 1.6 copy.34
  186.5 2.4 fusion.16
  189.0 9.0 %copy.42 = f32[1,4096,512]{2,1,0:T(8,128)} copy(f32[1,4096,512]{1,2,0:T(8,128)} %fusion.16) | data formatting | bytes 16777216
  198.0 0.0 collective-permute-done.5
  198.0 2.5 copy.38
  200.5 0.0 copy-done.6
  200.5 5.3 %fusion.9 = f32[896,512]{1,0:T(8,128)S(1)} fusion(f32[512,512]{1,0:T(8,128)S(1)} %copy-done.5, f32[448,512]{0,1:T(8,128)} %copy.38, f32[448,512]{0,1:T(8,128)S(1)} %copy-done.6, pred[]{:T(512)S(6)} %eq.31), kind=kOutput, calls=%fused_computation.14 | convolution fusion | flops 1410662400 | bytes 4718593 | tf_op jit(solution)/shard_map/dot_general | solution.py:148
  205.8 0.0 copy-start.9
  205.8 17.4 %fusion.30 = f32[4096,896]{0,1:T(8,128)} fusion(f32[4096,512]{0,1:T(8,128)} %copy-done.2, f32[896,512]{1,0:T(8,128)S(1)} %fusion.9), kind=kOutput, calls=%fused_computation.49 | convolution fusion | flops 11274289152 | bytes 24903680 | tf_op jit(solution)/shard_map/dot_general | solution.py:151
  223.1 16.5 %fusion.1 = f32[1,4096,896]{1,2,0:T(8,128)} fusion(f32[4096,896]{0,1:T(8,128)} %fusion.30, f32[4096,1408]{0,1:T(8,128)} %bitcast.45, s32[256]{0:T(256)S(1)} %eq.69, f32[256,1408]{1,0:T(8,128)S(1)} %bitcast.48), kind=kOutput, calls=%fused_computation.4 | convolution fusion | flops 5645533184 | bytes 44958720 | tf_op jit(solution)/shard_map/dot_general | solution.py:152
  239.7 16.1 %copy.43 = f32[1,4096,896]{2,1,0:T(8,128)} copy(f32[1,4096,896]{1,2,0:T(8,128)} %fusion.1) | data formatting | bytes 29360128
  (7 shorter events, 0.0 us)
Async XLA Ops:
  0.6 1.6 copy-start
  3.4 13.8 %all-to-all-start = ((s32[8,2,16]{2,1,0:T(2,128)}), s32[8,2,16]{2,1,0:T(2,128)S(1)}, u32[]{:S(2)}, u32[]{:S(2)}) async-start(s32[8,2,16]{2,1,0:T(2,128)} %bitcast.7), calls=%async_computation | async-start | bytes 16384 | tf_op jit(solution)/shard_map/all_to_all | solution.py:128
  17.2 37.0 %all-to-all-start.1 = ((f32[8,2,16,1408]{3,2,1,0:T(8,128)}), f32[8,2,16,1408]{3,2,1,0:T(8,128)S(1)}, u32[]{:S(2)}, u32[]{:S(2)}) async-start(f32[8,2,16,1408]{3,2,1,0:T(8,128)} %bitcast.9), calls=%async_computation.1 | async-start | bytes 2883584 | tf_op jit(solution)/shard_map/all_to_all | solution.py:129
  54.2 1.1 copy-start.8
  59.9 3.0 %collective-permute-start = (f32[512,512]{0,1:T(8,128)}, f32[512,512]{0,1:T(8,128)}, u32[]{:S(2)}, u32[]{:S(2)}) collective-permute-start(f32[512,512]{0,1:T(8,128)} %slice.50), channel_id=1, source_target_pairs={{0,1},{1,0},{2,3},{3,2},{4,5},{5,4},{6,7},{7,6},{8,9},{9,8},{10,11... | collective-permute-start | bytes 3145736 | tf_op jit(solution)/shard_map/ppermute | solution.py:28
  61.3 19.6 %collective-permute-start.3 = (f32[896,512]{0,1:T(8,128)}, f32[896,512]{0,1:T(8,128)}, u32[]{:S(2)}, u32[]{:S(2)}) collective-permute-start(f32[896,512]{0,1:T(8,128)} %slice.56), channel_id=1, source_target_pairs={{0,1},{1,0},{2,3},{3,2},{4,5},{5,4},{6,7},{7,6},{8,9},{9,8},{10,11... | collective-permute-start | bytes 5505032 | tf_op jit(solution)/shard_map/ppermute | solution.py:28
  63.1 1.0 copy-start.7
  64.2 15.4 %collective-permute-start.1 = (f32[256,512]{0,1:T(8,128)S(1)}, f32[256,512]{0,1:T(8,128)}, u32[]{:S(2)}, u32[]{:S(2)}) collective-permute-start(f32[256,512]{0,1:T(8,128)S(1)} %slice_select_fusion.2), channel_id=1, source_target_pairs={{0,2},{1,3},{2,0},{3,1},{4,6},{5,7},{6,4},{7,5},{8,10},{9,11},{10,... | collective-permute-start | bytes 1572872 | tf_op jit(solution)/shard_map/ppermute | solution.py:35
  80.8 6.5 %collective-permute-start.2 = (f32[256,512]{0,1:T(8,128)S(1)}, f32[256,512]{0,1:T(8,128)}, u32[]{:S(2)}, u32[]{:S(2)}) collective-permute-start(f32[256,512]{0,1:T(8,128)S(1)} %broadcast_select_fusion.3), channel_id=1, source_target_pairs={{0,1},{1,0},{2,3},{3,2},{4,5},{5,4},{6,7},{7,6},{8,9},{9,8},{10,11... | collective-permute-start | bytes 1572872 | tf_op jit(solution)/shard_map/ppermute | solution.py:38
  81.2 1.2 copy-start.3
  84.1 77.7 %collective-permute-start.4 = (f32[448,512]{1,0:T(8,128)}, f32[448,512]{1,0:T(8,128)}, u32[]{:S(2)}, u32[]{:S(2)}) collective-permute-start(f32[448,512]{1,0:T(8,128)} %copy.35), channel_id=1, source_target_pairs={{0,2},{1,3},{2,0},{3,1},{4,6},{5,7},{6,4},{7,5},{8,10},{9,11},{10,... | collective-permute-start | bytes 2752520 | tf_op jit(solution)/shard_map/ppermute | solution.py:35
  161.8 2.6 %copy-start.4 = (f32[896,512]{0,1:T(8,128)S(1)}, f32[896,512]{0,1:T(8,128)}, u32[]{:S(2)}) copy-start(f32[896,512]{0,1:T(8,128)} %copy-done.3) | copy-start | bytes 5505028
  164.5 4.0 %copy-start.5 = (f32[512,512]{1,0:T(8,128)S(1)}, f32[512,512]{1,0:T(8,128)}, u32[]{:S(2)}) copy-start(f32[512,512]{1,0:T(8,128)} %get-tuple-element.4) | copy-start | bytes 3145732
  168.3 29.7 %collective-permute-start.5 = (f32[448,512]{1,0:T(8,128)}, f32[448,512]{1,0:T(8,128)}, u32[]{:S(2)}, u32[]{:S(2)}) collective-permute-start(f32[448,512]{1,0:T(8,128)} %copy.37), channel_id=1, source_target_pairs={{0,1},{1,0},{2,3},{3,2},{4,5},{5,4},{6,7},{7,6},{8,9},{9,8},{10,11... | collective-permute-start | bytes 2752520 | tf_op jit(solution)/shard_map/ppermute | solution.py:38
  179.1 5.8 %copy-start.2 = (f32[4096,512]{0,1:T(8,128)}, f32[4096,512]{0,1:T(8,128)S(1)}, u32[]{:S(2)}) copy-start(f32[4096,512]{0,1:T(8,128)S(1)} %bitcast_add_fusion) | copy-start | bytes 25165828
  189.0 11.5 %copy-start.6 = (f32[448,512]{0,1:T(8,128)S(1)}, f32[448,512]{0,1:T(8,128)}, u32[]{:S(2)}) copy-start(f32[448,512]{0,1:T(8,128)} %broadcast_select_fusion.1) | copy-start | bytes 2752516
  205.8 17.4 %copy-start.9 = (f32[8,2,16,1408]{3,2,1,0:T(8,128)S(1)}, f32[8,2,16,1408]{3,2,1,0:T(8,128)}, u32[]{:S(2)}) copy-start(f32[8,2,16,1408]{3,2,1,0:T(8,128)} %copy-done.8) | copy-start | bytes 4325380
  239.7 16.1 %copy-start.1 = (s32[1,1,4,16]{3,2,1,0:T(4,128)S(1)}, s32[1,1,4,16]{3,2,1,0:T(4,128)}, u32[]{:S(2)}) copy-start(s32[1,1,4,16]{3,2,1,0:T(4,128)} %param.7) | copy-start | bytes 772

commit v4 on v2

--- a/solution.py
+++ b/solution.py
@@ -141,8 +141,8 @@
     window = jnp.dot(window_rows, factor_inverse.T, precision=FAST)
     schur_part = local_rows[:, PB:] - jnp.dot(solved, window.T, precision=FAST)
     schur_part = schur_part.at[flat_rows].add(trailing_rows.reshape(-1, win_cols))
-    top_rows = jnp.where(is_owner, pivot_factor, solved[:PB])
-    panel_rows = jnp.concatenate([top_rows, solved[PB:]], axis=0)
+    head = jnp.where(is_owner, pivot_factor, solved[:PB])
+    panel_rows = lax.dynamic_update_slice(solved, head, (0, 0))
     return (panel_rows[None], schur_part[None])
 
 

time: 210 us -> 209 us (level)
  waiting for transfers between devices: 13.3 us -> 20.9 us
  other arithmetic: 42.5 us -> 35.9 us
    ppermute x2, waiting for transfers between devices: 4.83 us -> 12.4 us  [broadcast_from(): got = lax.ppermute(half, axis, pairs(size, bit))]
    broadcast_in_dim x1, other arithmetic: 7.65 us -> 1.18 us  [local(): return (panel_rows[None], schur_part[None])]
    slice x2 -> x1, local copies, waits for them, and re-layouts: 5.02 us -> 1.04 us  [local(): head = jnp.where(is_owner, pivot_factor, solved[:PB])]
    select_n x1 -> x0, other arithmetic: 2.43 us -> none  [local(): top_rows = jnp.where(is_owner, pivot_factor, solved[:PB])]
    unnamed x12 -> x8, local copies, waits for them, and re-layouts: 5.28 us -> 5.29 us
  transfers between devices with their start and end apart: 9 -> 9, of which waited for: 3 -> 3; matrix products, arithmetic and copies ran while one was open for 39% -> 34% of each run, Pallas kernels for 30% -> 30%
where the time goes in v4:
time: 209 us; the launch traced here: 207 us
  Pallas kernels  63.1 us (30%)
  other arithmetic  35.9 us (17%)
  matrix products  34.2 us (16%)
  local copies, waits for them, and re-layouts  33 us (16%)
  waiting for transfers between devices  20.9 us (10%)
  starting transfers between devices  18.9 us (9%)
    pallas_call x1, Pallas kernels, factor_and_inverse(): pl.pallas_call(_factor_kernel, out_shape=(jax.ShapeDtypeStruct((n, n), jn...  63.1 us
    dot_general x1, matrix products, local(): schur_part = local_rows[:, PB:] - jnp.dot(solved, window.T, precision=FAST)  20.5 us
    scatter-add x1, other arithmetic, local(): schur_part.at[flat_rows].add(trailing_rows.reshape(-1, win_cols))  13.9 us
    ppermute x2, waiting for transfers between devices, broadcast_from(): got = lax.ppermute(half, axis, pairs(size, bit))  12.4 us
    dot_general x1, matrix products, local(): solved = jnp.dot(panel_part, factor_inverse.T, precision=FAST)  9.77 us
    scatter-add x1, other arithmetic, local(): panel_part = local_rows[:, :PB].at[flat_rows].add(got_panel.reshape(-1, PB))  9.03 us
    slice x1, local copies, waits for them, and re-layouts, local(): panel_part = local_rows[:, :PB].at[flat_rows].add(got_panel.reshape(-1, PB))  7.92 us
    all_to_all x1, starting transfers between devices, local(): lax.all_to_all(send_rows, 'front', split_axis=0, concat_axis=0, tiled=True)  7.25 us
  transfers between devices with their start and end apart: 9, of which 3 were waited for; matrix products, arithmetic and copies ran while one was open for 34% of the time, Pallas kernels for 30%

profile of v4, /device:TPU:0, one launch (start us, length us, event | category | flops | bytes accessed | tf_op | source)
XLA Modules:
  0.0 207.5 jit_solution(3244486085970804470)
XLA Ops:
  0.6 0.0 copy-start
  0.6 0.9 convert_reduce_fusion
  1.6 0.7 fusion.12
  2.2 0.0 copy-done
  2.2 1.2 scatter_custom_fusion
  3.4 7.3 %all-to-all-start = ((s32[8,2,16]{2,1,0:T(2,128)}), s32[8,2,16]{2,1,0:T(2,128)S(1)}, u32[]{:S(2)}, u32[]{:S(2)}) async-start(s32[8,2,16]{2,1,0:T(2,128)} %bitcast.6), calls=%async_computation | async-start | bytes 16384 | tf_op jit(solution)/shard_map/all_to_all | solution.py:127
  10.6 0.9 slice.45
  11.6 0.9 broadcast_in_dim.25
  12.4 2.0 scatter_fusion
  14.4 2.7 %all-to-all-done = s32[8,2,16]{2,1,0:T(2,128)S(1)} async-done(((s32[8,2,16]{2,1,0:T(2,128)}), s32[8,2,16]{2,1,0:T(2,128)S(1)}, u32[]{:S(2)}, u32[]{:S(2)}) %all-to-all-start) | async-done | bytes 1056 | tf_op jit(solution)/shard_map/all_to_all | solution.py:127
  17.2 3.5 %all-to-all-start.1 = ((f32[8,2,16,512]{3,2,1,0:T(8,128)}), f32[8,2,16,512]{3,2,1,0:T(8,128)S(1)}, u32[]{:S(2)}, u32[]{:S(2)}) async-start(f32[8,2,16,512]{3,2,1,0:T(8,128)} %bitcast.9), calls=%async_computation.1 | async-start | bytes 1048576 | tf_op jit(solution)/shard_map/all_to_all | solution.py:126
  20.7 7.9 %slice.44 = f32[4096,512]{1,0:T(8,128)} slice(f32[4096,1408]{1,0:T(8,128)} %bitcast.44), slice={[0:4096], [0:512]} | slice | bytes 16777216 | tf_op jit(solution)/shard_map/slice | solution.py:129
  28.6 0.1 reshape.83
  28.7 5.7 %all-to-all-done.1 = f32[8,2,16,512]{3,2,1,0:T(8,128)S(1)} async-done(((f32[8,2,16,512]{3,2,1,0:T(8,128)}), f32[8,2,16,512]{3,2,1,0:T(8,128)S(1)}, u32[]{:S(2)}, u32[]{:S(2)}) %all-to-all-start.1) | async-done | bytes 524320 | tf_op jit(solution)/shard_map/all_to_all | solution.py:126
  34.4 9.0 %scatter_fusion.1 = f32[4096,512]{1,0:T(8,128)} fusion(f32[4096,512]{1,0:T(8,128)} %slice.44, s32[256]{0:T(256)S(1)} %bitcast.49, f32[256,512]{1,0:T(8,128)S(1)} %bitcast.46), kind=kCustom, calls=%fused_computation.2 | custom fusion | flops 131072 | bytes 1573888 | tf_op jit(solution)/shard_map/scatter-add | solution.py:129
  43.4 1.3 slice.46
  44.7 0.3 copy.24
  45.1 0.1 collective-permute-start
  45.1 2.9 %slice.51 = f32[896,512]{1,0:T(8,128)} slice(f32[4096,512]{1,0:T(8,128)} %scatter_fusion.1), slice={[512:1408], [0:512]} | slice | bytes 3670016 | tf_op jit(solution)/shard_map/slice | solution.py:137
  48.0 0.5 collective-permute-start.3
  49.2 0.0 collective-permute-done
  49.2 0.2 broadcast_select_fusion.1
  49.4 0.1 slice_select_fusion.1
  49.5 1.5 collective-permute-start.1
  51.0 12.4 %collective-permute-done.1 = f32[256,512]{0,1:T(8,128)S(1)} collective-permute-done((f32[256,512]{0,1:T(8,128)S(1)}, f32[256,512]{0,1:T(8,128)S(1)}, u32[]{:S(2)}, u32[]{:S(2)}) %collective-permute-start.1) | collective-permute-done | bytes 524320 | tf_op jit(solution)/shard_map/ppermute | solution.py:35
  63.4 0.1 broadcast_select_fusion.3
  63.5 0.1 collective-permute-start.2
  63.6 0.0 collective-permute-done.3
  63.6 2.5 %broadcast_select_fusion = f32[896,512]{1,0:T(8,128)S(1)} fusion(f32[896,512]{1,0:T(8,128)} %collective-permute-done.3, pred[]{:T(512)S(6)} %eq.39, f32[4096,512]{1,0:T(8,128)} %scatter_fusion.1), kind=kLoop, calls=%fused_computation.18 | loop fusion | flops 458752 | bytes 5505025 | tf_op jit(solution)/shard_map/jit(_where)/select_n | solution.py:29
  66.0 1.1 slice_select_fusion
  67.2 0.9 collective-permute-start.4
  68.0 1.0 slice.54
  69.0 1.0 broadcast_in_dim.28
  70.0 2.2 %scatter_fusion.2 = f32[16,16,896]{2,1,0:T(8,128)} fusion(f32[16,16,896]{2,1,0:T(8,128)} %broadcast_in_dim.28, s32[4]{0:T(128)S(1)} %fusion.12, f32[4,16,896]{2,1,0:T(8,128)S(1)} %slice.54), kind=kCustom, calls=%fused_computation.3 | custom fusion | bytes 688144 | tf_op jit(solution)/shard_map/scatter | solution.py:17
  72.2 4.4 %all-to-all-start.2 = ((f32[8,2,16,896]{3,2,1,0:T(8,128)}), f32[8,2,16,896]{3,2,1,0:T(8,128)}, u32[]{:S(2)}, u32[]{:S(2)}) async-start(f32[8,2,16,896]{3,2,1,0:T(8,128)} %bitcast.15), calls=%async_computation.2 | async-start | bytes 1835008 | tf_op jit(solution)/shard_map/all_to_all | solution.py:131
  76.6 0.0 collective-permute-done.2
  76.6 1.4 maximum_select_fusion.2
  78.0 1.3 copy.20
  79.3 2.4 %fusion.6.s_ref = f32[512,512]{1,0:T(8,128)} fusion(f32[512,512]{1,0:T(8,128)} %copy.20, f32[512,512]{0,1:T(8,128)S(1)} %maximum_select_fusion.2), kind=kLoop, calls=%fused_computation.15 | loop fusion | flops 524288 | bytes 3145728 | tf_op jit(solution)/shard_map/mul | solution.py:138
  81.8 63.1 %shard_map.68 = (f32[512,512]{1,0:T(8,128)}, f32[512,512]{1,0:T(8,128)}) custom-call(f32[512,512]{1,0:T(8,128)} %fusion.6.s_ref), custom_call_target="tpu_custom_call" | custom-call | tf_op jit(solution)/shard_map/pallas_call | solution.py:104
  144.9 1.6 copy.22
  146.5 0.0 collective-permute-done.4
  146.5 2.4 %broadcast_select_fusion.2 = f32[448,512]{1,0:T(8,128)} fusion(f32[448,512]{1,0:T(8,128)} %collective-permute-done.4, pred[]{:T(512)S(6)} %eq.38, f32[896,512]{1,0:T(8,128)S(1)} %broadcast_select_fusion, pred[]{:T(512)S(6)} %eq.37), kind=kLoop, calls=%fused_computation.22 | loop fusion | flops 458752 | bytes 3670018 | tf_op jit(solution)/shard_map/jit(_where)/select_n | solution.py:36
  148.9 0.7 collective-permute-start.5
  149.6 9.8 %fusion.14 = f32[4096,512]{1,0:T(8,128)S(1)} fusion(f32[4096,512]{1,0:T(8,128)} %scatter_fusion.1, f32[512,512]{1,0:T(8,128)} %get-tuple-element.4), kind=kOutput, calls=%fused_computation.36 | convolution fusion | flops 6442450944 | bytes 17825792 | tf_op jit(solution)/shard_map/dot_general | solution.py:140
  159.4 0.0 copy-start.2
  159.4 3.4 %copy-done.2 = f32[4096,512]{1,0:T(8,128)} copy-done((f32[4096,512]{1,0:T(8,128)}, f32[4096,512]{1,0:T(8,128)S(1)}, u32[]{:S(2)}) %copy-start.2) | copy-done | bytes 8388632
  162.8 1.0 slice.49
  163.8 1.6 copy.25
  165.4 1.2 select_bitcast_fusion
  166.6 1.6 copy.23
  168.1 0.0 collective-permute-done.5
  168.1 4.0 %fusion = f32[896,512]{1,0:T(8,128)S(1)} fusion(f32[512,512]{1,0:T(8,128)} %get-tuple-element.4, f32[448,512]{1,0:T(8,128)} %collective-permute-done.5, f32[448,512]{1,0:T(8,128)} %broadcast_select_fusion.2, pred[]{:T(512)S(6)} %eq.37), kind=kOutput, calls=%fused_computation.7 | convolution fusion | flops 1410662400 | bytes 4718593 | tf_op jit(solution)/shard_map/dot_general | solution.py:141
  172.1 20.5 %slice_subtract_fusion = f32[4096,896]{1,0:T(8,128)} fusion(f32[4096,1408]{1,0:T(8,128)} %bitcast.45, f32[4096,512]{1,0:T(8,128)} %copy-done.2, f32[896,512]{1,0:T(8,128)S(1)} %fusion), kind=kOutput, calls=%fused_computation.5 | convolution fusion | flops 11277959168 | bytes 39583744 | tf_op jit(solution)/shard_map/dot_general | solution.py:142
  192.6 0.0 all-to-all-done.2
  192.6 0.0 copy-start.1
  192.6 13.9 %scatter_fusion.3 = f32[4096,896]{1,0:T(8,128)} fusion(f32[4096,896]{1,0:T(8,128)} %slice_subtract_fusion, s32[256]{0:T(256)S(1)} %bitcast.50, f32[256,896]{1,0:T(8,128)} %bitcast.16), kind=kCustom, calls=%fused_computation.4 | custom fusion | flops 229376 | bytes 2753536 | tf_op jit(solution)/shard_map/scatter-add | solution.py:143
  206.4 1.0 constant_dynamic-update-slice_fusion
  207.5 0.0 copy-done.1
  (1 shorter events, 0.0 us)
Async XLA Ops:
  0.6 1.6 copy-start
  3.4 13.8 %all-to-all-start = ((s32[8,2,16]{2,1,0:T(2,128)}), s32[8,2,16]{2,1,0:T(2,128)S(1)}, u32[]{:S(2)}, u32[]{:S(2)}) async-start(s32[8,2,16]{2,1,0:T(2,128)} %bitcast.6), calls=%async_computation | async-start | bytes 16384 | tf_op jit(solution)/shard_map/all_to_all | solution.py:127
  17.2 17.2 %all-to-all-start.1 = ((f32[8,2,16,512]{3,2,1,0:T(8,128)}), f32[8,2,16,512]{3,2,1,0:T(8,128)S(1)}, u32[]{:S(2)}, u32[]{:S(2)}) async-start(f32[8,2,16,512]{3,2,1,0:T(8,128)} %bitcast.9), calls=%async_computation.1 | async-start | bytes 1048576 | tf_op jit(solution)/shard_map/all_to_all | solution.py:126
  45.1 4.1 %collective-permute-start = (f32[512,512]{0,1:T(8,128)S(1)}, f32[512,512]{0,1:T(8,128)S(1)}, u32[]{:S(2)}, u32[]{:S(2)}) collective-permute-start(f32[512,512]{0,1:T(8,128)S(1)} %copy.24), channel_id=1, source_target_pairs={{0,1},{1,0},{2,3},{3,2},{4,5},{5,4},{6,7},{7,6},{8,9},{9,8},{10,11... | collective-permute-start | bytes 3145736 | tf_op jit(solution)/shard_map/ppermute | solution.py:28
  48.0 15.5 %collective-permute-start.3 = (f32[896,512]{1,0:T(8,128)}, f32[896,512]{1,0:T(8,128)}, u32[]{:S(2)}, u32[]{:S(2)}) collective-permute-start(f32[896,512]{1,0:T(8,128)} %slice.51), channel_id=1, source_target_pairs={{0,1},{1,0},{2,3},{3,2},{4,5},{5,4},{6,7},{7,6},{8,9},{9,8},{10,11... | collective-permute-start | bytes 5505032 | tf_op jit(solution)/shard_map/ppermute | solution.py:28
  49.5 13.9 %collective-permute-start.1 = (f32[256,512]{0,1:T(8,128)S(1)}, f32[256,512]{0,1:T(8,128)S(1)}, u32[]{:S(2)}, u32[]{:S(2)}) collective-permute-start(f32[256,512]{0,1:T(8,128)S(1)} %slice_select_fusion.1), channel_id=1, source_target_pairs={{0,2},{1,3},{2,0},{3,1},{4,6},{5,7},{6,4},{7,5},{8,10},{9,11},{10,... | collective-permute-start | bytes 1572872 | tf_op jit(solution)/shard_map/ppermute | solution.py:35
  63.5 13.1 %collective-permute-start.2 = (f32[256,512]{0,1:T(8,128)S(1)}, f32[256,512]{0,1:T(8,128)}, u32[]{:S(2)}, u32[]{:S(2)}) collective-permute-start(f32[256,512]{0,1:T(8,128)S(1)} %broadcast_select_fusion.3), channel_id=1, source_target_pairs={{0,1},{1,0},{2,3},{3,2},{4,5},{5,4},{6,7},{7,6},{8,9},{9,8},{10,11... | collective-permute-start | bytes 1572872 | tf_op jit(solution)/shard_map/ppermute | solution.py:38
  67.2 79.3 %collective-permute-start.4 = (f32[448,512]{1,0:T(8,128)}, f32[448,512]{1,0:T(8,128)}, u32[]{:S(2)}, u32[]{:S(2)}) collective-permute-start(f32[448,512]{1,0:T(8,128)} %slice_select_fusion), channel_id=1, source_target_pairs={{0,2},{1,3},{2,0},{3,1},{4,6},{5,7},{6,4},{7,5},{8,10},{9,11},{10,... | collective-permute-start | bytes 2752520 | tf_op jit(solution)/shard_map/ppermute | solution.py:35
  72.2 120.4 %all-to-all-start.2 = ((f32[8,2,16,896]{3,2,1,0:T(8,128)}), f32[8,2,16,896]{3,2,1,0:T(8,128)}, u32[]{:S(2)}, u32[]{:S(2)}) async-start(f32[8,2,16,896]{3,2,1,0:T(8,128)} %bitcast.15), calls=%async_computation.2 | async-start | bytes 1835008 | tf_op jit(solution)/shard_map/all_to_all | solution.py:131
  148.9 19.2 %collective-permute-start.5 = (f32[448,512]{1,0:T(8,128)}, f32[448,512]{1,0:T(8,128)}, u32[]{:S(2)}, u32[]{:S(2)}) collective-permute-start(f32[448,512]{1,0:T(8,128)} %broadcast_select_fusion.2), channel_id=1, source_target_pairs={{0,1},{1,0},{2,3},{3,2},{4,5},{5,4},{6,7},{7,6},{8,9},{9,8},{10,11... | collective-permute-start | bytes 2752520 | tf_op jit(solution)/shard_map/ppermute | solution.py:38
  159.4 3.4 %copy-start.2 = (f32[4096,512]{1,0:T(8,128)}, f32[4096,512]{1,0:T(8,128)S(1)}, u32[]{:S(2)}) copy-start(f32[4096,512]{1,0:T(8,128)S(1)} %fusion.14) | copy-start | bytes 25165828
  192.6 14.9 %copy-start.1 = (s32[1,1,4,16]{3,2,1,0:T(4,128)S(1)}, s32[1,1,4,16]{3,2,1,0:T(4,128)}, u32[]{:S(2)}) copy-start(s32[1,1,4,16]{3,2,1,0:T(4,128)} %param.7) | copy-start | bytes 772

commit v5 on v4

--- a/solution.py
+++ b/solution.py
@@ -133,8 +133,12 @@
     owner_index = panel_owner[0]
     is_owner = lax.axis_index("grp") == owner_index
 
-    pivot_block = broadcast_from(panel_part[:PB], owner_index, "grp")
-    window_rows = broadcast_from(panel_part[PB:PB + win_cols], owner_index, "grp")
+    top_count = PB + win_cols
+    top_hits = (jnp.arange(top_count, dtype=jnp.int32)[:, None] == flat_rows[None, :]).astype(jnp.float32)
+    top_front = lax.optimization_barrier(front_block[0, :top_count, :PB])
+    top_rows = top_front + jnp.dot(top_hits, got_panel.reshape(-1, PB), precision=EXACT)
+    pivot_block = broadcast_from(top_rows[:PB], owner_index, "grp")
+    window_rows = broadcast_from(top_rows[PB:], owner_index, "grp")
     symmetric = 0.5 * (pivot_block + pivot_block.T)
     pivot_factor, factor_inverse = factor_and_inverse(symmetric)
     solved = jnp.dot(panel_part, factor_inverse.T, precision=FAST)

time: 209 us -> 230 us (1.10)
  local copies, waits for them, and re-layouts: 33 us -> 44.1 us
  matrix products: 34.2 us -> 38.9 us
  waiting for transfers between devices: 20.9 us -> 25.1 us
    ppermute x0 -> x2, local copies, waits for them, and re-layouts: none -> 4.99 us  [the longest x1 2.5 us: broadcast_from(): got = lax.ppermute(half, axis, pairs(size, bit))]
    unnamed x8 -> x20, local copies, waits for them, and re-layouts: 5.29 us -> 9.14 us
    all_to_all x1, waiting for transfers between devices: 5.72 us -> 9.33 us  [local(): lax.all_to_all(send_panel, 'front', split_axis=0, concat_axis=0, tiled=True)]
    dot_general x0 -> x1, matrix products: none -> 3.38 us  [local(): jnp.dot(top_hits, got_panel.reshape(-1, PB), precision=EXACT)]
    select_n x0 -> x2, local copies, waits for them, and re-layouts: none -> 2.53 us  [the longest x1 1.27 us: broadcast_from(): half = jnp.where(core == 0, x[:half_rows], x[half_rows:])]
  transfers between devices with their start and end apart: 9 -> 9, of which waited for: 3 -> 4; matrix products, arithmetic and copies ran while one was open for 34% -> 40% of each run, Pallas kernels for 30% -> 28%
where the time goes in v5:
time: 230 us; the launch traced here: 229 us
  Pallas kernels  63.3 us (28%)
  local copies, waits for them, and re-layouts  44.1 us (19%)
  matrix products  38.9 us (17%)
  other arithmetic  36.9 us (16%)
  waiting for transfers between devices  25.1 us (11%)
  starting transfers between devices  19.2 us (8%)
    pallas_call x1, Pallas kernels, factor_and_inverse(): pl.pallas_call(_factor_kernel, out_shape=(jax.ShapeDtypeStruct((n, n), jn...  63.3 us
    dot_general x1, matrix products, local(): schur_part = local_rows[:, PB:] - jnp.dot(solved, window.T, precision=FAST)  20.2 us
    scatter-add x1, other arithmetic, local(): schur_part.at[flat_rows].add(trailing_rows.reshape(-1, win_cols))  13.9 us
    ppermute x2, waiting for transfers between devices, broadcast_from(): got = lax.ppermute(half, axis, pairs(size, bit))  12.5 us
    dot_general x1, matrix products, local(): solved = jnp.dot(panel_part, factor_inverse.T, precision=FAST)  10 us
    all_to_all x1, waiting for transfers between devices, local(): lax.all_to_all(send_panel, 'front', split_axis=0, concat_axis=0, tiled=True)  9.33 us
    unnamed x20, local copies, waits for them, and re-layouts  9.14 us
    scatter-add x1, other arithmetic, local(): panel_part = local_rows[:, :PB].at[flat_rows].add(got_panel.reshape(-1, PB))  8.98 us
  transfers between devices with their start and end apart: 9, of which 4 were waited for; matrix products, arithmetic and copies ran while one was open for 40% of the time, Pallas kernels for 28%

profile of v5, /device:TPU:0, one launch (start us, length us, event | category | flops | bytes accessed | tf_op | source)
XLA Modules:
  0.0 228.8 jit_solution(1404259922505081236)
XLA Ops:
  0.6 0.0 copy-start
  0.6 0.9 convert_reduce_fusion
  1.6 0.7 fusion.13
  2.2 1.2 scatter_custom_fusion
  3.4 7.3 %all-to-all-start = ((s32[8,2,16]{2,1,0:T(2,128)}), s32[8,2,16]{2,1,0:T(2,128)S(1)}, u32[]{:S(2)}, u32[]{:S(2)}) async-start(s32[8,2,16]{2,1,0:T(2,128)} %bitcast.6), calls=%async_computation | async-start | bytes 16384 | tf_op jit(solution)/shard_map/all_to_all | solution.py:127
  10.6 0.9 slice.49
  11.6 0.9 broadcast_in_dim.26
  12.4 2.0 scatter_fusion
  14.4 2.7 %all-to-all-done = s32[8,2,16]{2,1,0:T(2,128)S(1)} async-done(((s32[8,2,16]{2,1,0:T(2,128)}), s32[8,2,16]{2,1,0:T(2,128)S(1)}, u32[]{:S(2)}, u32[]{:S(2)}) %all-to-all-start) | async-done | bytes 1056 | tf_op jit(solution)/shard_map/all_to_all | solution.py:127
  17.2 3.5 %all-to-all-start.1 = ((f32[8,2,16,512]{3,2,1,0:T(8,128)}), f32[8,2,16,512]{3,2,1,0:T(8,128)S(1)}, u32[]{:S(2)}, u32[]{:S(2)}) async-start(f32[8,2,16,512]{3,2,1,0:T(8,128)} %bitcast.9), calls=%async_computation.1 | async-start | bytes 1048576 | tf_op jit(solution)/shard_map/all_to_all | solution.py:126
  20.7 2.1 slice.38
  22.7 2.2 copy.36
  25.0 0.1 eq.56
  25.1 9.3 %all-to-all-done.1 = f32[8,2,16,512]{3,2,1,0:T(8,128)S(1)} async-done(((f32[8,2,16,512]{3,2,1,0:T(8,128)}), f32[8,2,16,512]{3,2,1,0:T(8,128)S(1)}, u32[]{:S(2)}, u32[]{:S(2)}) %all-to-all-start.1) | async-done | bytes 524320 | tf_op jit(solution)/shard_map/all_to_all | solution.py:126
  34.4 3.4 %convolution_add_fusion = f32[1408,512]{0,1:T(8,128)S(1)} fusion(f32[1408,512]{0,1:T(8,128)} %bitcast.48, f32[256,512]{1,0:T(8,128)S(1)} %bitcast.49, s32[256]{0:T(256)S(1)} %eq.56), kind=kOutput, calls=%fused_computation.6 | convolution fusion | flops 2215673856 | bytes 6292480 | tf_op jit(solution)/shard_map/dot_general | solution.py:139
  37.8 1.1 slice.50
  38.9 0.0 collective-permute-start
  38.9 1.3 slice.55
  40.2 0.5 collective-permute-start.3
  41.4 0.5 collective-permute-done
  41.9 1.4 broadcast_select_fusion.2
  43.3 0.0 copy-start.5
  43.3 1.0 copy-done.5
  44.3 0.9 slice_select_fusion.1
  45.2 1.5 collective-permute-start.1
  46.7 12.5 %collective-permute-done.1 = f32[256,512]{0,1:T(8,128)} collective-permute-done((f32[256,512]{0,1:T(8,128)}, f32[256,512]{0,1:T(8,128)}, u32[]{:S(2)}, u32[]{:S(2)}) %collective-permute-start.1) | collective-permute-done | bytes 524320 | tf_op jit(solution)/shard_map/ppermute | solution.py:35
  59.2 2.1 broadcast_select_fusion.3
  61.3 0.0 collective-permute-start.2
  61.3 0.0 collective-permute-done.3
  61.3 1.8 broadcast_select_fusion
  63.1 1.2 copy-done.3
  64.4 0.3 slice_select_fusion
  64.7 1.3 copy.30
  66.0 1.9 collective-permute-start.4
  67.9 1.0 broadcast_in_dim.29
  68.9 2.2 scatter_fusion.2
  71.1 4.2 %all-to-all-start.2 = ((f32[8,2,16,896]{3,2,1,0:T(8,128)}), f32[8,2,16,896]{3,2,1,0:T(8,128)}, u32[]{:S(2)}, u32[]{:S(2)}) async-start(f32[8,2,16,896]{3,2,1,0:T(8,128)} %bitcast.16), calls=%async_computation.2 | async-start | bytes 1835008 | tf_op jit(solution)/shard_map/all_to_all | solution.py:131
  75.3 7.9 %slice.48 = f32[4096,512]{1,0:T(8,128)} slice(f32[4096,1408]{1,0:T(8,128)} %bitcast.46), slice={[0:4096], [0:512]} | slice | bytes 16777216 | tf_op jit(solution)/shard_map/slice | solution.py:129
  83.2 0.1 reshape.85
  83.3 9.0 %scatter_fusion.1 = f32[4096,512]{1,0:T(8,128)} fusion(f32[4096,512]{1,0:T(8,128)} %slice.48, s32[256]{0:T(256)S(1)} %bitcast.53, f32[256,512]{1,0:T(8,128)S(1)} %bitcast.50), kind=kCustom, calls=%fused_computation.2 | custom fusion | flops 131072 | bytes 1573888 | tf_op jit(solution)/shard_map/scatter-add | solution.py:129
  92.3 0.0 collective-permute-done.2
  92.3 1.7 maximum_select_fusion.2
  94.1 0.3 copy.26
  94.4 1.3 fusion.6.s_ref
  95.6 63.3 %shard_map.68 = (f32[512,512]{1,0:T(8,128)}, f32[512,512]{1,0:T(8,128)}) custom-call(f32[512,512]{1,0:T(8,128)} %fusion.6.s_ref), custom_call_target="tpu_custom_call" | custom-call | tf_op jit(solution)/shard_map/pallas_call | solution.py:104
  158.9 2.6 %copy.28 = f32[512,512]{0,1:T(8,128)} copy(f32[512,512]{1,0:T(8,128)} %get-tuple-element.5) | data formatting | bytes 2097152 | tf_op jit(solution)/shard_map/pallas_call | solution.py:104
  161.5 2.5 %copy.31 = f32[448,512]{0,1:T(8,128)} copy(f32[448,512]{1,0:T(8,128)} %collective-permute-done.4) | data formatting | bytes 1835008 | tf_op jit(solution)/shard_map/ppermute | solution.py:35
  164.0 0.4 broadcast_select_fusion.1
  164.4 1.3 copy.32
  165.7 0.3 collective-permute-start.5
  165.9 10.0 %fusion.15 = f32[4096,512]{1,0:T(8,128)S(1)} fusion(f32[4096,512]{1,0:T(8,128)} %scatter_fusion.1, f32[512,512]{1,0:T(8,128)} %get-tuple-element.4), kind=kOutput, calls=%fused_computation.39 | convolution fusion | flops 6442450944 | bytes 17825792 | tf_op jit(solution)/shard_map/dot_general | solution.py:144
  175.9 0.0 copy-start.2
  175.9 3.4 %copy-done.2 = f32[4096,512]{1,0:T(8,128)} copy-done((f32[4096,512]{1,0:T(8,128)}, f32[4096,512]{1,0:T(8,128)S(1)}, u32[]{:S(2)}) %copy-start.2) | copy-done | bytes 8388632
  179.3 0.1 slice.53
  179.4 1.3 copy.37
  180.7 2.5 %select_bitcast_fusion = f32[1,512,512]{1,2,0:T(8,128)} fusion(f32[512,512]{0,1:T(8,128)} %copy.28, f32[512,512]{0,1:T(8,128)} %copy.37, pred[]{:T(512)S(6)} %eq.54), kind=kLoop, calls=%fused_computation.19 | loop fusion | flops 262144 | bytes 3145729 | tf_op jit(solution)/shard_map/broadcast_in_dim | solution.py:150
  183.2 2.6 %copy.29 = f32[1,512,512]{2,1,0:T(8,128)} copy(f32[1,512,512]{1,2,0:T(8,128)} %select_bitcast_fusion) | data formatting | bytes 2097152 | tf_op jit(solution)/shard_map/broadcast_in_dim | solution.py:150
  185.8 0.0 collective-permute-done.5
  185.8 2.5 %copy.33 = f32[448,512]{0,1:T(8,128)} copy(f32[448,512]{1,0:T(8,128)} %collective-permute-done.5) | data formatting | bytes 1835008 | tf_op jit(solution)/shard_map/ppermute | solution.py:38
  188.3 5.3 %fusion = f32[896,512]{1,0:T(8,128)S(1)} fusion(f32[512,512]{1,0:T(8,128)S(1)} %copy-done.6, f32[448,512]{0,1:T(8,128)} %copy.33, f32[448,512]{0,1:T(8,128)S(1)} %broadcast_select_fusion.1, pred[]{:T(512)S(6)} %eq.52), kind=kOutput, calls=%fused_computation.8 | convolution fusion | flops 1410662400 | bytes 4718593 | tf_op jit(solution)/shard_map/dot_general | solution.py:145
  193.6 20.2 %slice_subtract_fusion = f32[4096,896]{1,0:T(8,128)} fusion(f32[4096,1408]{1,0:T(8,128)} %bitcast.47, f32[4096,512]{1,0:T(8,128)} %copy-done.2, f32[896,512]{1,0:T(8,128)S(1)} %fusion), kind=kOutput, calls=%fused_computation.5 | convolution fusion | flops 11277959168 | bytes 39583744 | tf_op jit(solution)/shard_map/dot_general | solution.py:146
  213.8 0.0 all-to-all-done.2
  213.8 13.9 %scatter_fusion.3 = f32[4096,896]{1,0:T(8,128)} fusion(f32[4096,896]{1,0:T(8,128)} %slice_subtract_fusion, s32[256]{0:T(256)S(1)} %bitcast.54, f32[256,896]{1,0:T(8,128)} %bitcast.17), kind=kCustom, calls=%fused_computation.4 | custom fusion | flops 229376 | bytes 2753536 | tf_op jit(solution)/shard_map/scatter-add | solution.py:147
  227.7 1.0 constant_dynamic-update-slice_fusion
  (15 shorter events, 0.0 us)
Async XLA Ops:
  0.6 1.6 copy-start
  3.4 13.8 %all-to-all-start = ((s32[8,2,16]{2,1,0:T(2,128)}), s32[8,2,16]{2,1,0:T(2,128)S(1)}, u32[]{:S(2)}, u32[]{:S(2)}) async-start(s32[8,2,16]{2,1,0:T(2,128)} %bitcast.6), calls=%async_computation | async-start | bytes 16384 | tf_op jit(solution)/shard_map/all_to_all | solution.py:127
  17.2 17.2 %all-to-all-start.1 = ((f32[8,2,16,512]{3,2,1,0:T(8,128)}), f32[8,2,16,512]{3,2,1,0:T(8,128)S(1)}, u32[]{:S(2)}, u32[]{:S(2)}) async-start(f32[8,2,16,512]{3,2,1,0:T(8,128)} %bitcast.9), calls=%async_computation.1 | async-start | bytes 1048576 | tf_op jit(solution)/shard_map/all_to_all | solution.py:126
  38.9 3.0 %collective-permute-start = (f32[512,512]{0,1:T(8,128)}, f32[512,512]{0,1:T(8,128)}, u32[]{:S(2)}, u32[]{:S(2)}) collective-permute-start(f32[512,512]{0,1:T(8,128)} %slice.50), channel_id=1, source_target_pairs={{0,1},{1,0},{2,3},{3,2},{4,5},{5,4},{6,7},{7,6},{8,9},{9,8},{10,11... | collective-permute-start | bytes 3145736 | tf_op jit(solution)/shard_map/ppermute | solution.py:28
  40.2 21.1 %collective-permute-start.3 = (f32[896,512]{0,1:T(8,128)}, f32[896,512]{0,1:T(8,128)}, u32[]{:S(2)}, u32[]{:S(2)}) collective-permute-start(f32[896,512]{0,1:T(8,128)} %slice.55), channel_id=1, source_target_pairs={{0,1},{1,0},{2,3},{3,2},{4,5},{5,4},{6,7},{7,6},{8,9},{9,8},{10,11... | collective-permute-start | bytes 5505032 | tf_op jit(solution)/shard_map/ppermute | solution.py:28
  43.3 1.0 copy-start.5
  45.2 14.1 %collective-permute-start.1 = (f32[256,512]{0,1:T(8,128)}, f32[256,512]{0,1:T(8,128)}, u32[]{:S(2)}, u32[]{:S(2)}) collective-permute-start(f32[256,512]{0,1:T(8,128)} %slice_select_fusion.1), channel_id=1, source_target_pairs={{0,2},{1,3},{2,0},{3,1},{4,6},{5,7},{6,4},{7,5},{8,10},{9,11},{10,... | collective-permute-start | bytes 1572872 | tf_op jit(solution)/shard_map/ppermute | solution.py:35
  61.3 31.0 %collective-permute-start.2 = (f32[256,512]{0,1:T(8,128)}, f32[256,512]{0,1:T(8,128)}, u32[]{:S(2)}, u32[]{:S(2)}) collective-permute-start(f32[256,512]{0,1:T(8,128)} %broadcast_select_fusion.3), channel_id=1, source_target_pairs={{0,1},{1,0},{2,3},{3,2},{4,5},{5,4},{6,7},{7,6},{8,9},{9,8},{10,11... | collective-permute-start | bytes 1572872 | tf_op jit(solution)/shard_map/ppermute | solution.py:38
  63.1 1.2 copy-start.3
  64.4 3.5 %copy-start.8 = (f32[1,1,4,16,1408]{4,3,2,1,0:T(8,128)S(1)}, f32[1,1,4,16,1408]{4,3,2,1,0:T(8,128)}, u32[]{:S(2)}) copy-start(f32[1,1,4,16,1408]{4,3,2,1,0:T(8,128)} %param.6) | copy-start | bytes 1081348
  66.0 95.5 %collective-permute-start.4 = (f32[448,512]{1,0:T(8,128)}, f32[448,512]{1,0:T(8,128)}, u32[]{:S(2)}, u32[]{:S(2)}) collective-permute-start(f32[448,512]{1,0:T(8,128)} %copy.30), channel_id=1, source_target_pairs={{0,2},{1,3},{2,0},{3,1},{4,6},{5,7},{6,4},{7,5},{8,10},{9,11},{10,... | collective-permute-start | bytes 2752520 | tf_op jit(solution)/shard_map/ppermute | solution.py:35
  71.1 142.7 %all-to-all-start.2 = ((f32[8,2,16,896]{3,2,1,0:T(8,128)}), f32[8,2,16,896]{3,2,1,0:T(8,128)}, u32[]{:S(2)}, u32[]{:S(2)}) async-start(f32[8,2,16,896]{3,2,1,0:T(8,128)} %bitcast.16), calls=%async_computation.2 | async-start | bytes 1835008 | tf_op jit(solution)/shard_map/all_to_all | solution.py:131
  95.6 68.4 %copy-start.4 = (f32[896,512]{0,1:T(8,128)S(1)}, f32[896,512]{0,1:T(8,128)}, u32[]{:S(2)}) copy-start(f32[896,512]{0,1:T(8,128)} %copy-done.3) | copy-start | bytes 5505028
  165.7 20.1 %collective-permute-start.5 = (f32[448,512]{1,0:T(8,128)}, f32[448,512]{1,0:T(8,128)}, u32[]{:S(2)}, u32[]{:S(2)}) collective-permute-start(f32[448,512]{1,0:T(8,128)} %copy.32), channel_id=1, source_target_pairs={{0,1},{1,0},{2,3},{3,2},{4,5},{5,4},{6,7},{7,6},{8,9},{9,8},{10,11... | collective-permute-start | bytes 2752520 | tf_op jit(solution)/shard_map/ppermute | solution.py:38
  175.9 3.4 %copy-start.2 = (f32[4096,512]{1,0:T(8,128)}, f32[4096,512]{1,0:T(8,128)S(1)}, u32[]{:S(2)}) copy-start(f32[4096,512]{1,0:T(8,128)S(1)} %fusion.15) | copy-start | bytes 25165828
  180.7 7.6 %copy-start.6 = (f32[512,512]{1,0:T(8,128)S(1)}, f32[512,512]{1,0:T(8,128)}, u32[]{:S(2)}) copy-start(f32[512,512]{1,0:T(8,128)} %get-tuple-element.4) | copy-start | bytes 3145732
  213.8 14.0 %copy-start.7 = (f32[1,512,512]{2,1,0:T(8,128)S(1)}, f32[1,512,512]{2,1,0:T(8,128)}, u32[]{:S(2)}) copy-start(f32[1,512,512]{2,1,0:T(8,128)} %copy.29) | copy-start | bytes 3145732
  213.8 15.0 %copy-start.1 = (s32[1,1,4,16]{3,2,1,0:T(4,128)S(1)}, s32[1,1,4,16]{3,2,1,0:T(4,128)}, u32[]{:S(2)}) copy-start(s32[1,1,4,16]{3,2,1,0:T(4,128)} %param.7) | copy-start | bytes 772

commit v6 on v4

--- a/solution.py
+++ b/solution.py
@@ -63,19 +63,32 @@
     sub1 = lax.broadcasted_iota(jnp.int32, (BLK, 1), 0)
     eye = jnp.where(sub == lane, 1.0, 0.0).astype(jnp.float32)
 
-    def step(j, carry):
-        row = d_ref[pl.ds(j, 1), :]
-        d = jnp.sum(jnp.where(lane1 == j, row, 0.0), axis=1, keepdims=True)
-        s = lax.rsqrt(d)
-        c = jnp.where(lane1 >= j, row * s, 0.0)
+    def step(t, carry):
+        j = 2 * t
+        r0 = d_ref[pl.ds(j, 1), :]
+        r1 = d_ref[pl.ds(j + 1, 1), :]
+        d0 = jnp.sum(jnp.where(lane1 == j, r0, 0.0), axis=1, keepdims=True)
+        e = jnp.sum(jnp.where(lane1 == j, r1, 0.0), axis=1, keepdims=True)
+        d1 = jnp.sum(jnp.where(lane1 == j + 1, r1, 0.0), axis=1, keepdims=True)
+        s0 = lax.rsqrt(d0)
+        l10 = e * s0
+        s1 = lax.rsqrt(d1 - l10 * l10)
+        c0 = jnp.where(lane1 >= j, r0 * s0, 0.0)
+        c1 = jnp.where(lane1 >= j + 1, (r1 - l10 * c0) * s1, 0.0)
         wv = d_ref[...]
-        col = jnp.sum(jnp.where(lane == j, wv, 0.0), axis=1, keepdims=True)
-        ccol = jnp.where(sub1 >= j, col * s, 0.0)
-        d_ref[...] = wv - ccol * c
-        dt_ref[pl.ds(j, 1), :] = c
-        xrow = di_ref[pl.ds(j, 1), :] * s
-        di_ref[...] = di_ref[...] - jnp.where(sub1 > j, ccol, 0.0) * xrow
-        di_ref[pl.ds(j, 1), :] = xrow
+        col0 = jnp.sum(jnp.where(lane == j, wv, 0.0), axis=1, keepdims=True)
+        col1 = jnp.sum(jnp.where(lane == j + 1, wv, 0.0), axis=1, keepdims=True)
+        ccol0 = jnp.where(sub1 >= j, col0 * s0, 0.0)
+        ccol1 = jnp.where(sub1 >= j + 1, (col1 - l10 * ccol0) * s1, 0.0)
+        d_ref[...] = wv - ccol0 * c0 - ccol1 * c1
+        dt_ref[pl.ds(j, 1), :] = c0
+        dt_ref[pl.ds(j + 1, 1), :] = c1
+        x0 = di_ref[pl.ds(j, 1), :] * s0
+        x1 = (di_ref[pl.ds(j + 1, 1), :] - l10 * x0) * s1
+        below = sub1 > j + 1
+        di_ref[...] = di_ref[...] - jnp.where(below, ccol0, 0.0) * x0 - jnp.where(below, ccol1, 0.0) * x1
+        di_ref[pl.ds(j, 1), :] = x0
+        di_ref[pl.ds(j + 1, 1), :] = x1
         return carry
 
     inv_diag = []
@@ -83,7 +96,7 @@
         lo, hi = k * BLK, (k + 1) * BLK
         d_ref[...] = w_ref[lo:hi, lo:hi]
         di_ref[...] = eye
-        lax.fori_loop(0, BLK, step, 0)
+        lax.fori_loop(0, BLK // 2, step, 0)
         lkk = dt_ref[...].T
         ikk = di_ref[...]
         l_ref[lo:hi, lo:hi] = lkk

time: 209 us -> 186 us (0.89)
  Pallas kernels: 63.1 us -> 41.4 us
    pallas_call x1, Pallas kernels: 63.1 us -> 41.4 us  [factor_and_inverse(): pl.pallas_call(_factor_kernel, out_shape=(jax.ShapeDtypeStruct((n, n), jn...]
  transfers between devices with their start and end apart: 9 -> 9, of which waited for: 3 -> 3; matrix products, arithmetic and copies ran while one was open for 34% -> 38% of each run, Pallas kernels for 30% -> 22%
where the time goes in v6:
time: 186 us; the launch traced here: 185 us
  Pallas kernels  41.4 us (22%)
  matrix products  34.2 us (18%)
  other arithmetic  34 us (18%)
  local copies, waits for them, and re-layouts  33 us (18%)
  waiting for transfers between devices  20.8 us (11%)
  starting transfers between devices  19.7 us (11%)
    pallas_call x1, Pallas kernels, factor_and_inverse(): pl.pallas_call(_factor_kernel, out_shape=(jax.ShapeDtypeStruct((n, n), jn...  41.4 us
    dot_general x1, matrix products, local(): schur_part = local_rows[:, PB:] - jnp.dot(solved, window.T, precision=FAST)  20.5 us
    scatter-add x1, other arithmetic, local(): schur_part.at[flat_rows].add(trailing_rows.reshape(-1, win_cols))  13.9 us
    ppermute x2, waiting for transfers between devices, broadcast_from(): got = lax.ppermute(half, axis, pairs(size, bit))  12.3 us
    dot_general x1, matrix products, local(): solved = jnp.dot(panel_part, factor_inverse.T, precision=FAST)  9.77 us
    scatter-add x1, other arithmetic, local(): panel_part = local_rows[:, :PB].at[flat_rows].add(got_panel.reshape(-1, PB))  8.82 us
    slice x1, local copies, waits for them, and re-layouts, local(): panel_part = local_rows[:, :PB].at[flat_rows].add(got_panel.reshape(-1, PB))  7.92 us
    all_to_all x1, starting transfers between devices, local(): lax.all_to_all(send_rows, 'front', split_axis=0, concat_axis=0, tiled=True)  7.25 us
  transfers between devices with their start and end apart: 9, of which 3 were waited for; matrix products, arithmetic and copies ran while one was open for 38% of the time, Pallas kernels for 22%

profile of v6, /device:TPU:0, one launch (start us, length us, event | category | flops | bytes accessed | tf_op | source)
XLA Modules:
  0.0 184.5 jit_solution(10320480799622849565)
XLA Ops:
  0.6 0.0 copy-start
  0.6 0.9 convert_reduce_fusion
  1.6 0.7 fusion.12
  2.2 0.0 copy-done
  2.2 1.2 scatter_custom_fusion
  3.4 7.3 %all-to-all-start = ((s32[8,2,16]{2,1,0:T(2,128)}), s32[8,2,16]{2,1,0:T(2,128)S(1)}, u32[]{:S(2)}, u32[]{:S(2)}) async-start(s32[8,2,16]{2,1,0:T(2,128)} %bitcast.6), calls=%async_computation | async-start | bytes 16384 | tf_op jit(solution)/shard_map/all_to_all | solution.py:140
  10.6 0.9 slice.45
  11.6 0.9 broadcast_in_dim.25
  12.4 2.0 %scatter_fusion = f32[16,16,512]{2,1,0:T(8,128)} fusion(f32[16,16,512]{2,1,0:T(8,128)} %broadcast_in_dim.25, s32[4]{0:T(128)S(1)} %fusion.12, f32[4,16,512]{2,1,0:T(8,128)S(1)} %slice.45), kind=kCustom, calls=%fused_computation.1 | custom fusion | bytes 393232 | tf_op jit(solution)/shard_map/scatter | solution.py:17
  14.4 2.7 %all-to-all-done = s32[8,2,16]{2,1,0:T(2,128)S(1)} async-done(((s32[8,2,16]{2,1,0:T(2,128)}), s32[8,2,16]{2,1,0:T(2,128)S(1)}, u32[]{:S(2)}, u32[]{:S(2)}) %all-to-all-start) | async-done | bytes 1056 | tf_op jit(solution)/shard_map/all_to_all | solution.py:140
  17.2 3.5 %all-to-all-start.1 = ((f32[8,2,16,512]{3,2,1,0:T(8,128)}), f32[8,2,16,512]{3,2,1,0:T(8,128)S(1)}, u32[]{:S(2)}, u32[]{:S(2)}) async-start(f32[8,2,16,512]{3,2,1,0:T(8,128)} %bitcast.9), calls=%async_computation.1 | async-start | bytes 1048576 | tf_op jit(solution)/shard_map/all_to_all | solution.py:139
  20.7 7.9 %slice.44 = f32[4096,512]{1,0:T(8,128)} slice(f32[4096,1408]{1,0:T(8,128)} %bitcast.44), slice={[0:4096], [0:512]} | slice | bytes 16777216 | tf_op jit(solution)/shard_map/slice | solution.py:142
  28.6 0.1 reshape.83
  28.7 5.7 %all-to-all-done.1 = f32[8,2,16,512]{3,2,1,0:T(8,128)S(1)} async-done(((f32[8,2,16,512]{3,2,1,0:T(8,128)}), f32[8,2,16,512]{3,2,1,0:T(8,128)S(1)}, u32[]{:S(2)}, u32[]{:S(2)}) %all-to-all-start.1) | async-done | bytes 524320 | tf_op jit(solution)/shard_map/all_to_all | solution.py:139
  34.4 8.8 %scatter_fusion.1 = f32[4096,512]{1,0:T(8,128)} fusion(f32[4096,512]{1,0:T(8,128)} %slice.44, s32[256]{0:T(256)S(1)} %bitcast.49, f32[256,512]{1,0:T(8,128)S(1)} %bitcast.46), kind=kCustom, calls=%fused_computation.2 | custom fusion | flops 131072 | bytes 1573888 | tf_op jit(solution)/shard_map/scatter-add | solution.py:142
  43.2 1.3 slice.46
  44.5 0.3 copy.24
  44.9 0.1 collective-permute-start
  44.9 2.9 %slice.51 = f32[896,512]{1,0:T(8,128)} slice(f32[4096,512]{1,0:T(8,128)} %scatter_fusion.1), slice={[512:1408], [0:512]} | slice | bytes 3670016 | tf_op jit(solution)/shard_map/slice | solution.py:150
  47.8 0.5 collective-permute-start.3
  49.0 0.0 collective-permute-done
  49.0 0.2 broadcast_select_fusion.1
  49.2 0.1 slice_select_fusion.1
  49.3 1.6 collective-permute-start.1
  50.8 12.3 %collective-permute-done.1 = f32[256,512]{0,1:T(8,128)S(1)} collective-permute-done((f32[256,512]{0,1:T(8,128)S(1)}, f32[256,512]{0,1:T(8,128)S(1)}, u32[]{:S(2)}, u32[]{:S(2)}) %collective-permute-start.1) | collective-permute-done | bytes 524320 | tf_op jit(solution)/shard_map/ppermute | solution.py:35
  63.2 0.1 broadcast_select_fusion.3
  63.3 0.1 collective-permute-start.2
  63.4 0.0 collective-permute-done.3
  63.4 1.9 %broadcast_select_fusion = f32[896,512]{1,0:T(8,128)S(1)} fusion(f32[896,512]{1,0:T(8,128)} %collective-permute-done.3, pred[]{:T(512)S(6)} %eq.39, f32[4096,512]{1,0:T(8,128)} %scatter_fusion.1), kind=kLoop, calls=%fused_computation.18 | loop fusion | flops 458752 | bytes 5505025 | tf_op jit(solution)/shard_map/jit(_where)/select_n | solution.py:29
  65.3 1.1 slice_select_fusion
  66.4 2.1 %collective-permute-start.4 = (f32[448,512]{1,0:T(8,128)}, f32[448,512]{1,0:T(8,128)}, u32[]{:S(2)}, u32[]{:S(2)}) collective-permute-start(f32[448,512]{1,0:T(8,128)} %slice_select_fusion), channel_id=1, source_target_pairs={{0,2},{1,3},{2,0},{3,1},{4,6},{5,7},{6,4},{7,5},{8,10},{9,11},{10,... | collective-permute-start | bytes 2752520 | tf_op jit(solution)/shard_map/ppermute | solution.py:35
  68.5 1.0 slice.54
  69.4 1.0 broadcast_in_dim.28
  70.4 2.1 %scatter_fusion.2 = f32[16,16,896]{2,1,0:T(8,128)} fusion(f32[16,16,896]{2,1,0:T(8,128)} %broadcast_in_dim.28, s32[4]{0:T(128)S(1)} %fusion.12, f32[4,16,896]{2,1,0:T(8,128)S(1)} %slice.54), kind=kCustom, calls=%fused_computation.3 | custom fusion | bytes 688144 | tf_op jit(solution)/shard_map/scatter | solution.py:17
  72.6 4.4 %all-to-all-start.2 = ((f32[8,2,16,896]{3,2,1,0:T(8,128)}), f32[8,2,16,896]{3,2,1,0:T(8,128)}, u32[]{:S(2)}, u32[]{:S(2)}) async-start(f32[8,2,16,896]{3,2,1,0:T(8,128)} %bitcast.15), calls=%async_computation.2 | async-start | bytes 1835008 | tf_op jit(solution)/shard_map/all_to_all | solution.py:144
  77.0 0.0 collective-permute-done.2
  77.0 1.4 maximum_select_fusion.2
  78.4 1.3 copy.20
  79.7 2.4 %fusion.6.s_ref = f32[512,512]{1,0:T(8,128)} fusion(f32[512,512]{1,0:T(8,128)} %copy.20, f32[512,512]{0,1:T(8,128)S(1)} %maximum_select_fusion.2), kind=kLoop, calls=%fused_computation.15 | loop fusion | flops 524288 | bytes 3145728 | tf_op jit(solution)/shard_map/mul | solution.py:151
  82.1 41.4 %shard_map.68 = (f32[512,512]{1,0:T(8,128)}, f32[512,512]{1,0:T(8,128)}) custom-call(f32[512,512]{1,0:T(8,128)} %fusion.6.s_ref), custom_call_target="tpu_custom_call" | custom-call | tf_op jit(solution)/shard_map/pallas_call | solution.py:117
  123.6 1.6 copy.22
  125.1 0.0 collective-permute-done.4
  125.1 1.3 broadcast_select_fusion.2
  126.4 0.2 collective-permute-start.5
  126.6 9.8 %fusion.14 = f32[4096,512]{1,0:T(8,128)S(1)} fusion(f32[4096,512]{1,0:T(8,128)} %scatter_fusion.1, f32[512,512]{1,0:T(8,128)} %get-tuple-element.4), kind=kOutput, calls=%fused_computation.36 | convolution fusion | flops 6442450944 | bytes 17825792 | tf_op jit(solution)/shard_map/dot_general | solution.py:153
  136.4 0.0 copy-start.2
  136.4 3.4 %copy-done.2 = f32[4096,512]{1,0:T(8,128)} copy-done((f32[4096,512]{1,0:T(8,128)}, f32[4096,512]{1,0:T(8,128)S(1)}, u32[]{:S(2)}) %copy-start.2) | copy-done | bytes 8388632
  139.8 1.0 slice.49
  140.9 1.6 copy.25
  142.4 1.2 select_bitcast_fusion
  143.6 1.6 copy.23
  145.2 0.0 collective-permute-done.5
  145.2 4.0 %fusion = f32[896,512]{1,0:T(8,128)S(1)} fusion(f32[512,512]{1,0:T(8,128)} %get-tuple-element.4, f32[448,512]{1,0:T(8,128)} %collective-permute-done.5, f32[448,512]{1,0:T(8,128)} %broadcast_select_fusion.2, pred[]{:T(512)S(6)} %eq.37), kind=kOutput, calls=%fused_computation.7 | convolution fusion | flops 1410662400 | bytes 4718593 | tf_op jit(solution)/shard_map/dot_general | solution.py:154
  149.1 20.5 %slice_subtract_fusion = f32[4096,896]{1,0:T(8,128)} fusion(f32[4096,1408]{1,0:T(8,128)} %bitcast.45, f32[4096,512]{1,0:T(8,128)} %copy-done.2, f32[896,512]{1,0:T(8,128)S(1)} %fusion), kind=kOutput, calls=%fused_computation.5 | convolution fusion | flops 11277959168 | bytes 39583744 | tf_op jit(solution)/shard_map/dot_general | solution.py:155
  169.6 0.0 all-to-all-done.2
  169.6 0.0 copy-start.1
  169.6 13.9 %scatter_fusion.3 = f32[4096,896]{1,0:T(8,128)} fusion(f32[4096,896]{1,0:T(8,128)} %slice_subtract_fusion, s32[256]{0:T(256)S(1)} %bitcast.50, f32[256,896]{1,0:T(8,128)} %bitcast.16), kind=kCustom, calls=%fused_computation.4 | custom fusion | flops 229376 | bytes 2753536 | tf_op jit(solution)/shard_map/scatter-add | solution.py:156
  183.5 1.0 constant_dynamic-update-slice_fusion
  184.5 0.0 copy-done.1
  (1 shorter events, 0.0 us)
Async XLA Ops:
  0.6 1.6 copy-start
  3.4 13.8 %all-to-all-start = ((s32[8,2,16]{2,1,0:T(2,128)}), s32[8,2,16]{2,1,0:T(2,128)S(1)}, u32[]{:S(2)}, u32[]{:S(2)}) async-start(s32[8,2,16]{2,1,0:T(2,128)} %bitcast.6), calls=%async_computation | async-start | bytes 16384 | tf_op jit(solution)/shard_map/all_to_all | solution.py:140
  17.2 17.2 %all-to-all-start.1 = ((f32[8,2,16,512]{3,2,1,0:T(8,128)}), f32[8,2,16,512]{3,2,1,0:T(8,128)S(1)}, u32[]{:S(2)}, u32[]{:S(2)}) async-start(f32[8,2,16,512]{3,2,1,0:T(8,128)} %bitcast.9), calls=%async_computation.1 | async-start | bytes 1048576 | tf_op jit(solution)/shard_map/all_to_all | solution.py:139
  44.9 4.1 %collective-permute-start = (f32[512,512]{0,1:T(8,128)S(1)}, f32[512,512]{0,1:T(8,128)S(1)}, u32[]{:S(2)}, u32[]{:S(2)}) collective-permute-start(f32[512,512]{0,1:T(8,128)S(1)} %copy.24), channel_id=1, source_target_pairs={{0,1},{1,0},{2,3},{3,2},{4,5},{5,4},{6,7},{7,6},{8,9},{9,8},{10,11... | collective-permute-start | bytes 3145736 | tf_op jit(solution)/shard_map/ppermute | solution.py:28
  47.8 15.5 %collective-permute-start.3 = (f32[896,512]{1,0:T(8,128)}, f32[896,512]{1,0:T(8,128)}, u32[]{:S(2)}, u32[]{:S(2)}) collective-permute-start(f32[896,512]{1,0:T(8,128)} %slice.51), channel_id=1, source_target_pairs={{0,1},{1,0},{2,3},{3,2},{4,5},{5,4},{6,7},{7,6},{8,9},{9,8},{10,11... | collective-permute-start | bytes 5505032 | tf_op jit(solution)/shard_map/ppermute | solution.py:28
  49.3 13.9 %collective-permute-start.1 = (f32[256,512]{0,1:T(8,128)S(1)}, f32[256,512]{0,1:T(8,128)S(1)}, u32[]{:S(2)}, u32[]{:S(2)}) collective-permute-start(f32[256,512]{0,1:T(8,128)S(1)} %slice_select_fusion.1), channel_id=1, source_target_pairs={{0,2},{1,3},{2,0},{3,1},{4,6},{5,7},{6,4},{7,5},{8,10},{9,11},{10,... | collective-permute-start | bytes 1572872 | tf_op jit(solution)/shard_map/ppermute | solution.py:35
  63.3 13.7 %collective-permute-start.2 = (f32[256,512]{0,1:T(8,128)S(1)}, f32[256,512]{0,1:T(8,128)}, u32[]{:S(2)}, u32[]{:S(2)}) collective-permute-start(f32[256,512]{0,1:T(8,128)S(1)} %broadcast_select_fusion.3), channel_id=1, source_target_pairs={{0,1},{1,0},{2,3},{3,2},{4,5},{5,4},{6,7},{7,6},{8,9},{9,8},{10,11... | collective-permute-start | bytes 1572872 | tf_op jit(solution)/shard_map/ppermute | solution.py:38
  66.4 58.7 %collective-permute-start.4 = (f32[448,512]{1,0:T(8,128)}, f32[448,512]{1,0:T(8,128)}, u32[]{:S(2)}, u32[]{:S(2)}) collective-permute-start(f32[448,512]{1,0:T(8,128)} %slice_select_fusion), channel_id=1, source_target_pairs={{0,2},{1,3},{2,0},{3,1},{4,6},{5,7},{6,4},{7,5},{8,10},{9,11},{10,... | collective-permute-start | bytes 2752520 | tf_op jit(solution)/shard_map/ppermute | solution.py:35
  72.6 97.0 %all-to-all-start.2 = ((f32[8,2,16,896]{3,2,1,0:T(8,128)}), f32[8,2,16,896]{3,2,1,0:T(8,128)}, u32[]{:S(2)}, u32[]{:S(2)}) async-start(f32[8,2,16,896]{3,2,1,0:T(8,128)} %bitcast.15), calls=%async_computation.2 | async-start | bytes 1835008 | tf_op jit(solution)/shard_map/all_to_all | solution.py:144
  126.4 18.8 %collective-permute-start.5 = (f32[448,512]{1,0:T(8,128)}, f32[448,512]{1,0:T(8,128)}, u32[]{:S(2)}, u32[]{:S(2)}) collective-permute-start(f32[448,512]{1,0:T(8,128)} %broadcast_select_fusion.2), channel_id=1, source_target_pairs={{0,1},{1,0},{2,3},{3,2},{4,5},{5,4},{6,7},{7,6},{8,9},{9,8},{10,11... | collective-permute-start | bytes 2752520 | tf_op jit(solution)/shard_map/ppermute | solution.py:38
  136.4 3.4 %copy-start.2 = (f32[4096,512]{1,0:T(8,128)}, f32[4096,512]{1,0:T(8,128)S(1)}, u32[]{:S(2)}) copy-start(f32[4096,512]{1,0:T(8,128)S(1)} %fusion.14) | copy-start | bytes 25165828
  169.6 14.9 %copy-start.1 = (s32[1,1,4,16]{3,2,1,0:T(4,128)S(1)}, s32[1,1,4,16]{3,2,1,0:T(4,128)}, u32[]{:S(2)}) copy-start(s32[1,1,4,16]{3,2,1,0:T(4,128)} %param.7) | copy-start | bytes 772

commit v7 on v6

--- a/solution.py
+++ b/solution.py
@@ -123,6 +123,68 @@
     )(sym)
 
 
+def _row_add_kernel(idx_ref, lead_ref, base_ref, add_ref, out_ref, buf, sems):
+    count = add_ref.shape[0]
+
+    def fetch(i):
+        return pltpu.make_async_copy(base_ref.at[pl.ds(idx_ref[i], 1)], buf.at[pl.ds(i, 1)], sems.at[i])
+
+    def store(i):
+        return pltpu.make_async_copy(buf.at[pl.ds(i, 1)], out_ref.at[pl.ds(idx_ref[i], 1)], sems.at[i])
+
+    def start_fetch(i, c):
+        fetch(i).start()
+        return c
+
+    def wait_fetch(i, c):
+        fetch(i).wait()
+        return c
+
+    lax.fori_loop(0, count, start_fetch, 0)
+    lax.fori_loop(0, count, wait_fetch, 0)
+
+    def accumulate(i, c):
+        lead = lead_ref[i]
+        buf[pl.ds(lead, 1), :] = buf[pl.ds(lead, 1), :] + add_ref[pl.ds(i, 1), :]
+        return c
+
+    lax.fori_loop(0, count, accumulate, 0)
+
+    def start_store(i, c):
+        @pl.when(lead_ref[i] == i)
+        def _():
+            store(i).start()
+        return c
+
+    def wait_store(i, c):
+        @pl.when(lead_ref[i] == i)
+        def _():
+            store(i).wait()
+        return c
+
+    lax.fori_loop(0, count, start_store, 0)
+    lax.fori_loop(0, count, wait_store, 0)
+
+
+def add_rows(base, rows, values):
+    count, width = values.shape
+    same = rows[:, None] == rows[None, :]
+    lead = jnp.argmax(same, axis=1).astype(jnp.int32)
+    return pl.pallas_call(
+        _row_add_kernel,
+        out_shape=jax.ShapeDtypeStruct(base.shape, base.dtype),
+        in_specs=[
+            pl.BlockSpec(memory_space=pltpu.SMEM),
+            pl.BlockSpec(memory_space=pltpu.SMEM),
+            pl.BlockSpec(memory_space=pl.ANY),
+            pl.BlockSpec(memory_space=pltpu.VMEM),
+        ],
+        out_specs=pl.BlockSpec(memory_space=pl.ANY),
+        scratch_shapes=[pltpu.VMEM((count, width), jnp.float32), pltpu.SemaphoreType.DMA((count,))],
+        input_output_aliases={2: 0},
+    )(rows, lead, base, values)
+
+
 def local(front_block, child_blocks, child_rows, child_dest, panel_owner):
     local_rows = front_block[0]
     front_count = lax.axis_size("front")
@@ -139,7 +201,7 @@
     got_panel = lax.all_to_all(send_panel, "front", split_axis=0, concat_axis=0, tiled=True)
     got_rows = lax.all_to_all(send_rows, "front", split_axis=0, concat_axis=0, tiled=True)
     flat_rows = got_rows.reshape(-1)
-    panel_part = local_rows[:, :PB].at[flat_rows].add(got_panel.reshape(-1, PB))
+    panel_part = add_rows(local_rows[:, :PB], flat_rows, got_panel.reshape(-1, PB))
     send_trail = pack_slots(blocks[:, :, PB:], slot_index, front_count)
     trailing_rows = lax.all_to_all(send_trail, "front", split_axis=0, concat_axis=0, tiled=True)
     win_cols = local_rows.shape[1] - PB
@@ -153,7 +215,7 @@
     solved = jnp.dot(panel_part, factor_inverse.T, precision=FAST)
     window = jnp.dot(window_rows, factor_inverse.T, precision=FAST)
     schur_part = local_rows[:, PB:] - jnp.dot(solved, window.T, precision=FAST)
-    schur_part = schur_part.at[flat_rows].add(trailing_rows.reshape(-1, win_cols))
+    schur_part = add_rows(schur_part, flat_rows, trailing_rows.reshape(-1, win_cols))
     head = jnp.where(is_owner, pivot_factor, solved[:PB])
     panel_rows = lax.dynamic_update_slice(solved, head, (0, 0))
     return (panel_rows[None], schur_part[None])

time: 186 us -> 205 us (1.10)
  the two profiles are of different devices: /device:TPU:0 before, /device:TPU:11 now
where the time goes in v7:
time: 205 us; the launch traced here: 203 us
  Pallas kernels  82.1 us (40%)
  matrix products  34.2 us (17%)
  local copies, waits for them, and re-layouts  33.8 us (16%)
  starting transfers between devices  23.2 us (11%)
  waiting for transfers between devices  14.4 us (7%)
  other arithmetic  13.8 us (7%)
    pallas_call x1, Pallas kernels, factor_and_inverse(): pl.pallas_call(_factor_kernel, out_shape=(jax.ShapeDtypeStruct((n, n), jn...  41.4 us
    pallas_call x2, Pallas kernels, add_rows(): pl.pallas_call(_row_add_kernel, out_shape=jax.ShapeDtypeStruct(base.shape...  40.6 us
    dot_general x1, matrix products, local(): schur_part = local_rows[:, PB:] - jnp.dot(solved, window.T, precision=FAST)  20.5 us
    ppermute x2, waiting for transfers between devices, broadcast_from(): got = lax.ppermute(half, axis, pairs(size, bit))  11.9 us
    dot_general x1, matrix products, local(): solved = jnp.dot(panel_part, factor_inverse.T, precision=FAST)  9.77 us
    slice x1, local copies, waits for them, and re-layouts, local(): local_rows[:, :PB]  7.92 us
    all_to_all x1, starting transfers between devices, local(): lax.all_to_all(send_trail, 'front', split_axis=0, concat_axis=0, tiled=True)  6.37 us
    unnamed x12, local copies, waits for them, and re-layouts  6.08 us
  transfers between devices with their start and end apart: 9, of which 2 were waited for; matrix products, arithmetic and copies ran while one was open for 36% of the time, Pallas kernels for 20%

profile of v7, /device:TPU:11, one launch (start us, length us, event | category | flops | bytes accessed | tf_op | source)
XLA Modules:
  0.0 203.0 jit_solution(95387416166986955)
XLA Ops:
  0.6 0.0 copy-start
  0.6 0.9 convert_reduce_fusion
  1.6 0.7 fusion.12
  2.2 0.0 copy-done
  2.2 1.2 scatter_custom_fusion
  3.4 5.7 %all-to-all-start = ((s32[8,2,16]{2,1,0:T(2,128)}), s32[8,2,16]{2,1,0:T(2,128)S(1)}, u32[]{:S(2)}, u32[]{:S(2)}) async-start(s32[8,2,16]{2,1,0:T(2,128)} %bitcast.5), calls=%async_computation | async-start | bytes 16384 | tf_op jit(solution)/shard_map/all_to_all | solution.py:202
  9.0 0.9 slice.45
  10.0 0.9 broadcast_in_dim.23
  10.8 2.0 scatter_fusion
  12.8 0.0 all-to-all-done
  12.8 5.4 %all-to-all-start.1 = ((f32[8,2,16,512]{3,2,1,0:T(8,128)}), f32[8,2,16,512]{3,2,1,0:T(8,128)S(1)}, u32[]{:S(2)}, u32[]{:S(2)}) async-start(f32[8,2,16,512]{3,2,1,0:T(8,128)} %bitcast.8), calls=%async_computation.1 | async-start | bytes 1048576 | tf_op jit(solution)/shard_map/all_to_all | solution.py:201
  18.3 7.9 %slice.44.base_ref = f32[4096,512]{1,0:T(8,128)} slice(f32[4096,1408]{1,0:T(8,128)} %bitcast.43), slice={[0:4096], [0:512]} | slice | bytes 16777216 | tf_op jit(solution)/shard_map/slice | solution.py:204
  26.2 0.1 reshape.57.idx_ref
  26.3 0.0 copy-start.4
  26.3 0.8 iota_reduce_fusion
  27.1 2.6 %all-to-all-done.1 = f32[8,2,16,512]{3,2,1,0:T(8,128)S(1)} async-done(((f32[8,2,16,512]{3,2,1,0:T(8,128)}), f32[8,2,16,512]{3,2,1,0:T(8,128)S(1)}, u32[]{:S(2)}, u32[]{:S(2)}) %all-to-all-start.1) | async-done | bytes 524320 | tf_op jit(solution)/shard_map/all_to_all | solution.py:201
  29.6 0.0 copy-start.3
  29.6 0.0 copy-done.4
  29.6 0.8 copy-done.3
  30.4 19.7 %shard_map.68 = f32[4096,512]{1,0:T(8,128)} custom-call(s32[256]{0:T(256)} %copy-done.4, s32[256]{0:T(256)} %get-tuple-element.5.lead_ref, f32[4096,512]{1,0:T(8,128)} %slice.44.base_ref, f32[256,512]{1,0:T(8,128)} %bitcast.45), custom_call_target="tpu_custom_call", output_to_operand_aliasing={{}: (2, {})} | custom-call | tf_op jit(solution)/shard_map/pallas_call | solution.py:173
  50.1 1.3 slice.46
  51.4 0.3 copy.19
  51.8 0.8 collective-permute-start
  52.6 2.9 %slice.51 = f32[896,512]{1,0:T(8,128)} slice(f32[4096,512]{1,0:T(8,128)} %shard_map.68), slice={[512:1408], [0:512]} | slice | bytes 3670016 | tf_op jit(solution)/shard_map/slice | solution.py:212
  55.5 0.0 collective-permute-start.3
  56.2 0.0 collective-permute-done
  56.2 0.2 broadcast_select_fusion.1
  56.4 0.1 slice_select_fusion.1
  56.5 2.0 %collective-permute-start.1 = (f32[256,512]{0,1:T(8,128)S(1)}, f32[256,512]{0,1:T(8,128)S(1)}, u32[]{:S(2)}, u32[]{:S(2)}) collective-permute-start(f32[256,512]{0,1:T(8,128)S(1)} %slice_select_fusion.1), channel_id=1, source_target_pairs={{0,2},{1,3},{2,0},{3,1},{4,6},{5,7},{6,4},{7,5},{8,10},{9,11},{10,... | collective-permute-start | bytes 1572872 | tf_op jit(solution)/shard_map/ppermute | solution.py:35
  58.5 11.9 %collective-permute-done.1 = f32[256,512]{0,1:T(8,128)S(1)} collective-permute-done((f32[256,512]{0,1:T(8,128)S(1)}, f32[256,512]{0,1:T(8,128)S(1)}, u32[]{:S(2)}, u32[]{:S(2)}) %collective-permute-start.1) | collective-permute-done | bytes 524320 | tf_op jit(solution)/shard_map/ppermute | solution.py:35
  70.4 0.1 broadcast_select_fusion.3
  70.5 1.1 collective-permute-start.2
  71.5 0.0 collective-permute-done.3
  71.6 2.5 %broadcast_select_fusion = f32[896,512]{1,0:T(8,128)S(1)} fusion(f32[896,512]{1,0:T(8,128)} %collective-permute-done.3, pred[]{:T(512)S(6)} %eq.64, f32[4096,512]{1,0:T(8,128)} %shard_map.68), kind=kLoop, calls=%fused_computation.16 | loop fusion | flops 458752 | bytes 5505025 | tf_op jit(solution)/shard_map/jit(_where)/select_n | solution.py:29
  74.0 1.1 slice_select_fusion
  75.1 0.9 collective-permute-start.4
  76.0 1.0 slice.54
  77.0 1.0 broadcast_in_dim.26
  78.0 2.2 %scatter_fusion.1 = f32[16,16,896]{2,1,0:T(8,128)} fusion(f32[16,16,896]{2,1,0:T(8,128)} %broadcast_in_dim.26, s32[4]{0:T(128)S(1)} %fusion.12, f32[4,16,896]{2,1,0:T(8,128)S(1)} %slice.54), kind=kCustom, calls=%fused_computation.2 | custom fusion | bytes 688144 | tf_op jit(solution)/shard_map/scatter | solution.py:17
  80.2 6.4 %all-to-all-start.2 = ((f32[8,2,16,896]{3,2,1,0:T(8,128)}), f32[8,2,16,896]{3,2,1,0:T(8,128)}, u32[]{:S(2)}, u32[]{:S(2)}) async-start(f32[8,2,16,896]{3,2,1,0:T(8,128)} %bitcast.14), calls=%async_computation.2 | async-start | bytes 1835008 | tf_op jit(solution)/shard_map/all_to_all | solution.py:206
  86.6 0.0 collective-permute-done.2
  86.6 1.4 maximum_select_fusion.2
  88.0 1.3 copy.15
  89.3 2.4 %fusion.6.s_ref = f32[512,512]{1,0:T(8,128)} fusion(f32[512,512]{1,0:T(8,128)} %copy.15, f32[512,512]{0,1:T(8,128)S(1)} %maximum_select_fusion.2), kind=kLoop, calls=%fused_computation.13 | loop fusion | flops 524288 | bytes 3145728 | tf_op jit(solution)/shard_map/mul | solution.py:213
  91.7 41.4 %shard_map.69 = (f32[512,512]{1,0:T(8,128)}, f32[512,512]{1,0:T(8,128)}) custom-call(f32[512,512]{1,0:T(8,128)} %fusion.6.s_ref), custom_call_target="tpu_custom_call" | custom-call | tf_op jit(solution)/shard_map/pallas_call | solution.py:117
  133.1 1.6 copy.17
  134.7 0.0 collective-permute-done.4
  134.7 2.4 %broadcast_select_fusion.2 = f32[448,512]{1,0:T(8,128)} fusion(f32[448,512]{1,0:T(8,128)} %collective-permute-done.4, pred[]{:T(512)S(6)} %eq.33, f32[896,512]{1,0:T(8,128)S(1)} %broadcast_select_fusion, pred[]{:T(512)S(6)} %eq.32), kind=kLoop, calls=%fused_computation.20 | loop fusion | flops 458752 | bytes 3670018 | tf_op jit(solution)/shard_map/jit(_where)/select_n | solution.py:36
  137.1 0.9 collective-permute-start.5
  138.0 9.8 %fusion.14 = f32[4096,512]{1,0:T(8,128)S(1)} fusion(f32[4096,512]{1,0:T(8,128)} %shard_map.68, f32[512,512]{1,0:T(8,128)} %get-tuple-element.6), kind=kOutput, calls=%fused_computation.34 | convolution fusion | flops 6442450944 | bytes 17825792 | tf_op jit(solution)/shard_map/dot_general | solution.py:215
  147.8 0.0 copy-start.2
  147.8 3.4 %copy-done.2 = f32[4096,512]{1,0:T(8,128)} copy-done((f32[4096,512]{1,0:T(8,128)}, f32[4096,512]{1,0:T(8,128)S(1)}, u32[]{:S(2)}) %copy-start.2) | copy-done | bytes 8388632
  151.2 1.0 slice.49
  152.2 1.6 copy.20
  153.8 1.2 select_bitcast_fusion
  155.0 1.6 copy.18
  156.5 0.0 collective-permute-done.5
  156.5 4.0 %fusion = f32[896,512]{1,0:T(8,128)S(1)} fusion(f32[512,512]{1,0:T(8,128)} %get-tuple-element.6, f32[448,512]{1,0:T(8,128)} %collective-permute-done.5, f32[448,512]{1,0:T(8,128)} %broadcast_select_fusion.2, pred[]{:T(512)S(6)} %eq.32), kind=kOutput, calls=%fused_computation.5 | convolution fusion | flops 1410662400 | bytes 4718593 | tf_op jit(solution)/shard_map/dot_general | solution.py:216
  160.5 20.5 %slice_subtract_fusion.base_ref = f32[4096,896]{1,0:T(8,128)} fusion(f32[4096,1408]{1,0:T(8,128)} %bitcast.44, f32[4096,512]{1,0:T(8,128)} %copy-done.2, f32[896,512]{1,0:T(8,128)S(1)} %fusion), kind=kOutput, calls=%fused_computation.3 | convolution fusion | flops 11277959168 | bytes 39583744 | tf_op jit(solution)/shard_map/dot_general | solution.py:217
  181.0 0.0 all-to-all-done.2
  181.0 0.0 copy-start.1
  181.0 20.9 %shard_map.70 = f32[4096,896]{1,0:T(8,128)} custom-call(s32[256]{0:T(256)} %copy-done.4, s32[256]{0:T(256)} %get-tuple-element.5.lead_ref, f32[4096,896]{1,0:T(8,128)} %slice_subtract_fusion.base_ref, f32[256,896]{1,0:T(8,128)} %bitcast.15.add_ref), custom_call_target="tpu_custom_call", output_to_operand_aliasing={{}: (2, {})} | custom-call | tf_op jit(solution)/shard_map/pallas_call | solution.py:173
  201.9 1.0 constant_dynamic-update-slice_fusion
  203.0 0.0 copy-done.1
Async XLA Ops:
  0.6 1.6 copy-start
  3.4 9.4 %all-to-all-start = ((s32[8,2,16]{2,1,0:T(2,128)}), s32[8,2,16]{2,1,0:T(2,128)S(1)}, u32[]{:S(2)}, u32[]{:S(2)}) async-start(s32[8,2,16]{2,1,0:T(2,128)} %bitcast.5), calls=%async_computation | async-start | bytes 16384 | tf_op jit(solution)/shard_map/all_to_all | solution.py:202
  12.8 16.8 %all-to-all-start.1 = ((f32[8,2,16,512]{3,2,1,0:T(8,128)}), f32[8,2,16,512]{3,2,1,0:T(8,128)S(1)}, u32[]{:S(2)}, u32[]{:S(2)}) async-start(f32[8,2,16,512]{3,2,1,0:T(8,128)} %bitcast.8), calls=%async_computation.1 | async-start | bytes 1048576 | tf_op jit(solution)/shard_map/all_to_all | solution.py:201
  26.3 3.4 %copy-start.4 = (s32[256]{0:T(256)}, s32[256]{0:T(256)S(1)}, u32[]{:S(2)}) copy-start(s32[256]{0:T(256)S(1)} %reshape.57.idx_ref) | copy-start | bytes 3076
  29.6 0.8 copy-start.3
  51.8 4.4 %collective-permute-start = (f32[512,512]{0,1:T(8,128)S(1)}, f32[512,512]{0,1:T(8,128)S(1)}, u32[]{:S(2)}, u32[]{:S(2)}) collective-permute-start(f32[512,512]{0,1:T(8,128)S(1)} %copy.19), channel_id=1, source_target_pairs={{0,1},{1,0},{2,3},{3,2},{4,5},{5,4},{6,7},{7,6},{8,9},{9,8},{10,11... | collective-permute-start | bytes 3145736 | tf_op jit(solution)/shard_map/ppermute | solution.py:28
  55.5 16.1 %collective-permute-start.3 = (f32[896,512]{1,0:T(8,128)}, f32[896,512]{1,0:T(8,128)}, u32[]{:S(2)}, u32[]{:S(2)}) collective-permute-start(f32[896,512]{1,0:T(8,128)} %slice.51), channel_id=1, source_target_pairs={{0,1},{1,0},{2,3},{3,2},{4,5},{5,4},{6,7},{7,6},{8,9},{9,8},{10,11... | collective-permute-start | bytes 5505032 | tf_op jit(solution)/shard_map/ppermute | solution.py:28
  56.5 13.9 %collective-permute-start.1 = (f32[256,512]{0,1:T(8,128)S(1)}, f32[256,512]{0,1:T(8,128)S(1)}, u32[]{:S(2)}, u32[]{:S(2)}) collective-permute-start(f32[256,512]{0,1:T(8,128)S(1)} %slice_select_fusion.1), channel_id=1, source_target_pairs={{0,2},{1,3},{2,0},{3,1},{4,6},{5,7},{6,4},{7,5},{8,10},{9,11},{10,... | collective-permute-start | bytes 1572872 | tf_op jit(solution)/shard_map/ppermute | solution.py:35
  70.5 16.1 %collective-permute-start.2 = (f32[256,512]{0,1:T(8,128)S(1)}, f32[256,512]{0,1:T(8,128)}, u32[]{:S(2)}, u32[]{:S(2)}) collective-permute-start(f32[256,512]{0,1:T(8,128)S(1)} %broadcast_select_fusion.3), channel_id=1, source_target_pairs={{0,1},{1,0},{2,3},{3,2},{4,5},{5,4},{6,7},{7,6},{8,9},{9,8},{10,11... | collective-permute-start | bytes 1572872 | tf_op jit(solution)/shard_map/ppermute | solution.py:38
  75.1 59.6 %collective-permute-start.4 = (f32[448,512]{1,0:T(8,128)}, f32[448,512]{1,0:T(8,128)}, u32[]{:S(2)}, u32[]{:S(2)}) collective-permute-start(f32[448,512]{1,0:T(8,128)} %slice_select_fusion), channel_id=1, source_target_pairs={{0,2},{1,3},{2,0},{3,1},{4,6},{5,7},{6,4},{7,5},{8,10},{9,11},{10,... | collective-permute-start | bytes 2752520 | tf_op jit(solution)/shard_map/ppermute | solution.py:35
  80.2 100.8 %all-to-all-start.2 = ((f32[8,2,16,896]{3,2,1,0:T(8,128)}), f32[8,2,16,896]{3,2,1,0:T(8,128)}, u32[]{:S(2)}, u32[]{:S(2)}) async-start(f32[8,2,16,896]{3,2,1,0:T(8,128)} %bitcast.14), calls=%async_computation.2 | async-start | bytes 1835008 | tf_op jit(solution)/shard_map/all_to_all | solution.py:206
  137.1 19.4 %collective-permute-start.5 = (f32[448,512]{1,0:T(8,128)}, f32[448,512]{1,0:T(8,128)}, u32[]{:S(2)}, u32[]{:S(2)}) collective-permute-start(f32[448,512]{1,0:T(8,128)} %broadcast_select_fusion.2), channel_id=1, source_target_pairs={{0,1},{1,0},{2,3},{3,2},{4,5},{5,4},{6,7},{7,6},{8,9},{9,8},{10,11... | collective-permute-start | bytes 2752520 | tf_op jit(solution)/shard_map/ppermute | solution.py:38
  147.8 3.4 %copy-start.2 = (f32[4096,512]{1,0:T(8,128)}, f32[4096,512]{1,0:T(8,128)S(1)}, u32[]{:S(2)}) copy-start(f32[4096,512]{1,0:T(8,128)S(1)} %fusion.14) | copy-start | bytes 25165828
  181.0 22.0 %copy-start.1 = (s32[1,1,4,16]{3,2,1,0:T(4,128)S(1)}, s32[1,1,4,16]{3,2,1,0:T(4,128)}, u32[]{:S(2)}) copy-start(s32[1,1,4,16]{3,2,1,0:T(4,128)} %param.7) | copy-start | bytes 772

commit v8 on v6

--- a/solution.py
+++ b/solution.py
@@ -1,3 +1,5 @@
+import functools
+
 import jax
 import jax.numpy as jnp
 from jax import lax
@@ -123,6 +125,34 @@
     )(sym)
 
 
+def _block_add_kernel(col0, idx_ref, base_ref, add_ref, out_ref, sem):
+    width = out_ref.shape[1]
+    copy = pltpu.make_async_copy(base_ref.at[:, pl.ds(col0, width)], out_ref, sem)
+    copy.start()
+    copy.wait()
+
+    def accumulate(i, c):
+        r = idx_ref[i]
+        out_ref[pl.ds(r, 1), :] = out_ref[pl.ds(r, 1), :] + add_ref[pl.ds(i, 1), :]
+        return c
+
+    lax.fori_loop(0, add_ref.shape[0], accumulate, 0)
+
+
+def add_rows(base, col0, width, rows, values):
+    return pl.pallas_call(
+        functools.partial(_block_add_kernel, col0),
+        out_shape=jax.ShapeDtypeStruct((base.shape[0], width), base.dtype),
+        in_specs=[
+            pl.BlockSpec(memory_space=pltpu.SMEM),
+            pl.BlockSpec(memory_space=pl.ANY),
+            pl.BlockSpec(memory_space=pltpu.VMEM),
+        ],
+        out_specs=pl.BlockSpec(memory_space=pltpu.VMEM),
+        scratch_shapes=[pltpu.SemaphoreType.DMA(())],
+    )(rows, base, values)
+
+
 def local(front_block, child_blocks, child_rows, child_dest, panel_owner):
     local_rows = front_block[0]
     front_count = lax.axis_size("front")
@@ -139,7 +169,7 @@
     got_panel = lax.all_to_all(send_panel, "front", split_axis=0, concat_axis=0, tiled=True)
     got_rows = lax.all_to_all(send_rows, "front", split_axis=0, concat_axis=0, tiled=True)
     flat_rows = got_rows.reshape(-1)
-    panel_part = local_rows[:, :PB].at[flat_rows].add(got_panel.reshape(-1, PB))
+    panel_part = add_rows(local_rows, 0, PB, flat_rows, got_panel.reshape(-1, PB))
     send_trail = pack_slots(blocks[:, :, PB:], slot_index, front_count)
     trailing_rows = lax.all_to_all(send_trail, "front", split_axis=0, concat_axis=0, tiled=True)
     win_cols = local_rows.shape[1] - PB
@@ -153,7 +183,7 @@
     solved = jnp.dot(panel_part, factor_inverse.T, precision=FAST)
     window = jnp.dot(window_rows, factor_inverse.T, precision=FAST)
     schur_part = local_rows[:, PB:] - jnp.dot(solved, window.T, precision=FAST)
-    schur_part = schur_part.at[flat_rows].add(trailing_rows.reshape(-1, win_cols))
+    schur_part = add_rows(schur_part, 0, win_cols, flat_rows, trailing_rows.reshape(-1, win_cols))
     head = jnp.where(is_owner, pivot_factor, solved[:PB])
     panel_rows = lax.dynamic_update_slice(solved, head, (0, 0))
     return (panel_rows[None], schur_part[None])

time: 186 us -> 187 us (level)
  Pallas kernels: 41.4 us -> 65.5 us
  other arithmetic: 34 us -> 11.9 us
  local copies, waits for them, and re-layouts: 33 us -> 25.5 us
  waiting for transfers between devices: 20.8 us -> 28.2 us
    pallas_call x0 -> x2, Pallas kernels: none -> 24.1 us  [add_rows(): pl.pallas_call(functools.partial(_block_add_kernel, col0), out_shape=jax....]
    scatter-add x2 -> x0, other arithmetic: 22.7 us -> none  [the longest x1 13.9 us: local(): schur_part.at[flat_rows].add(trailing_rows.reshape(-1, win_cols))]
    slice x1 -> x0, local copies, waits for them, and re-layouts: 7.92 us -> none  [local(): panel_part = local_rows[:, :PB].at[flat_rows].add(got_panel.reshape(-1, PB))]
    all_to_all x1, waiting for transfers between devices: 5.72 us -> 13.1 us  [local(): lax.all_to_all(send_panel, 'front', split_axis=0, concat_axis=0, tiled=True)]
    unnamed x8 -> x16, local copies, waits for them, and re-layouts: 5.29 us -> 6.1 us
  transfers between devices with their start and end apart: 9 -> 9, of which waited for: 3 -> 3; matrix products, arithmetic and copies ran while one was open for 38% -> 33% of each run, Pallas kernels for 22% -> 22%
where the time goes in v8:
time: 187 us; the launch traced here: 186 us
  Pallas kernels  65.5 us (35%)
  matrix products  33.8 us (18%)
  waiting for transfers between devices  28.2 us (15%)
  local copies, waits for them, and re-layouts  25.5 us (14%)
  starting transfers between devices  19.1 us (10%)
  other arithmetic  11.9 us (6%)
    pallas_call x1, Pallas kernels, factor_and_inverse(): pl.pallas_call(_factor_kernel, out_shape=(jax.ShapeDtypeStruct((n, n), jn...  41.4 us
    pallas_call x2, Pallas kernels, add_rows(): pl.pallas_call(functools.partial(_block_add_kernel, col0), out_shape=jax....  24.1 us
    dot_general x1, matrix products, local(): schur_part = local_rows[:, PB:] - jnp.dot(solved, window.T, precision=FAST)  20.5 us
    all_to_all x1, waiting for transfers between devices, local(): lax.all_to_all(send_panel, 'front', split_axis=0, concat_axis=0, tiled=True)  13.1 us
    ppermute x2, waiting for transfers between devices, broadcast_from(): got = lax.ppermute(half, axis, pairs(size, bit))  12.3 us
    dot_general x1, matrix products, local(): solved = jnp.dot(panel_part, factor_inverse.T, precision=FAST)  9.52 us
    all_to_all x1, starting transfers between devices, local(): lax.all_to_all(send_rows, 'front', split_axis=0, concat_axis=0, tiled=True)  7.25 us
    unnamed x16, local copies, waits for them, and re-layouts  6.1 us
  transfers between devices with their start and end apart: 9, of which 3 were waited for; matrix products, arithmetic and copies ran while one was open for 33% of the time, Pallas kernels for 22%

profile of v8, /device:TPU:0, one launch (start us, length us, event | category | flops | bytes accessed | tf_op | source)
XLA Modules:
  0.0 185.6 jit_solution(16151189502276041039)
XLA Ops:
  0.6 0.0 copy-start
  0.6 0.9 convert_reduce_fusion
  1.6 0.7 fusion.12
  2.2 0.0 copy-done
  2.2 1.2 scatter_custom_fusion
  3.4 7.3 %all-to-all-start = ((s32[8,2,16]{2,1,0:T(2,128)}), s32[8,2,16]{2,1,0:T(2,128)S(1)}, u32[]{:S(2)}, u32[]{:S(2)}) async-start(s32[8,2,16]{2,1,0:T(2,128)} %bitcast.5), calls=%async_computation | async-start | bytes 16384 | tf_op jit(solution)/shard_map/all_to_all | solution.py:170
  10.6 0.9 slice.40
  11.6 0.9 broadcast_in_dim.23
  12.4 2.0 %scatter_fusion = f32[16,16,512]{2,1,0:T(8,128)} fusion(f32[16,16,512]{2,1,0:T(8,128)} %broadcast_in_dim.23, s32[4]{0:T(128)S(1)} %fusion.12, f32[4,16,512]{2,1,0:T(8,128)S(1)} %slice.40), kind=kCustom, calls=%fused_computation.1 | custom fusion | bytes 393232 | tf_op jit(solution)/shard_map/scatter | solution.py:19
  14.4 2.7 %all-to-all-done = s32[8,2,16]{2,1,0:T(2,128)S(1)} async-done(((s32[8,2,16]{2,1,0:T(2,128)}), s32[8,2,16]{2,1,0:T(2,128)S(1)}, u32[]{:S(2)}, u32[]{:S(2)}) %all-to-all-start) | async-done | bytes 1056 | tf_op jit(solution)/shard_map/all_to_all | solution.py:170
  17.2 3.5 %all-to-all-start.1 = ((f32[8,2,16,512]{3,2,1,0:T(8,128)}), f32[8,2,16,512]{3,2,1,0:T(8,128)S(1)}, u32[]{:S(2)}, u32[]{:S(2)}) async-start(f32[8,2,16,512]{3,2,1,0:T(8,128)} %bitcast.8), calls=%async_computation.1 | async-start | bytes 1048576 | tf_op jit(solution)/shard_map/all_to_all | solution.py:169
  20.7 0.6 reshape.55.idx_ref
  21.3 13.1 %all-to-all-done.1 = f32[8,2,16,512]{3,2,1,0:T(8,128)S(1)} async-done(((f32[8,2,16,512]{3,2,1,0:T(8,128)}), f32[8,2,16,512]{3,2,1,0:T(8,128)S(1)}, u32[]{:S(2)}, u32[]{:S(2)}) %all-to-all-start.1) | async-done | bytes 524320 | tf_op jit(solution)/shard_map/all_to_all | solution.py:169
  34.4 0.0 copy-start.3
  34.4 0.8 copy-done.3
  35.2 9.9 %shard_map.68 = f32[4096,512]{1,0:T(8,128)} custom-call(s32[256]{0:T(256)} %reshape.55.idx_ref, f32[4096,1408]{1,0:T(8,128)} %bitcast.41, f32[256,512]{1,0:T(8,128)} %bitcast.45), custom_call_target="tpu_custom_call" | custom-call | tf_op jit(solution)/shard_map/pallas_call | solution.py:143
  45.1 0.0 slice-start
  45.1 1.2 slice-done
  46.3 0.3 copy.17
  46.6 0.1 collective-permute-start
  46.7 2.9 %slice.46 = f32[896,512]{1,0:T(8,128)} slice(f32[4096,512]{1,0:T(8,128)} %shard_map.68), slice={[512:1408], [0:512]} | slice | bytes 3670016 | tf_op jit(solution)/shard_map/slice | solution.py:180
  49.6 0.5 collective-permute-start.3
  50.7 0.0 collective-permute-done
  50.7 0.2 broadcast_select_fusion.1
  51.0 0.1 slice_select_fusion.1
  51.0 1.6 collective-permute-start.1
  52.6 12.3 %collective-permute-done.1 = f32[256,512]{0,1:T(8,128)S(1)} collective-permute-done((f32[256,512]{0,1:T(8,128)S(1)}, f32[256,512]{0,1:T(8,128)S(1)}, u32[]{:S(2)}, u32[]{:S(2)}) %collective-permute-start.1) | collective-permute-done | bytes 524320 | tf_op jit(solution)/shard_map/ppermute | solution.py:37
  64.9 0.1 broadcast_select_fusion.3
  65.0 0.1 collective-permute-start.2
  65.1 0.0 collective-permute-done.3
  65.1 2.5 %broadcast_select_fusion = f32[896,512]{1,0:T(8,128)S(1)} fusion(f32[896,512]{1,0:T(8,128)} %collective-permute-done.3, pred[]{:T(512)S(6)} %eq.39, f32[4096,512]{1,0:T(8,128)} %shard_map.68), kind=kLoop, calls=%fused_computation.16 | loop fusion | flops 458752 | bytes 5505025 | tf_op jit(solution)/shard_map/jit(_where)/select_n | solution.py:31
  67.6 0.0 copy-start.6
  67.6 1.1 slice_select_fusion
  68.7 1.5 collective-permute-start.4
  70.3 0.0 copy-done.6
  70.3 1.0 broadcast_in_dim.26
  71.3 2.2 %scatter_fusion.1 = f32[16,16,896]{2,1,0:T(8,128)} fusion(f32[16,16,896]{2,1,0:T(8,128)} %broadcast_in_dim.26, s32[4]{0:T(128)S(1)} %fusion.12, f32[4,16,896]{2,1,0:T(8,128)S(1)} %slice.49), kind=kCustom, calls=%fused_computation.2 | custom fusion | bytes 688144 | tf_op jit(solution)/shard_map/scatter | solution.py:19
  73.5 4.4 %all-to-all-start.2 = ((f32[8,2,16,896]{3,2,1,0:T(8,128)}), f32[8,2,16,896]{3,2,1,0:T(8,128)}, u32[]{:S(2)}, u32[]{:S(2)}) async-start(f32[8,2,16,896]{3,2,1,0:T(8,128)} %bitcast.14), calls=%async_computation.2 | async-start | bytes 1835008 | tf_op jit(solution)/shard_map/all_to_all | solution.py:174
  77.9 0.0 collective-permute-done.2
  77.9 1.4 maximum_select_fusion.2
  79.3 1.3 copy.13
  80.6 2.4 %fusion.6.s_ref = f32[512,512]{1,0:T(8,128)} fusion(f32[512,512]{1,0:T(8,128)} %copy.13, f32[512,512]{0,1:T(8,128)S(1)} %maximum_select_fusion.2), kind=kLoop, calls=%fused_computation.13 | loop fusion | flops 524288 | bytes 3145728 | tf_op jit(solution)/shard_map/mul | solution.py:181
  83.1 41.4 %shard_map.69 = (f32[512,512]{1,0:T(8,128)}, f32[512,512]{1,0:T(8,128)}) custom-call(f32[512,512]{1,0:T(8,128)} %fusion.6.s_ref), custom_call_target="tpu_custom_call" | custom-call | tf_op jit(solution)/shard_map/pallas_call | solution.py:119
  124.5 1.6 copy.15
  126.0 0.0 copy-start.4
  126.0 0.0 collective-permute-done.4
  126.0 1.3 broadcast_select_fusion.2
  127.3 0.2 collective-permute-start.5
  127.6 0.0 copy-done.4
  127.6 9.5 %fusion.14 = f32[4096,512]{1,0:T(8,128)S(1)} fusion(f32[4096,512]{1,0:T(8,128)} %shard_map.68, f32[512,512]{1,0:T(8,128)S(1)} %copy-done.4), kind=kOutput, calls=%fused_computation.33 | convolution fusion | flops 6442450944 | bytes 17825792 | tf_op jit(solution)/shard_map/dot_general | solution.py:183
  137.1 0.0 copy-start.2
  137.1 3.4 %copy-done.2 = f32[4096,512]{1,0:T(8,128)} copy-done((f32[4096,512]{1,0:T(8,128)}, f32[4096,512]{1,0:T(8,128)S(1)}, u32[]{:S(2)}) %copy-start.2) | copy-done | bytes 8388632
  140.5 1.0 slice.44
  141.5 1.6 copy.18
  143.1 1.2 select_bitcast_fusion
  144.3 1.6 copy.16
  145.9 0.0 collective-permute-done.5
  146.0 0.0 copy-done.5
  146.0 3.7 %fusion = f32[896,512]{1,0:T(8,128)S(1)} fusion(f32[512,512]{1,0:T(8,128)S(1)} %copy-done.5, f32[448,512]{1,0:T(8,128)} %collective-permute-done.5, f32[448,512]{1,0:T(8,128)} %broadcast_select_fusion.2, pred[]{:T(512)S(6)} %eq.37), kind=kOutput, calls=%fused_computation.5 | convolution fusion | flops 1410662400 | bytes 4718593 | tf_op jit(solution)/shard_map/dot_general | solution.py:184
  149.7 20.5 %slice_subtract_fusion.base_ref = f32[4096,896]{1,0:T(8,128)} fusion(f32[4096,1408]{1,0:T(8,128)} %bitcast.42, f32[4096,512]{1,0:T(8,128)} %copy-done.2, f32[896,512]{1,0:T(8,128)S(1)} %fusion), kind=kOutput, calls=%fused_computation.3 | convolution fusion | flops 11277959168 | bytes 39583744 | tf_op jit(solution)/shard_map/dot_general | solution.py:185
  170.2 0.0 all-to-all-done.2
  170.3 14.3 %shard_map.70 = f32[4096,896]{1,0:T(8,128)} custom-call(s32[256]{0:T(256)} %reshape.55.idx_ref, f32[4096,896]{1,0:T(8,128)} %slice_subtract_fusion.base_ref, f32[256,896]{1,0:T(8,128)} %bitcast.15.add_ref), custom_call_target="tpu_custom_call" | custom-call | tf_op jit(solution)/shard_map/pallas_call | solution.py:143
  184.5 1.0 constant_dynamic-update-slice_fusion
  185.6 0.0 copy-done.1
  (3 shorter events, 0.0 us)
Async XLA Ops:
  0.6 1.6 copy-start
  3.4 13.8 %all-to-all-start = ((s32[8,2,16]{2,1,0:T(2,128)}), s32[8,2,16]{2,1,0:T(2,128)S(1)}, u32[]{:S(2)}, u32[]{:S(2)}) async-start(s32[8,2,16]{2,1,0:T(2,128)} %bitcast.5), calls=%async_computation | async-start | bytes 16384 | tf_op jit(solution)/shard_map/all_to_all | solution.py:170
  17.2 17.2 %all-to-all-start.1 = ((f32[8,2,16,512]{3,2,1,0:T(8,128)}), f32[8,2,16,512]{3,2,1,0:T(8,128)S(1)}, u32[]{:S(2)}, u32[]{:S(2)}) async-start(f32[8,2,16,512]{3,2,1,0:T(8,128)} %bitcast.8), calls=%async_computation.1 | async-start | bytes 1048576 | tf_op jit(solution)/shard_map/all_to_all | solution.py:169
  34.4 0.8 copy-start.3
  45.1 1.2 slice-start
  46.6 4.1 %collective-permute-start = (f32[512,512]{0,1:T(8,128)S(1)}, f32[512,512]{0,1:T(8,128)S(1)}, u32[]{:S(2)}, u32[]{:S(2)}) collective-permute-start(f32[512,512]{0,1:T(8,128)S(1)} %copy.17), channel_id=1, source_target_pairs={{0,1},{1,0},{2,3},{3,2},{4,5},{5,4},{6,7},{7,6},{8,9},{9,8},{10,11... | collective-permute-start | bytes 3145736 | tf_op jit(solution)/shard_map/ppermute | solution.py:30
  49.6 15.5 %collective-permute-start.3 = (f32[896,512]{1,0:T(8,128)}, f32[896,512]{1,0:T(8,128)}, u32[]{:S(2)}, u32[]{:S(2)}) collective-permute-start(f32[896,512]{1,0:T(8,128)} %slice.46), channel_id=1, source_target_pairs={{0,1},{1,0},{2,3},{3,2},{4,5},{5,4},{6,7},{7,6},{8,9},{9,8},{10,11... | collective-permute-start | bytes 5505032 | tf_op jit(solution)/shard_map/ppermute | solution.py:30
  51.0 13.9 %collective-permute-start.1 = (f32[256,512]{0,1:T(8,128)S(1)}, f32[256,512]{0,1:T(8,128)S(1)}, u32[]{:S(2)}, u32[]{:S(2)}) collective-permute-start(f32[256,512]{0,1:T(8,128)S(1)} %slice_select_fusion.1), channel_id=1, source_target_pairs={{0,2},{1,3},{2,0},{3,1},{4,6},{5,7},{6,4},{7,5},{8,10},{9,11},{10,... | collective-permute-start | bytes 1572872 | tf_op jit(solution)/shard_map/ppermute | solution.py:37
  65.0 12.9 %collective-permute-start.2 = (f32[256,512]{0,1:T(8,128)S(1)}, f32[256,512]{0,1:T(8,128)}, u32[]{:S(2)}, u32[]{:S(2)}) collective-permute-start(f32[256,512]{0,1:T(8,128)S(1)} %broadcast_select_fusion.3), channel_id=1, source_target_pairs={{0,1},{1,0},{2,3},{3,2},{4,5},{5,4},{6,7},{7,6},{8,9},{9,8},{10,11... | collective-permute-start | bytes 1572872 | tf_op jit(solution)/shard_map/ppermute | solution.py:40
  67.6 2.7 %copy-start.6 = (f32[1,1,4,16,1408]{4,3,2,1,0:T(8,128)S(1)}, f32[1,1,4,16,1408]{4,3,2,1,0:T(8,128)}, u32[]{:S(2)}) copy-start(f32[1,1,4,16,1408]{4,3,2,1,0:T(8,128)} %param.6) | copy-start | bytes 1081348
  68.7 57.3 %collective-permute-start.4 = (f32[448,512]{1,0:T(8,128)}, f32[448,512]{1,0:T(8,128)}, u32[]{:S(2)}, u32[]{:S(2)}) collective-permute-start(f32[448,512]{1,0:T(8,128)} %slice_select_fusion), channel_id=1, source_target_pairs={{0,2},{1,3},{2,0},{3,1},{4,6},{5,7},{6,4},{7,5},{8,10},{9,11},{10,... | collective-permute-start | bytes 2752520 | tf_op jit(solution)/shard_map/ppermute | solution.py:37
  73.5 96.8 %all-to-all-start.2 = ((f32[8,2,16,896]{3,2,1,0:T(8,128)}), f32[8,2,16,896]{3,2,1,0:T(8,128)}, u32[]{:S(2)}, u32[]{:S(2)}) async-start(f32[8,2,16,896]{3,2,1,0:T(8,128)} %bitcast.14), calls=%async_computation.2 | async-start | bytes 1835008 | tf_op jit(solution)/shard_map/all_to_all | solution.py:174
  126.0 1.6 copy-start.4
  127.3 18.6 %collective-permute-start.5 = (f32[448,512]{1,0:T(8,128)}, f32[448,512]{1,0:T(8,128)}, u32[]{:S(2)}, u32[]{:S(2)}) collective-permute-start(f32[448,512]{1,0:T(8,128)} %broadcast_select_fusion.2), channel_id=1, source_target_pairs={{0,1},{1,0},{2,3},{3,2},{4,5},{5,4},{6,7},{7,6},{8,9},{9,8},{10,11... | collective-permute-start | bytes 2752520 | tf_op jit(solution)/shard_map/ppermute | solution.py:40
  137.1 3.4 %copy-start.2 = (f32[4096,512]{1,0:T(8,128)}, f32[4096,512]{1,0:T(8,128)S(1)}, u32[]{:S(2)}) copy-start(f32[4096,512]{1,0:T(8,128)S(1)} %fusion.14) | copy-start | bytes 25165828
  144.3 1.7 copy-start.5
  170.3 15.3 %copy-start.1 = (s32[1,1,4,16]{3,2,1,0:T(4,128)S(1)}, s32[1,1,4,16]{3,2,1,0:T(4,128)}, u32[]{:S(2)}) copy-start(s32[1,1,4,16]{3,2,1,0:T(4,128)} %param.7) | copy-start | bytes 772

commit v9 on v8

--- a/solution.py
+++ b/solution.py
@@ -164,11 +164,11 @@
     same_front = target_front[:, None] == target_front[None, :]
     earlier = position[None, :] < position[:, None]
     slot_index = target_front * CAP + jnp.sum((same_front & earlier).astype(jnp.int32), axis=1)
-    send_rows = pack_slots(row_lists, slot_index, front_count)
-    send_panel = pack_slots(blocks[:, :, :PB], slot_index, front_count)
-    got_panel = lax.all_to_all(send_panel, "front", split_axis=0, concat_axis=0, tiled=True)
-    got_rows = lax.all_to_all(send_rows, "front", split_axis=0, concat_axis=0, tiled=True)
-    flat_rows = got_rows.reshape(-1)
+    row_lanes = jnp.zeros(blocks.shape[:2] + (128,), jnp.float32).at[:, :, 0].set(row_lists.astype(jnp.float32))
+    send_panel = pack_slots(jnp.concatenate([blocks[:, :, :PB], row_lanes], axis=2), slot_index, front_count)
+    got_both = lax.all_to_all(send_panel, "front", split_axis=0, concat_axis=0, tiled=True)
+    got_panel = got_both[..., :PB]
+    flat_rows = got_both[..., PB].reshape(-1).astype(jnp.int32)
     panel_part = add_rows(local_rows, 0, PB, flat_rows, got_panel.reshape(-1, PB))
     send_trail = pack_slots(blocks[:, :, PB:], slot_index, front_count)
     trailing_rows = lax.all_to_all(send_trail, "front", split_axis=0, concat_axis=0, tiled=True)

time: 187 us -> 183 us (0.979)
  blocking collectives: 0 us -> 24.8 us
  waiting for transfers between devices: 28.2 us -> 12.3 us
  starting transfers between devices: 19.1 us -> 8.35 us
  local copies, waits for them, and re-layouts: 25.5 us -> 22.4 us
    all_to_all x0 -> x1, blocking collectives: none -> 24.8 us  [local(): lax.all_to_all(send_panel, 'front', split_axis=0, concat_axis=0, tiled=True)]
    all_to_all x2 -> x0, waiting for transfers between devices: 15.9 us -> none  [the longest x1 13.1 us: local(): lax.all_to_all(send_panel, 'front', split_axis=0, concat_axis=0, tiled=True)]
    all_to_all x2 -> x0, starting transfers between devices: 10.7 us -> none  [the longest x1 7.25 us: local(): lax.all_to_all(send_rows, 'front', split_axis=0, concat_axis=0, tiled=True)]
    scatter x3 -> x2, local copies, waits for them, and re-layouts: 5.33 us -> 2.83 us  [pack_slots(): filled = empty.at[slot_index].set(values)]
    unnamed x16 -> x11, local copies, waits for them, and re-layouts: 6.1 us -> 5.39 us
  transfers between devices with their start and end apart: 9 -> 7, of which waited for: 3 -> 1; matrix products, arithmetic and copies ran while one was open for 33% -> 32% of each run, Pallas kernels for 22% -> 23%
where the time goes in v9:
time: 183 us; the launch traced here: 182 us
  Pallas kernels  65.5 us (36%)
  matrix products  33.9 us (19%)
  blocking collectives  24.8 us (14%)
  local copies, waits for them, and re-layouts  22.4 us (12%)
  other arithmetic  12.9 us (7%)
  waiting for transfers between devices  12.3 us (7%)
  starting transfers between devices  8.35 us (5%)
    pallas_call x1, Pallas kernels, factor_and_inverse(): pl.pallas_call(_factor_kernel, out_shape=(jax.ShapeDtypeStruct((n, n), jn...  41.4 us
    all_to_all x1, blocking collectives, local(): lax.all_to_all(send_panel, 'front', split_axis=0, concat_axis=0, tiled=True)  24.8 us
    pallas_call x2, Pallas kernels, add_rows(): pl.pallas_call(functools.partial(_block_add_kernel, col0), out_shape=jax....  24.1 us
    dot_general x1, matrix products, local(): schur_part = local_rows[:, PB:] - jnp.dot(solved, window.T, precision=FAST)  20.6 us
    ppermute x2, waiting for transfers between devices, broadcast_from(): got = lax.ppermute(half, axis, pairs(size, bit))  12.3 us
    dot_general x1, matrix products, local(): solved = jnp.dot(panel_part, factor_inverse.T, precision=FAST)  9.57 us
    unnamed x11, local copies, waits for them, and re-layouts  5.39 us
    all_to_all x1, starting transfers between devices, local(): lax.all_to_all(send_trail, 'front', split_axis=0, concat_axis=0, tiled=True)  4.42 us
  transfers between devices with their start and end apart: 7, of which 1 were waited for; matrix products, arithmetic and copies ran while one was open for 32% of the time, Pallas kernels for 23%

profile of v9, /device:TPU:0, one launch (start us, length us, event | category | flops | bytes accessed | tf_op | source)
XLA Modules:
  0.0 181.7 jit_solution(7372015444906185837)
XLA Ops:
  0.6 0.9 convert_reduce_fusion
  1.5 0.7 fusion.10
  2.2 0.7 convert_bitcast_fusion
  2.9 0.1 copy.42
  3.0 0.9 slice.67
  4.0 0.7 scatter_fusion
  4.6 24.8 %all_to_all.10 = f32[8,2,16,640]{3,2,1,0:T(8,128)S(1)} all-to-all(f32[8,2,16,640]{3,2,1,0:T(8,128)S(1)} %bitcast.42), channel_id=1, replica_groups=mesh['front'=8,'grp'=4] {'front'}, dimensions={0} | all-to-all | bytes 1310720 | tf_op jit(solution)/shard_map/all_to_all | solution.py:169
  29.4 0.4 fusion.8
  29.8 0.7 convert_element_type.23.idx_ref
  30.4 0.9 slice.69
  31.3 9.9 %shard_map.68 = f32[4096,512]{1,0:T(8,128)} custom-call(s32[256]{0:T(256)} %convert_element_type.23.idx_ref, f32[4096,1408]{1,0:T(8,128)} %bitcast.38, f32[256,512]{1,0:T(8,128)} %bitcast.43), custom_call_target="tpu_custom_call" | custom-call | tf_op jit(solution)/shard_map/pallas_call | solution.py:143
  41.2 0.0 slice-start
  41.2 1.2 slice-done
  42.4 0.3 copy.40
  42.7 0.1 collective-permute-start
  42.8 2.9 %slice.75 = f32[896,512]{1,0:T(8,128)} slice(f32[4096,512]{1,0:T(8,128)} %shard_map.68), slice={[512:1408], [0:512]} | slice | bytes 3670016 | tf_op jit(solution)/shard_map/slice | solution.py:180
  45.7 0.5 collective-permute-start.3
  46.8 0.0 collective-permute-done
  46.8 0.2 broadcast_select_fusion.1
  47.1 0.1 slice_select_fusion.1
  47.1 1.6 collective-permute-start.1
  48.7 12.3 %collective-permute-done.1 = f32[256,512]{0,1:T(8,128)S(1)} collective-permute-done((f32[256,512]{0,1:T(8,128)S(1)}, f32[256,512]{0,1:T(8,128)S(1)}, u32[]{:S(2)}, u32[]{:S(2)}) %collective-permute-start.1) | collective-permute-done | bytes 524320 | tf_op jit(solution)/shard_map/ppermute | solution.py:37
  61.1 0.1 broadcast_select_fusion.3
  61.2 0.1 collective-permute-start.2
  61.2 0.0 collective-permute-done.3
  61.2 2.5 %broadcast_select_fusion = f32[896,512]{1,0:T(8,128)S(1)} fusion(f32[896,512]{1,0:T(8,128)} %collective-permute-done.3, pred[]{:T(512)S(6)} %eq.39, f32[4096,512]{1,0:T(8,128)} %shard_map.68), kind=kLoop, calls=%fused_computation.15 | loop fusion | flops 458752 | bytes 5505025 | tf_op jit(solution)/shard_map/jit(_where)/select_n | solution.py:31
  63.7 0.0 copy-start.3
  63.7 1.1 slice_select_fusion
  64.8 1.5 collective-permute-start.4
  66.3 0.0 copy-done.3
  66.4 1.0 broadcast_in_dim.22
  67.4 2.2 %scatter_fusion.1 = f32[16,16,896]{2,1,0:T(8,128)} fusion(f32[16,16,896]{2,1,0:T(8,128)} %broadcast_in_dim.22, s32[4]{0:T(128)S(1)} %fusion.10, f32[4,16,896]{2,1,0:T(8,128)S(1)} %slice.78), kind=kCustom, calls=%fused_computation.1 | custom fusion | bytes 688144 | tf_op jit(solution)/shard_map/scatter | solution.py:19
  69.6 4.4 %all-to-all-start.1 = ((f32[8,2,16,896]{3,2,1,0:T(8,128)}), f32[8,2,16,896]{3,2,1,0:T(8,128)}, u32[]{:S(2)}, u32[]{:S(2)}) async-start(f32[8,2,16,896]{3,2,1,0:T(8,128)} %bitcast.13), calls=%async_computation.1 | async-start | bytes 1835008 | tf_op jit(solution)/shard_map/all_to_all | solution.py:174
  74.0 0.0 collective-permute-done.2
  74.0 1.4 maximum_select_fusion.2
  75.4 1.3 copy.36
  76.7 2.4 %fusion.6.s_ref = f32[512,512]{1,0:T(8,128)} fusion(f32[512,512]{1,0:T(8,128)} %copy.36, f32[512,512]{0,1:T(8,128)S(1)} %maximum_select_fusion.2), kind=kLoop, calls=%fused_computation.12 | loop fusion | flops 524288 | bytes 3145728 | tf_op jit(solution)/shard_map/mul | solution.py:181
  79.1 41.4 %shard_map.69 = (f32[512,512]{1,0:T(8,128)}, f32[512,512]{1,0:T(8,128)}) custom-call(f32[512,512]{1,0:T(8,128)} %fusion.6.s_ref), custom_call_target="tpu_custom_call" | custom-call | tf_op jit(solution)/shard_map/pallas_call | solution.py:119
  120.5 1.6 copy.38
  122.1 0.0 copy-start.1
  122.1 0.0 collective-permute-done.4
  122.1 1.3 broadcast_select_fusion.2
  123.4 0.2 collective-permute-start.5
  123.6 0.0 copy-done.1
  123.6 9.6 %fusion.12 = f32[4096,512]{1,0:T(8,128)S(1)} fusion(f32[4096,512]{1,0:T(8,128)} %shard_map.68, f32[512,512]{1,0:T(8,128)S(1)} %copy-done.1), kind=kOutput, calls=%fused_computation.34 | convolution fusion | flops 6442450944 | bytes 17825792 | tf_op jit(solution)/shard_map/dot_general | solution.py:183
  133.2 0.0 copy-start
  133.2 3.4 %copy-done = f32[4096,512]{1,0:T(8,128)} copy-done((f32[4096,512]{1,0:T(8,128)}, f32[4096,512]{1,0:T(8,128)S(1)}, u32[]{:S(2)}) %copy-start) | copy-done | bytes 8388632
  136.6 1.0 slice.73
  137.6 1.6 copy.41
  139.2 1.2 select_bitcast_fusion
  140.4 0.0 copy-start.2
  140.4 1.6 copy.39
  142.0 0.0 collective-permute-done.5
  142.0 0.0 copy-done.2
  142.0 3.8 %fusion = f32[896,512]{1,0:T(8,128)S(1)} fusion(f32[512,512]{1,0:T(8,128)S(1)} %copy-done.2, f32[448,512]{1,0:T(8,128)} %collective-permute-done.5, f32[448,512]{1,0:T(8,128)} %broadcast_select_fusion.2, pred[]{:T(512)S(6)} %eq.37), kind=kOutput, calls=%fused_computation.4 | convolution fusion | flops 1410662400 | bytes 4718593 | tf_op jit(solution)/shard_map/dot_general | solution.py:184
  145.8 20.6 %slice_subtract_fusion.base_ref = f32[4096,896]{1,0:T(8,128)} fusion(f32[4096,1408]{1,0:T(8,128)} %bitcast.39, f32[4096,512]{1,0:T(8,128)} %copy-done, f32[896,512]{1,0:T(8,128)S(1)} %fusion), kind=kOutput, calls=%fused_computation.2 | convolution fusion | flops 11277959168 | bytes 39583744 | tf_op jit(solution)/shard_map/dot_general | solution.py:185
  166.4 0.0 all-to-all-done.1
  166.4 14.2 %shard_map.70 = f32[4096,896]{1,0:T(8,128)} custom-call(s32[256]{0:T(256)} %convert_element_type.23.idx_ref, f32[4096,896]{1,0:T(8,128)} %slice_subtract_fusion.base_ref, f32[256,896]{1,0:T(8,128)} %bitcast.14.add_ref), custom_call_target="tpu_custom_call" | custom-call | tf_op jit(solution)/shard_map/pallas_call | solution.py:143
  180.6 1.0 constant_dynamic-update-slice_fusion
  (3 shorter events, 0.1 us)
Async XLA Ops:
  41.2 1.2 slice-start
  42.7 4.1 %collective-permute-start = (f32[512,512]{0,1:T(8,128)S(1)}, f32[512,512]{0,1:T(8,128)S(1)}, u32[]{:S(2)}, u32[]{:S(2)}) collective-permute-start(f32[512,512]{0,1:T(8,128)S(1)} %copy.40), channel_id=1, source_target_pairs={{0,1},{1,0},{2,3},{3,2},{4,5},{5,4},{6,7},{7,6},{8,9},{9,8},{10,11... | collective-permute-start | bytes 3145736 | tf_op jit(solution)/shard_map/ppermute | solution.py:30
  45.7 15.5 %collective-permute-start.3 = (f32[896,512]{1,0:T(8,128)}, f32[896,512]{1,0:T(8,128)}, u32[]{:S(2)}, u32[]{:S(2)}) collective-permute-start(f32[896,512]{1,0:T(8,128)} %slice.75), channel_id=1, source_target_pairs={{0,1},{1,0},{2,3},{3,2},{4,5},{5,4},{6,7},{7,6},{8,9},{9,8},{10,11... | collective-permute-start | bytes 5505032 | tf_op jit(solution)/shard_map/ppermute | solution.py:30
  47.1 13.9 %collective-permute-start.1 = (f32[256,512]{0,1:T(8,128)S(1)}, f32[256,512]{0,1:T(8,128)S(1)}, u32[]{:S(2)}, u32[]{:S(2)}) collective-permute-start(f32[256,512]{0,1:T(8,128)S(1)} %slice_select_fusion.1), channel_id=1, source_target_pairs={{0,2},{1,3},{2,0},{3,1},{4,6},{5,7},{6,4},{7,5},{8,10},{9,11},{10,... | collective-permute-start | bytes 1572872 | tf_op jit(solution)/shard_map/ppermute | solution.py:37
  61.2 12.8 %collective-permute-start.2 = (f32[256,512]{0,1:T(8,128)S(1)}, f32[256,512]{0,1:T(8,128)}, u32[]{:S(2)}, u32[]{:S(2)}) collective-permute-start(f32[256,512]{0,1:T(8,128)S(1)} %broadcast_select_fusion.3), channel_id=1, source_target_pairs={{0,1},{1,0},{2,3},{3,2},{4,5},{5,4},{6,7},{7,6},{8,9},{9,8},{10,11... | collective-permute-start | bytes 1572872 | tf_op jit(solution)/shard_map/ppermute | solution.py:40
  63.7 2.6 %copy-start.3 = (f32[1,1,4,16,1408]{4,3,2,1,0:T(8,128)S(1)}, f32[1,1,4,16,1408]{4,3,2,1,0:T(8,128)}, u32[]{:S(2)}) copy-start(f32[1,1,4,16,1408]{4,3,2,1,0:T(8,128)} %param.8) | copy-start | bytes 1081348
  64.8 57.3 %collective-permute-start.4 = (f32[448,512]{1,0:T(8,128)}, f32[448,512]{1,0:T(8,128)}, u32[]{:S(2)}, u32[]{:S(2)}) collective-permute-start(f32[448,512]{1,0:T(8,128)} %slice_select_fusion), channel_id=1, source_target_pairs={{0,2},{1,3},{2,0},{3,1},{4,6},{5,7},{6,4},{7,5},{8,10},{9,11},{10,... | collective-permute-start | bytes 2752520 | tf_op jit(solution)/shard_map/ppermute | solution.py:37
  69.6 96.8 %all-to-all-start.1 = ((f32[8,2,16,896]{3,2,1,0:T(8,128)}), f32[8,2,16,896]{3,2,1,0:T(8,128)}, u32[]{:S(2)}, u32[]{:S(2)}) async-start(f32[8,2,16,896]{3,2,1,0:T(8,128)} %bitcast.13), calls=%async_computation.1 | async-start | bytes 1835008 | tf_op jit(solution)/shard_map/all_to_all | solution.py:174
  122.1 1.5 copy-start.1
  123.4 18.6 %collective-permute-start.5 = (f32[448,512]{1,0:T(8,128)}, f32[448,512]{1,0:T(8,128)}, u32[]{:S(2)}, u32[]{:S(2)}) collective-permute-start(f32[448,512]{1,0:T(8,128)} %broadcast_select_fusion.2), channel_id=1, source_target_pairs={{0,1},{1,0},{2,3},{3,2},{4,5},{5,4},{6,7},{7,6},{8,9},{9,8},{10,11... | collective-permute-start | bytes 2752520 | tf_op jit(solution)/shard_map/ppermute | solution.py:40
  133.2 3.4 %copy-start = (f32[4096,512]{1,0:T(8,128)}, f32[4096,512]{1,0:T(8,128)S(1)}, u32[]{:S(2)}) copy-start(f32[4096,512]{1,0:T(8,128)S(1)} %fusion.12) | copy-start | bytes 25165828
  140.4 1.7 copy-start.2

commit v10 on v9

--- a/solution.py
+++ b/solution.py
@@ -153,6 +153,17 @@
     )(rows, base, values)
 
 
+def exchange(send, axis):
+    size = lax.axis_size(axis)
+    me = lax.axis_index(axis)
+    got = [lax.dynamic_index_in_dim(send, me, axis=0, keepdims=False)]
+    for shift in range(1, size):
+        outgoing = lax.dynamic_index_in_dim(send, (me + shift) % size, axis=0, keepdims=False)
+        got.append(lax.ppermute(outgoing, axis, [(d, (d + shift) % size) for d in range(size)]))
+    by_shift = jnp.stack(got, axis=0)
+    return jnp.take(by_shift, (me - jnp.arange(size)) % size, axis=0)
+
+
 def local(front_block, child_blocks, child_rows, child_dest, panel_owner):
     local_rows = front_block[0]
     front_count = lax.axis_size("front")
@@ -166,7 +177,7 @@
     slot_index = target_front * CAP + jnp.sum((same_front & earlier).astype(jnp.int32), axis=1)
     row_lanes = jnp.zeros(blocks.shape[:2] + (128,), jnp.float32).at[:, :, 0].set(row_lists.astype(jnp.float32))
     send_panel = pack_slots(jnp.concatenate([blocks[:, :, :PB], row_lanes], axis=2), slot_index, front_count)
-    got_both = lax.all_to_all(send_panel, "front", split_axis=0, concat_axis=0, tiled=True)
+    got_both = exchange(send_panel, "front")
     got_panel = got_both[..., :PB]
     flat_rows = got_both[..., PB].reshape(-1).astype(jnp.int32)
     panel_part = add_rows(local_rows, 0, PB, flat_rows, got_panel.reshape(-1, PB))

time: 183 us -> 189 us (1.033)
  blocking collectives: 24.8 us -> 0 us
  waiting for transfers between devices: 12.3 us -> 30.6 us
  starting transfers between devices: 8.35 us -> 19.1 us
    all_to_all x1 -> x0, blocking collectives: 24.8 us -> none  [local(): lax.all_to_all(send_panel, 'front', split_axis=0, concat_axis=0, tiled=True)]
    ppermute x0 -> x7, waiting for transfers between devices: none -> 18.2 us  [exchange(): lax.ppermute(outgoing, axis, [(d, (d + shift) % size) for d in range(size)])]
    ppermute x0 -> x7, starting transfers between devices: none -> 11 us  [exchange(): lax.ppermute(outgoing, axis, [(d, (d + shift) % size) for d in range(size)])]
    unnamed x11 -> x17, local copies, waits for them, and re-layouts: 5.39 us -> 5.44 us
  transfers between devices with their start and end apart: 7 -> 14, of which waited for: 1 -> 4; matrix products, arithmetic and copies ran while one was open for 32% -> 31% of each run, Pallas kernels for 23% -> 22%
where the time goes in v10:
time: 189 us; the launch traced here: 188 us
  Pallas kernels  65.5 us (35%)
  matrix products  33.9 us (18%)
  waiting for transfers between devices  30.6 us (16%)
  local copies, waits for them, and re-layouts  23.1 us (12%)
  starting transfers between devices  19.1 us (10%)
  other arithmetic  14.2 us (8%)
    pallas_call x1, Pallas kernels, factor_and_inverse(): pl.pallas_call(_factor_kernel, out_shape=(jax.ShapeDtypeStruct((n, n), jn...  41.4 us
    pallas_call x2, Pallas kernels, add_rows(): pl.pallas_call(functools.partial(_block_add_kernel, col0), out_shape=jax....  24.1 us
    dot_general x1, matrix products, local(): schur_part = local_rows[:, PB:] - jnp.dot(solved, window.T, precision=FAST)  20.5 us
    ppermute x7, waiting for transfers between devices, exchange(): lax.ppermute(outgoing, axis, [(d, (d + shift) % size) for d in range(size)])  18.2 us
    ppermute x2, waiting for transfers between devices, broadcast_from(): got = lax.ppermute(half, axis, pairs(size, bit))  12.3 us
    ppermute x7, starting transfers between devices, exchange(): lax.ppermute(outgoing, axis, [(d, (d + shift) % size) for d in range(size)])  11 us
    dot_general x1, matrix products, local(): solved = jnp.dot(panel_part, factor_inverse.T, precision=FAST)  9.58 us
    unnamed x17, local copies, waits for them, and re-layouts  5.44 us
  transfers between devices with their start and end apart: 14, of which 4 were waited for; matrix products, arithmetic and copies ran while one was open for 31% of the time, Pallas kernels for 22%

profile of v10, /device:TPU:0, one launch (start us, length us, event | category | flops | bytes accessed | tf_op | source)
XLA Modules:
  0.0 188.2 jit_solution(13927709726592400154)
XLA Ops:
  0.7 0.9 convert_reduce_fusion
  1.6 0.7 fusion.12
  2.3 0.7 convert_bitcast_fusion
  3.0 0.1 copy.34
  3.1 0.9 slice.69
  4.1 0.7 scatter_fusion
  4.8 0.1 dynamic-slice_bitcast_fusion
  4.9 6.0 %collective-permute-start.6 = (f32[2,16,640]{2,1,0:T(8,128)S(1)}, f32[2,16,640]{2,1,0:T(8,128)S(1)}, u32[]{:S(2)}, u32[]{:S(2)}) collective-permute-start(f32[2,16,640]{2,1,0:T(8,128)S(1)} %get-tuple-element.18), channel_id=1, source_target_pairs={{0,28},{4,0},{8,4},{12,8},{16,12},{20,16},{24,20},{28,24},{1,29},{... | collective-permute-start | bytes 245768 | tf_op jit(solution)/shard_map/ppermute | solution.py:162
  10.9 0.4 collective-permute-start.5
  11.3 0.0 collective-permute-start.4
  11.3 3.0 %collective-permute-start.3 = (f32[2,16,640]{2,1,0:T(8,128)S(1)}, f32[2,16,640]{2,1,0:T(8,128)S(1)}, u32[]{:S(2)}, u32[]{:S(2)}) collective-permute-start(f32[2,16,640]{2,1,0:T(8,128)S(1)} %get-tuple-element.21), channel_id=1, source_target_pairs={{0,16},{4,20},{8,24},{12,28},{16,0},{20,4},{24,8},{28,12},{1,17},{... | collective-permute-start | bytes 245768 | tf_op jit(solution)/shard_map/ppermute | solution.py:162
  14.3 1.5 collective-permute-start
  15.9 5.7 %collective-permute-done = f32[2,16,640]{2,1,0:T(8,128)S(1)} collective-permute-done((f32[2,16,640]{2,1,0:T(8,128)S(1)}, f32[2,16,640]{2,1,0:T(8,128)S(1)}, u32[]{:S(2)}, u32[]{:S(2)}) %collective-permute-start) | collective-permute-done | bytes 81952 | tf_op jit(solution)/shard_map/ppermute | solution.py:162
  21.6 0.0 collective-permute-start.1
  21.6 6.3 %collective-permute-done.1 = f32[2,16,640]{2,1,0:T(8,128)S(1)} collective-permute-done((f32[2,16,640]{2,1,0:T(8,128)S(1)}, f32[2,16,640]{2,1,0:T(8,128)S(1)}, u32[]{:S(2)}, u32[]{:S(2)}) %collective-permute-start.1) | collective-permute-done | bytes 81952 | tf_op jit(solution)/shard_map/ppermute | solution.py:162
  27.9 0.0 collective-permute-start.2
  27.9 6.2 %collective-permute-done.2 = f32[2,16,640]{2,1,0:T(8,128)S(1)} collective-permute-done((f32[2,16,640]{2,1,0:T(8,128)S(1)}, f32[2,16,640]{2,1,0:T(8,128)S(1)}, u32[]{:S(2)}, u32[]{:S(2)}) %collective-permute-start.2) | collective-permute-done | bytes 81952 | tf_op jit(solution)/shard_map/ppermute | solution.py:162
  34.1 0.0 collective-permute-done.3
  34.2 0.0 collective-permute-done.4
  34.3 0.6 gather_fusion
  34.9 0.1 broadcast_select_fusion.3
  35.0 0.4 fusion.8
  35.3 0.9 slice.71
  36.2 0.6 convert_element_type.23.idx_ref
  36.8 9.9 %shard_map.68 = f32[4096,512]{1,0:T(8,128)} custom-call(s32[256]{0:T(256)} %convert_element_type.23.idx_ref, f32[4096,1408]{1,0:T(8,128)} %bitcast.68, f32[256,512]{1,0:T(8,128)} %bitcast.73), custom_call_target="tpu_custom_call" | custom-call | tf_op jit(solution)/shard_map/pallas_call | solution.py:143
  46.7 0.0 slice-start
  46.7 1.2 slice-done
  47.9 0.3 copy.32
  48.3 0.1 collective-permute-start.7
  48.3 2.9 %slice.77 = f32[896,512]{1,0:T(8,128)} slice(f32[4096,512]{1,0:T(8,128)} %shard_map.68), slice={[512:1408], [0:512]} | slice | bytes 3670016 | tf_op jit(solution)/shard_map/slice | solution.py:191
  51.2 0.5 collective-permute-start.10
  52.4 0.2 broadcast_select_fusion.1
  52.6 0.1 slice_select_fusion.1
  52.7 1.6 collective-permute-start.8
  54.3 12.3 %collective-permute-done.8 = f32[256,512]{0,1:T(8,128)S(1)} collective-permute-done((f32[256,512]{0,1:T(8,128)S(1)}, f32[256,512]{0,1:T(8,128)S(1)}, u32[]{:S(2)}, u32[]{:S(2)}) %collective-permute-start.8) | collective-permute-done | bytes 524320 | tf_op jit(solution)/shard_map/ppermute | solution.py:37
  66.6 0.1 broadcast_select_fusion.4
  66.7 0.1 collective-permute-start.9
  66.8 2.5 %broadcast_select_fusion = f32[896,512]{1,0:T(8,128)S(1)} fusion(f32[896,512]{1,0:T(8,128)} %collective-permute-done.10, pred[]{:T(512)S(6)} %eq.48, f32[4096,512]{1,0:T(8,128)} %shard_map.68), kind=kLoop, calls=%fused_computation.16 | loop fusion | flops 458752 | bytes 5505025 | tf_op jit(solution)/shard_map/jit(_where)/select_n | solution.py:31
  69.2 0.0 copy-start.3
  69.3 1.1 slice_select_fusion
  70.4 1.5 collective-permute-start.11
  71.9 1.0 broadcast_in_dim.34
  73.0 2.2 %scatter_fusion.1 = f32[16,16,896]{2,1,0:T(8,128)} fusion(f32[16,16,896]{2,1,0:T(8,128)} %broadcast_in_dim.34, s32[4]{0:T(128)S(1)} %fusion.12, f32[4,16,896]{2,1,0:T(8,128)S(1)} %slice.80), kind=kCustom, calls=%fused_computation.2 | custom fusion | bytes 688144 | tf_op jit(solution)/shard_map/scatter | solution.py:19
  75.1 4.4 %all-to-all-start = ((f32[8,2,16,896]{3,2,1,0:T(8,128)}), f32[8,2,16,896]{3,2,1,0:T(8,128)}, u32[]{:S(2)}, u32[]{:S(2)}) async-start(f32[8,2,16,896]{3,2,1,0:T(8,128)} %bitcast.28), calls=%async_computation | async-start | bytes 1835008 | tf_op jit(solution)/shard_map/all_to_all | solution.py:185
  79.5 1.4 maximum_select_fusion.2
  80.9 1.3 copy.28
  82.2 2.4 %fusion.6.s_ref = f32[512,512]{1,0:T(8,128)} fusion(f32[512,512]{1,0:T(8,128)} %copy.28, f32[512,512]{0,1:T(8,128)S(1)} %maximum_select_fusion.2), kind=kLoop, calls=%fused_computation.13 | loop fusion | flops 524288 | bytes 3145728 | tf_op jit(solution)/shard_map/mul | solution.py:192
  84.6 41.4 %shard_map.69 = (f32[512,512]{1,0:T(8,128)}, f32[512,512]{1,0:T(8,128)}) custom-call(f32[512,512]{1,0:T(8,128)} %fusion.6.s_ref), custom_call_target="tpu_custom_call" | custom-call | tf_op jit(solution)/shard_map/pallas_call | solution.py:119
  126.0 1.6 copy.30
  127.6 0.0 collective-permute-done.11
  127.6 2.5 %broadcast_select_fusion.2 = f32[448,512]{1,0:T(8,128)} fusion(f32[448,512]{1,0:T(8,128)} %collective-permute-done.11, pred[]{:T(512)S(6)} %eq.47, f32[896,512]{1,0:T(8,128)S(1)} %broadcast_select_fusion, pred[]{:T(512)S(6)} %eq.46), kind=kLoop, calls=%fused_computation.20 | loop fusion | flops 458752 | bytes 3670018 | tf_op jit(solution)/shard_map/jit(_where)/select_n | solution.py:38
  130.2 9.6 %fusion.15 = f32[4096,512]{1,0:T(8,128)S(1)} fusion(f32[4096,512]{1,0:T(8,128)} %shard_map.68, f32[512,512]{1,0:T(8,128)S(1)} %copy-done.1), kind=kOutput, calls=%fused_computation.64 | convolution fusion | flops 6442450944 | bytes 17825792 | tf_op jit(solution)/shard_map/dot_general | solution.py:194
  139.7 0.0 copy-start
  139.8 3.4 %copy-done = f32[4096,512]{1,0:T(8,128)} copy-done((f32[4096,512]{1,0:T(8,128)}, f32[4096,512]{1,0:T(8,128)S(1)}, u32[]{:S(2)}) %copy-start) | copy-done | bytes 8388632
  143.1 1.0 slice.75
  144.2 1.6 copy.33
  145.7 1.2 select_bitcast_fusion
  146.9 1.6 copy.31
  148.6 0.0 collective-permute-done.12
  148.6 3.7 %fusion = f32[896,512]{1,0:T(8,128)S(1)} fusion(f32[512,512]{1,0:T(8,128)S(1)} %copy-done.2, f32[448,512]{1,0:T(8,128)} %collective-permute-done.12, f32[448,512]{1,0:T(8,128)} %broadcast_select_fusion.2, pred[]{:T(512)S(6)} %eq.46), kind=kOutput, calls=%fused_computation.5 | convolution fusion | flops 1410662400 | bytes 4718593 | tf_op jit(solution)/shard_map/dot_general | solution.py:195
  152.3 20.5 %slice_subtract_fusion.base_ref = f32[4096,896]{1,0:T(8,128)} fusion(f32[4096,1408]{1,0:T(8,128)} %bitcast.69, f32[4096,512]{1,0:T(8,128)} %copy-done, f32[896,512]{1,0:T(8,128)S(1)} %fusion), kind=kOutput, calls=%fused_computation.3 | convolution fusion | flops 11277959168 | bytes 39583744 | tf_op jit(solution)/shard_map/dot_general | solution.py:196
  172.9 0.0 all-to-all-done
  172.9 14.2 %shard_map.70 = f32[4096,896]{1,0:T(8,128)} custom-call(s32[256]{0:T(256)} %convert_element_type.23.idx_ref, f32[4096,896]{1,0:T(8,128)} %slice_subtract_fusion.base_ref, f32[256,896]{1,0:T(8,128)} %bitcast.29.add_ref), custom_call_target="tpu_custom_call" | custom-call | tf_op jit(solution)/shard_map/pallas_call | solution.py:143
  187.1 1.0 constant_dynamic-update-slice_fusion
  (24 shorter events, 0.2 us)
Async XLA Ops:
  4.9 29.4 %collective-permute-start.6 = (f32[2,16,640]{2,1,0:T(8,128)S(1)}, f32[2,16,640]{2,1,0:T(8,128)S(1)}, u32[]{:S(2)}, u32[]{:S(2)}) collective-permute-start(f32[2,16,640]{2,1,0:T(8,128)S(1)} %get-tuple-element.18), channel_id=1, source_target_pairs={{0,28},{4,0},{8,4},{12,8},{16,12},{20,16},{24,20},{28,24},{1,29},{... | collective-permute-start | bytes 245768 | tf_op jit(solution)/shard_map/ppermute | solution.py:162
  10.9 23.3 %collective-permute-start.5 = (f32[2,16,640]{2,1,0:T(8,128)S(1)}, f32[2,16,640]{2,1,0:T(8,128)S(1)}, u32[]{:S(2)}, u32[]{:S(2)}) collective-permute-start(f32[2,16,640]{2,1,0:T(8,128)S(1)} %get-tuple-element.19), channel_id=1, source_target_pairs={{0,24},{4,28},{8,0},{12,4},{16,8},{20,12},{24,16},{28,20},{1,25},{... | collective-permute-start | bytes 245768 | tf_op jit(solution)/shard_map/ppermute | solution.py:162
  11.3 22.8 %collective-permute-start.4 = (f32[2,16,640]{2,1,0:T(8,128)S(1)}, f32[2,16,640]{2,1,0:T(8,128)S(1)}, u32[]{:S(2)}, u32[]{:S(2)}) collective-permute-start(f32[2,16,640]{2,1,0:T(8,128)S(1)} %get-tuple-element.20), channel_id=1, source_target_pairs={{0,20},{4,24},{8,28},{12,0},{16,4},{20,8},{24,12},{28,16},{1,21},{... | collective-permute-start | bytes 245768 | tf_op jit(solution)/shard_map/ppermute | solution.py:162
  11.3 22.8 %collective-permute-start.3 = (f32[2,16,640]{2,1,0:T(8,128)S(1)}, f32[2,16,640]{2,1,0:T(8,128)S(1)}, u32[]{:S(2)}, u32[]{:S(2)}) collective-permute-start(f32[2,16,640]{2,1,0:T(8,128)S(1)} %get-tuple-element.21), channel_id=1, source_target_pairs={{0,16},{4,20},{8,24},{12,28},{16,0},{20,4},{24,8},{28,12},{1,17},{... | collective-permute-start | bytes 245768 | tf_op jit(solution)/shard_map/ppermute | solution.py:162
  14.3 7.2 %collective-permute-start = (f32[2,16,640]{2,1,0:T(8,128)S(1)}, f32[2,16,640]{2,1,0:T(8,128)S(1)}, u32[]{:S(2)}, u32[]{:S(2)}) collective-permute-start(f32[2,16,640]{2,1,0:T(8,128)S(1)} %get-tuple-element.24), channel_id=1, source_target_pairs={{0,4},{4,8},{8,12},{12,16},{16,20},{20,24},{24,28},{28,0},{1,5},{5... | collective-permute-start | bytes 245768 | tf_op jit(solution)/shard_map/ppermute | solution.py:162
  21.6 6.3 %collective-permute-start.1 = (f32[2,16,640]{2,1,0:T(8,128)S(1)}, f32[2,16,640]{2,1,0:T(8,128)S(1)}, u32[]{:S(2)}, u32[]{:S(2)}) collective-permute-start(f32[2,16,640]{2,1,0:T(8,128)S(1)} %get-tuple-element.23), channel_id=1, source_target_pairs={{0,8},{4,12},{8,16},{12,20},{16,24},{20,28},{24,0},{28,4},{1,9},{5... | collective-permute-start | bytes 245768 | tf_op jit(solution)/shard_map/ppermute | solution.py:162
  27.9 6.2 %collective-permute-start.2 = (f32[2,16,640]{2,1,0:T(8,128)S(1)}, f32[2,16,640]{2,1,0:T(8,128)S(1)}, u32[]{:S(2)}, u32[]{:S(2)}) collective-permute-start(f32[2,16,640]{2,1,0:T(8,128)S(1)} %get-tuple-element.22), channel_id=1, source_target_pairs={{0,12},{4,16},{8,20},{12,24},{16,28},{20,0},{24,4},{28,8},{1,13},{... | collective-permute-start | bytes 245768 | tf_op jit(solution)/shard_map/ppermute | solution.py:162
  46.7 1.2 slice-start
  48.3 4.1 %collective-permute-start.7 = (f32[512,512]{0,1:T(8,128)S(1)}, f32[512,512]{0,1:T(8,128)S(1)}, u32[]{:S(2)}, u32[]{:S(2)}) collective-permute-start(f32[512,512]{0,1:T(8,128)S(1)} %copy.32), channel_id=1, source_target_pairs={{0,1},{1,0},{2,3},{3,2},{4,5},{5,4},{6,7},{7,6},{8,9},{9,8},{10,11... | collective-permute-start | bytes 3145736 | tf_op jit(solution)/shard_map/ppermute | solution.py:30
  51.2 15.5 %collective-permute-start.10 = (f32[896,512]{1,0:T(8,128)}, f32[896,512]{1,0:T(8,128)}, u32[]{:S(2)}, u32[]{:S(2)}) collective-permute-start(f32[896,512]{1,0:T(8,128)} %slice.77), channel_id=1, source_target_pairs={{0,1},{1,0},{2,3},{3,2},{4,5},{5,4},{6,7},{7,6},{8,9},{9,8},{10,11... | collective-permute-start | bytes 5505032 | tf_op jit(solution)/shard_map/ppermute | solution.py:30
  52.7 13.9 %collective-permute-start.8 = (f32[256,512]{0,1:T(8,128)S(1)}, f32[256,512]{0,1:T(8,128)S(1)}, u32[]{:S(2)}, u32[]{:S(2)}) collective-permute-start(f32[256,512]{0,1:T(8,128)S(1)} %slice_select_fusion.1), channel_id=1, source_target_pairs={{0,2},{1,3},{2,0},{3,1},{4,6},{5,7},{6,4},{7,5},{8,10},{9,11},{10,... | collective-permute-start | bytes 1572872 | tf_op jit(solution)/shard_map/ppermute | solution.py:37
  66.7 12.9 %collective-permute-start.9 = (f32[256,512]{0,1:T(8,128)S(1)}, f32[256,512]{0,1:T(8,128)}, u32[]{:S(2)}, u32[]{:S(2)}) collective-permute-start(f32[256,512]{0,1:T(8,128)S(1)} %broadcast_select_fusion.4), channel_id=1, source_target_pairs={{0,1},{1,0},{2,3},{3,2},{4,5},{5,4},{6,7},{7,6},{8,9},{9,8},{10,11... | collective-permute-start | bytes 1572872 | tf_op jit(solution)/shard_map/ppermute | solution.py:40
  69.2 2.7 %copy-start.3 = (f32[1,1,4,16,1408]{4,3,2,1,0:T(8,128)S(1)}, f32[1,1,4,16,1408]{4,3,2,1,0:T(8,128)}, u32[]{:S(2)}) copy-start(f32[1,1,4,16,1408]{4,3,2,1,0:T(8,128)} %param.8) | copy-start | bytes 1081348
  70.4 57.2 %collective-permute-start.11 = (f32[448,512]{1,0:T(8,128)}, f32[448,512]{1,0:T(8,128)}, u32[]{:S(2)}, u32[]{:S(2)}) collective-permute-start(f32[448,512]{1,0:T(8,128)} %slice_select_fusion), channel_id=1, source_target_pairs={{0,2},{1,3},{2,0},{3,1},{4,6},{5,7},{6,4},{7,5},{8,10},{9,11},{10,... | collective-permute-start | bytes 2752520 | tf_op jit(solution)/shard_map/ppermute | solution.py:37
  75.1 97.8 %all-to-all-start = ((f32[8,2,16,896]{3,2,1,0:T(8,128)}), f32[8,2,16,896]{3,2,1,0:T(8,128)}, u32[]{:S(2)}, u32[]{:S(2)}) async-start(f32[8,2,16,896]{3,2,1,0:T(8,128)} %bitcast.28), calls=%async_computation | async-start | bytes 1835008 | tf_op jit(solution)/shard_map/all_to_all | solution.py:185
  127.6 2.6 %copy-start.1 = (f32[512,512]{1,0:T(8,128)S(1)}, f32[512,512]{1,0:T(8,128)}, u32[]{:S(2)}) copy-start(f32[512,512]{1,0:T(8,128)} %get-tuple-element.16) | copy-start | bytes 3145732
  130.2 18.4 %collective-permute-start.12 = (f32[448,512]{1,0:T(8,128)}, f32[448,512]{1,0:T(8,128)}, u32[]{:S(2)}, u32[]{:S(2)}) collective-permute-start(f32[448,512]{1,0:T(8,128)} %broadcast_select_fusion.2), channel_id=1, source_target_pairs={{0,1},{1,0},{2,3},{3,2},{4,5},{5,4},{6,7},{7,6},{8,9},{9,8},{10,11... | collective-permute-start | bytes 2752520 | tf_op jit(solution)/shard_map/ppermute | solution.py:40
  139.7 3.4 %copy-start = (f32[4096,512]{1,0:T(8,128)}, f32[4096,512]{1,0:T(8,128)S(1)}, u32[]{:S(2)}) copy-start(f32[4096,512]{1,0:T(8,128)S(1)} %fusion.15) | copy-start | bytes 25165828
  146.9 1.7 copy-start.2

commit v11 on v9

--- a/solution.py
+++ b/solution.py
@@ -153,6 +153,29 @@
     )(rows, base, values)
 
 
+def _head_kernel(flag_ref, factor_ref, solved_ref, out_ref, sem):
+    @pl.when(flag_ref[0] == 1)
+    def _():
+        copy = pltpu.make_async_copy(factor_ref, out_ref.at[pl.ds(0, factor_ref.shape[0])], sem)
+        copy.start()
+        copy.wait()
+
+
+def put_head(solved, factor, flag):
+    return pl.pallas_call(
+        _head_kernel,
+        out_shape=jax.ShapeDtypeStruct(solved.shape, solved.dtype),
+        in_specs=[
+            pl.BlockSpec(memory_space=pltpu.SMEM),
+            pl.BlockSpec(memory_space=pltpu.VMEM),
+            pl.BlockSpec(memory_space=pl.ANY),
+        ],
+        out_specs=pl.BlockSpec(memory_space=pl.ANY),
+        scratch_shapes=[pltpu.SemaphoreType.DMA(())],
+        input_output_aliases={2: 0},
+    )(flag, factor, solved)
+
+
 def local(front_block, child_blocks, child_rows, child_dest, panel_owner):
     local_rows = front_block[0]
     front_count = lax.axis_size("front")
@@ -184,8 +207,7 @@
     window = jnp.dot(window_rows, factor_inverse.T, precision=FAST)
     schur_part = local_rows[:, PB:] - jnp.dot(solved, window.T, precision=FAST)
     schur_part = add_rows(schur_part, 0, win_cols, flat_rows, trailing_rows.reshape(-1, win_cols))
-    head = jnp.where(is_owner, pivot_factor, solved[:PB])
-    panel_rows = lax.dynamic_update_slice(solved, head, (0, 0))
+    panel_rows = put_head(solved, pivot_factor, is_owner.astype(jnp.int32).reshape(1))
     return (panel_rows[None], schur_part[None])
 
 

time: 183 us -> 181 us (0.989)
  local copies, waits for them, and re-layouts: 22.4 us -> 12.2 us
  waiting for transfers between devices: 12.3 us -> 20.5 us
  other arithmetic: 12.9 us -> 10.5 us
    ppermute x2, waiting for transfers between devices: 12.3 us -> 17.5 us  [broadcast_from(): got = lax.ppermute(half, axis, pairs(size, bit))]
    unnamed x11 -> x10, local copies, waits for them, and re-layouts: 5.39 us -> 0.45 us
    ppermute x2, waiting for transfers between devices: 0.01 us -> 2.96 us  [broadcast_from(): got = lax.ppermute(x, axis, pairs(size, 1))]
    dot_general x1, matrix products: 3.76 us -> 6.46 us  [local(): window = jnp.dot(window_rows, factor_inverse.T, precision=FAST)]
    dot_general x1, matrix products: 20.6 us -> 18.3 us  [local(): schur_part = local_rows[:, PB:] - jnp.dot(solved, window.T, precision=FAST)]
  transfers between devices with their start and end apart: 7 -> 7, of which waited for: 1 -> 3; matrix products, arithmetic and copies ran while one was open for 32% -> 27% of each run, Pallas kernels for 23% -> 23%
where the time goes in v11:
time: 181 us; the launch traced here: 179 us
  Pallas kernels  66.8 us (37%)
  matrix products  35.7 us (20%)
  blocking collectives  24.8 us (14%)
  waiting for transfers between devices  20.5 us (11%)
  local copies, waits for them, and re-layouts  12.2 us (7%)
  other arithmetic  10.5 us (6%)
  starting transfers between devices  6.65 us (4%)
    pallas_call x1, Pallas kernels, factor_and_inverse(): pl.pallas_call(_factor_kernel, out_shape=(jax.ShapeDtypeStruct((n, n), jn...  41.4 us
    all_to_all x1, blocking collectives, local(): lax.all_to_all(send_panel, 'front', split_axis=0, concat_axis=0, tiled=True)  24.8 us
    pallas_call x2, Pallas kernels, add_rows(): pl.pallas_call(functools.partial(_block_add_kernel, col0), out_shape=jax....  24.1 us
    dot_general x1, matrix products, local(): schur_part = local_rows[:, PB:] - jnp.dot(solved, window.T, precision=FAST)  18.3 us
    ppermute x2, waiting for transfers between devices, broadcast_from(): got = lax.ppermute(half, axis, pairs(size, bit))  17.5 us
    dot_general x1, matrix products, local(): solved = jnp.dot(panel_part, factor_inverse.T, precision=FAST)  10.9 us
    dot_general x1, matrix products, local(): window = jnp.dot(window_rows, factor_inverse.T, precision=FAST)  6.46 us
    all_to_all x1, starting transfers between devices, local(): lax.all_to_all(send_trail, 'front', split_axis=0, concat_axis=0, tiled=True)  4.41 us
  transfers between devices with their start and end apart: 7, of which 3 were waited for; matrix products, arithmetic and copies ran while one was open for 27% of the time, Pallas kernels for 23%

profile of v11, /device:TPU:0, one launch (start us, length us, event | category | flops | bytes accessed | tf_op | source)
XLA Modules:
  0.0 178.8 jit_solution(11326875286175357573)
XLA Ops:
  0.6 0.9 convert_reduce_fusion
  1.5 0.7 fusion.10
  2.2 0.7 convert_bitcast_fusion
  2.9 0.1 copy.27
  3.0 0.9 slice.63
  4.0 0.7 scatter_fusion
  4.6 24.8 %all_to_all.10 = f32[8,2,16,640]{3,2,1,0:T(8,128)S(1)} all-to-all(f32[8,2,16,640]{3,2,1,0:T(8,128)S(1)} %bitcast.41), channel_id=1, replica_groups=mesh['front'=8,'grp'=4] {'front'}, dimensions={0} | all-to-all | bytes 1310720 | tf_op jit(solution)/shard_map/all_to_all | solution.py:192
  29.4 0.4 fusion.8
  29.8 0.7 convert_element_type.24.idx_ref
  30.4 0.9 slice.65
  31.3 9.9 %shard_map.68 = f32[4096,512]{1,0:T(8,128)} custom-call(s32[256]{0:T(256)} %convert_element_type.24.idx_ref, f32[4096,1408]{1,0:T(8,128)} %bitcast.38, f32[256,512]{1,0:T(8,128)} %bitcast.42), custom_call_target="tpu_custom_call" | custom-call | tf_op jit(solution)/shard_map/pallas_call | solution.py:143
  41.2 2.9 %slice.70 = f32[896,512]{1,0:T(8,128)} slice(f32[4096,512]{1,0:T(8,128)} %shard_map.68), slice={[512:1408], [0:512]} | slice | bytes 3670016 | tf_op jit(solution)/shard_map/slice | solution.py:203
  44.0 0.0 slice-start
  44.0 0.0 collective-permute-start.3
  44.0 1.2 slice-done
  45.3 0.3 copy.26
  45.6 0.1 collective-permute-start
  46.4 3.0 %collective-permute-done = f32[512,512]{0,1:T(8,128)S(1)} collective-permute-done((f32[512,512]{0,1:T(8,128)S(1)}, f32[512,512]{0,1:T(8,128)S(1)}, u32[]{:S(2)}, u32[]{:S(2)}) %collective-permute-start) | collective-permute-done | bytes 1048608 | tf_op jit(solution)/shard_map/ppermute | solution.py:30
  49.3 0.2 broadcast_select_fusion.1
  49.5 0.1 slice_select_fusion.1
  49.6 1.6 collective-permute-start.1
  51.2 0.0 collective-permute-done.3
  51.2 2.5 %broadcast_select_fusion = f32[896,512]{1,0:T(8,128)S(1)} fusion(f32[896,512]{1,0:T(8,128)} %collective-permute-done.3, pred[]{:T(512)S(6)} %eq.17, f32[4096,512]{1,0:T(8,128)} %shard_map.68), kind=kLoop, calls=%fused_computation.14 | loop fusion | flops 458752 | bytes 5505025 | tf_op jit(solution)/shard_map/jit(_where)/select_n | solution.py:31
  53.7 0.0 copy-start.3
  53.7 1.1 slice_select_fusion
  54.8 0.5 collective-permute-start.4
  55.3 9.1 %collective-permute-done.1 = f32[256,512]{0,1:T(8,128)S(1)} collective-permute-done((f32[256,512]{0,1:T(8,128)S(1)}, f32[256,512]{0,1:T(8,128)S(1)}, u32[]{:S(2)}, u32[]{:S(2)}) %collective-permute-start.1) | collective-permute-done | bytes 524320 | tf_op jit(solution)/shard_map/ppermute | solution.py:37
  64.5 0.2 broadcast_select_fusion.3
  64.6 0.1 collective-permute-start.2
  64.7 0.0 copy-done.3
  64.7 1.0 broadcast_in_dim.19
  65.7 2.2 %scatter_fusion.1 = f32[16,16,896]{2,1,0:T(8,128)} fusion(f32[16,16,896]{2,1,0:T(8,128)} %broadcast_in_dim.19, s32[4]{0:T(128)S(1)} %fusion.10, f32[4,16,896]{2,1,0:T(8,128)S(1)} %slice.73), kind=kCustom, calls=%fused_computation.1 | custom fusion | bytes 688144 | tf_op jit(solution)/shard_map/scatter | solution.py:19
  67.9 4.4 %all-to-all-start.1 = ((f32[8,2,16,896]{3,2,1,0:T(8,128)}), f32[8,2,16,896]{3,2,1,0:T(8,128)}, u32[]{:S(2)}, u32[]{:S(2)}) async-start(f32[8,2,16,896]{3,2,1,0:T(8,128)} %bitcast.13), calls=%async_computation.1 | async-start | bytes 1835008 | tf_op jit(solution)/shard_map/all_to_all | solution.py:197
  72.3 0.0 collective-permute-done.2
  72.3 1.4 maximum_select_fusion.2
  73.7 1.3 copy.25
  75.0 0.0 copy-start.1
  75.0 8.4 %collective-permute-done.4 = f32[448,512]{1,0:T(8,128)} collective-permute-done((f32[448,512]{1,0:T(8,128)}, f32[448,512]{1,0:T(8,128)}, u32[]{:S(2)}, u32[]{:S(2)}) %collective-permute-start.4) | collective-permute-done | bytes 917536 | tf_op jit(solution)/shard_map/ppermute | solution.py:37
  83.4 1.3 broadcast_select_fusion.2
  84.7 0.0 collective-permute-start.5
  84.7 0.0 copy-done.1
  84.7 1.2 fusion.6.s_ref
  85.9 41.4 %shard_map.69 = (f32[512,512]{1,0:T(8,128)}, f32[512,512]{1,0:T(8,128)}) custom-call(f32[512,512]{1,0:T(8,128)} %fusion.6.s_ref), custom_call_target="tpu_custom_call" | custom-call | tf_op jit(solution)/shard_map/pallas_call | solution.py:119
  127.4 0.0 copy-start.2
  127.4 10.9 %fusion.12.solved_ref = f32[4096,512]{1,0:T(8,128)S(1)} fusion(f32[4096,512]{1,0:T(8,128)} %shard_map.68, f32[512,512]{1,0:T(8,128)} %get-tuple-element.17), kind=kOutput, calls=%fused_computation.32 | convolution fusion | flops 6442450944 | bytes 17825792 | tf_op jit(solution)/shard_map/dot_general | solution.py:206
  138.3 0.0 copy-start
  138.3 0.0 collective-permute-done.5
  138.3 0.0 copy-done.2
  138.3 6.5 %fusion = f32[896,512]{1,0:T(8,128)S(1)} fusion(f32[512,512]{1,0:T(8,128)S(1)} %copy-done.2, f32[448,512]{1,0:T(8,128)} %collective-permute-done.5, f32[448,512]{1,0:T(8,128)} %broadcast_select_fusion.2, pred[]{:T(512)S(6)} %eq.34), kind=kOutput, calls=%fused_computation.4 | convolution fusion | flops 1410662400 | bytes 4718593 | tf_op jit(solution)/shard_map/dot_general | solution.py:207
  144.8 0.0 copy-done
  144.8 18.3 %slice_subtract_fusion.base_ref = f32[4096,896]{1,0:T(8,128)} fusion(f32[4096,1408]{1,0:T(8,128)} %bitcast.39, f32[4096,512]{1,0:T(8,128)S(1)} %fusion.12.solved_ref, f32[896,512]{1,0:T(8,128)S(1)} %fusion), kind=kOutput, calls=%fused_computation.2 | convolution fusion | flops 11277959168 | bytes 39583744 | tf_op jit(solution)/shard_map/dot_general | solution.py:208
  163.1 0.0 all-to-all-done.1
  163.1 14.2 %shard_map.71 = f32[4096,896]{1,0:T(8,128)} custom-call(s32[256]{0:T(256)} %convert_element_type.24.idx_ref, f32[4096,896]{1,0:T(8,128)} %slice_subtract_fusion.base_ref, f32[256,896]{1,0:T(8,128)} %bitcast.14.add_ref), custom_call_target="tpu_custom_call" | custom-call | tf_op jit(solution)/shard_map/pallas_call | solution.py:143
  177.4 1.2 shard_map.70
  (3 shorter events, 0.1 us)
Async XLA Ops:
  44.0 1.2 slice-start
  44.0 7.2 %collective-permute-start.3 = (f32[896,512]{1,0:T(8,128)}, f32[896,512]{1,0:T(8,128)}, u32[]{:S(2)}, u32[]{:S(2)}) collective-permute-start(f32[896,512]{1,0:T(8,128)} %slice.70), channel_id=1, source_target_pairs={{0,1},{1,0},{2,3},{3,2},{4,5},{5,4},{6,7},{7,6},{8,9},{9,8},{10,11... | collective-permute-start | bytes 5505032 | tf_op jit(solution)/shard_map/ppermute | solution.py:30
  45.6 3.7 %collective-permute-start = (f32[512,512]{0,1:T(8,128)S(1)}, f32[512,512]{0,1:T(8,128)S(1)}, u32[]{:S(2)}, u32[]{:S(2)}) collective-permute-start(f32[512,512]{0,1:T(8,128)S(1)} %copy.26), channel_id=1, source_target_pairs={{0,1},{1,0},{2,3},{3,2},{4,5},{5,4},{6,7},{7,6},{8,9},{9,8},{10,11... | collective-permute-start | bytes 3145736 | tf_op jit(solution)/shard_map/ppermute | solution.py:30
  49.6 14.8 %collective-permute-start.1 = (f32[256,512]{0,1:T(8,128)S(1)}, f32[256,512]{0,1:T(8,128)S(1)}, u32[]{:S(2)}, u32[]{:S(2)}) collective-permute-start(f32[256,512]{0,1:T(8,128)S(1)} %slice_select_fusion.1), channel_id=1, source_target_pairs={{0,2},{1,3},{2,0},{3,1},{4,6},{5,7},{6,4},{7,5},{8,10},{9,11},{10,... | collective-permute-start | bytes 1572872 | tf_op jit(solution)/shard_map/ppermute | solution.py:37
  53.7 11.0 %copy-start.3 = (f32[1,1,4,16,1408]{4,3,2,1,0:T(8,128)S(1)}, f32[1,1,4,16,1408]{4,3,2,1,0:T(8,128)}, u32[]{:S(2)}) copy-start(f32[1,1,4,16,1408]{4,3,2,1,0:T(8,128)} %param.8) | copy-start | bytes 1081348
  54.8 28.6 %collective-permute-start.4 = (f32[448,512]{1,0:T(8,128)}, f32[448,512]{1,0:T(8,128)}, u32[]{:S(2)}, u32[]{:S(2)}) collective-permute-start(f32[448,512]{1,0:T(8,128)} %slice_select_fusion), channel_id=1, source_target_pairs={{0,2},{1,3},{2,0},{3,1},{4,6},{5,7},{6,4},{7,5},{8,10},{9,11},{10,... | collective-permute-start | bytes 2752520 | tf_op jit(solution)/shard_map/ppermute | solution.py:37
  64.6 7.7 %collective-permute-start.2 = (f32[256,512]{0,1:T(8,128)S(1)}, f32[256,512]{0,1:T(8,128)}, u32[]{:S(2)}, u32[]{:S(2)}) collective-permute-start(f32[256,512]{0,1:T(8,128)S(1)} %broadcast_select_fusion.3), channel_id=1, source_target_pairs={{0,1},{1,0},{2,3},{3,2},{4,5},{5,4},{6,7},{7,6},{8,9},{9,8},{10,11... | collective-permute-start | bytes 1572872 | tf_op jit(solution)/shard_map/ppermute | solution.py:40
  67.9 95.2 %all-to-all-start.1 = ((f32[8,2,16,896]{3,2,1,0:T(8,128)}), f32[8,2,16,896]{3,2,1,0:T(8,128)}, u32[]{:S(2)}, u32[]{:S(2)}) async-start(f32[8,2,16,896]{3,2,1,0:T(8,128)} %bitcast.13), calls=%async_computation.1 | async-start | bytes 1835008 | tf_op jit(solution)/shard_map/all_to_all | solution.py:197
  75.0 9.7 %copy-start.1 = (f32[512,512]{1,0:T(8,128)S(1)}, f32[512,512]{1,0:T(8,128)}, u32[]{:S(2)}) copy-start(f32[512,512]{1,0:T(8,128)} %copy.25) | copy-start | bytes 3145732
  84.7 53.6 %collective-permute-start.5 = (f32[448,512]{1,0:T(8,128)}, f32[448,512]{1,0:T(8,128)}, u32[]{:S(2)}, u32[]{:S(2)}) collective-permute-start(f32[448,512]{1,0:T(8,128)} %broadcast_select_fusion.2), channel_id=1, source_target_pairs={{0,1},{1,0},{2,3},{3,2},{4,5},{5,4},{6,7},{7,6},{8,9},{9,8},{10,11... | collective-permute-start | bytes 2752520 | tf_op jit(solution)/shard_map/ppermute | solution.py:40
  127.4 11.0 %copy-start.2 = (f32[512,512]{1,0:T(8,128)S(1)}, f32[512,512]{1,0:T(8,128)}, u32[]{:S(2)}) copy-start(f32[512,512]{1,0:T(8,128)} %get-tuple-element.17) | copy-start | bytes 3145732
  138.3 6.5 %copy-start = (f32[4096,512]{1,0:T(8,128)}, f32[4096,512]{1,0:T(8,128)S(1)}, u32[]{:S(2)}) copy-start(f32[4096,512]{1,0:T(8,128)S(1)} %fusion.12.solved_ref) | copy-start | bytes 25165828

commit v12 on v11

--- a/solution.py
+++ b/solution.py
@@ -43,6 +43,17 @@
         jnp.concatenate([half, other], axis=0),
         jnp.concatenate([other, half], axis=0),
     )
+
+
+def broadcast_whole(x, owner, axis):
+    size = lax.axis_size(axis)
+    me = lax.axis_index(axis)
+    bit = 1
+    while bit < size:
+        got = lax.ppermute(x, axis, pairs(size, bit))
+        x = jnp.where(me // bit == owner // bit, x, got)
+        bit *= 2
+    return x
 
 
 def _mm(a, b):
@@ -200,7 +211,7 @@
     is_owner = lax.axis_index("grp") == owner_index
 
     pivot_block = broadcast_from(panel_part[:PB], owner_index, "grp")
-    window_rows = broadcast_from(panel_part[PB:PB + win_cols], owner_index, "grp")
+    window_rows = broadcast_whole(panel_part[PB:PB + win_cols], owner_index, "grp")
     symmetric = 0.5 * (pivot_block + pivot_block.T)
     pivot_factor, factor_inverse = factor_and_inverse(symmetric)
     solved = jnp.dot(panel_part, factor_inverse.T, precision=FAST)

time: 181 us -> 172 us (0.950); the launches traced: 179 us -> 172 us
  waiting for transfers between devices: 20.5 us -> 12.7 us
    ppermute x2 -> x1, waiting for transfers between devices: 17.5 us -> 10.3 us  [broadcast_from(): got = lax.ppermute(half, axis, pairs(size, bit))]
    select_n x2 -> x1, other arithmetic: 2.68 us -> 0.21 us  [broadcast_from(): x = jnp.where(me == owner, x, got)]
    select_n x0 -> x1, other arithmetic: none -> 2.47 us  [broadcast_whole(): x = jnp.where(me // bit == owner // bit, x, got)]
  transfers between devices with their start and end apart: 7 -> 6, of which waited for: 3 -> 2; matrix products, arithmetic and copies ran while one was open for 27% -> 29% of each run, Pallas kernels for 23% -> 24%
where the time goes in v12:
time: 172 us
  Pallas kernels  66.8 us (39%)
  matrix products  35.2 us (20%)
  blocking collectives  24.8 us (14%)
  local copies, waits for them, and re-layouts  13.2 us (8%)
  waiting for transfers between devices  12.7 us (7%)
  other arithmetic  10.3 us (6%)
  starting transfers between devices  7.2 us (4%)
    pallas_call x1, Pallas kernels, factor_and_inverse(): pl.pallas_call(_factor_kernel, out_shape=(jax.ShapeDtypeStruct((n, n), jn...  41.4 us
    all_to_all x1, blocking collectives, local(): lax.all_to_all(send_panel, 'front', split_axis=0, concat_axis=0, tiled=True)  24.8 us
    pallas_call x2, Pallas kernels, add_rows(): pl.pallas_call(functools.partial(_block_add_kernel, col0), out_shape=jax....  24.1 us
    dot_general x1, matrix products, local(): schur_part = local_rows[:, PB:] - jnp.dot(solved, window.T, precision=FAST)  18.5 us
    dot_general x1, matrix products, local(): solved = jnp.dot(panel_part, factor_inverse.T, precision=FAST)  10.8 us
    ppermute x1, waiting for transfers between devices, broadcast_from(): got = lax.ppermute(half, axis, pairs(size, bit))  10.3 us
    dot_general x1, matrix products, local(): window = jnp.dot(window_rows, factor_inverse.T, precision=FAST)  5.79 us
    all_to_all x1, starting transfers between devices, local(): lax.all_to_all(send_trail, 'front', split_axis=0, concat_axis=0, tiled=True)  4.4 us
  transfers between devices with their start and end apart: 6, of which 2 were waited for; matrix products, arithmetic and copies ran while one was open for 29% of the time, Pallas kernels for 24%

profile of v12, /device:TPU:0, one launch (start us, length us, event | category | flops | bytes accessed | tf_op | source)
XLA Modules:
  0.0 171.7 jit_solution(8720670056829847902)
XLA Ops:
  0.6 0.9 convert_reduce_fusion
  1.5 0.7 fusion.6
  2.2 0.7 convert_bitcast_fusion
  2.9 0.1 copy.27
  3.0 0.9 slice.55
  4.0 0.7 scatter_fusion
  4.6 24.8 %all_to_all.10 = f32[8,2,16,640]{3,2,1,0:T(8,128)S(1)} all-to-all(f32[8,2,16,640]{3,2,1,0:T(8,128)S(1)} %bitcast.41), channel_id=1, replica_groups=mesh['front'=8,'grp'=4] {'front'}, dimensions={0} | all-to-all | bytes 1310720 | tf_op jit(solution)/shard_map/all_to_all | solution.py:203
  29.4 0.4 fusion.4
  29.8 0.7 convert_element_type.24.idx_ref
  30.4 0.9 slice.57
  31.3 9.9 %shard_map.68 = f32[4096,512]{1,0:T(8,128)} custom-call(s32[256]{0:T(256)} %convert_element_type.24.idx_ref, f32[4096,1408]{1,0:T(8,128)} %bitcast.38, f32[256,512]{1,0:T(8,128)} %bitcast.42), custom_call_target="tpu_custom_call" | custom-call | tf_op jit(solution)/shard_map/pallas_call | solution.py:154
  41.2 2.9 %slice.62 = f32[896,512]{1,0:T(8,128)} slice(f32[4096,512]{1,0:T(8,128)} %shard_map.68), slice={[512:1408], [0:512]} | slice | bytes 3670016 | tf_op jit(solution)/shard_map/slice | solution.py:214
  44.0 0.0 collective-permute-start.3
  44.0 1.3 slice.58
  45.3 0.3 copy.26
  45.7 0.6 collective-permute-start
  46.9 2.4 %collective-permute-done = f32[512,512]{0,1:T(8,128)S(1)} collective-permute-done((f32[512,512]{0,1:T(8,128)S(1)}, f32[512,512]{0,1:T(8,128)S(1)}, u32[]{:S(2)}, u32[]{:S(2)}) %collective-permute-start) | collective-permute-done | bytes 1048608 | tf_op jit(solution)/shard_map/ppermute | solution.py:30
  49.3 0.2 broadcast_select_fusion.1
  49.5 0.1 slice_select_fusion
  49.6 1.6 collective-permute-start.1
  51.2 0.0 collective-permute-done.3
  51.2 2.5 %broadcast_select_fusion = f32[896,512]{1,0:T(8,128)S(1)} fusion(f32[896,512]{1,0:T(8,128)} %collective-permute-done.3, pred[]{:T(512)S(6)} %eq.30, f32[4096,512]{1,0:T(8,128)} %shard_map.68), kind=kLoop, calls=%fused_computation.8 | loop fusion | flops 458752 | bytes 5505025 | tf_op jit(solution)/shard_map/jit(_where)/select_n | solution.py:54
  53.7 0.6 collective-permute-start.4
  54.3 10.3 %collective-permute-done.1 = f32[256,512]{0,1:T(8,128)} collective-permute-done((f32[256,512]{0,1:T(8,128)S(1)}, f32[256,512]{0,1:T(8,128)}, u32[]{:S(2)}, u32[]{:S(2)}) %collective-permute-start.1) | collective-permute-done | bytes 524320 | tf_op jit(solution)/shard_map/ppermute | solution.py:37
  64.6 1.1 broadcast_select_fusion.2
  65.7 0.1 collective-permute-start.2
  65.8 1.0 slice.63
  66.7 1.0 broadcast_in_dim.19
  67.7 2.2 %scatter_fusion.1 = f32[16,16,896]{2,1,0:T(8,128)} fusion(f32[16,16,896]{2,1,0:T(8,128)} %broadcast_in_dim.19, s32[4]{0:T(128)S(1)} %fusion.6, f32[4,16,896]{2,1,0:T(8,128)S(1)} %slice.63), kind=kCustom, calls=%fused_computation.1 | custom fusion | bytes 688144 | tf_op jit(solution)/shard_map/scatter | solution.py:19
  69.9 4.4 %all-to-all-start.1 = ((f32[8,2,16,896]{3,2,1,0:T(8,128)}), f32[8,2,16,896]{3,2,1,0:T(8,128)}, u32[]{:S(2)}, u32[]{:S(2)}) async-start(f32[8,2,16,896]{3,2,1,0:T(8,128)} %bitcast.13), calls=%async_computation.1 | async-start | bytes 1835008 | tf_op jit(solution)/shard_map/all_to_all | solution.py:208
  74.3 0.0 collective-permute-done.2
  74.3 1.4 maximum_select_fusion
  75.7 1.3 copy.25
  77.0 2.4 %fusion.2.s_ref = f32[512,512]{1,0:T(8,128)} fusion(f32[512,512]{1,0:T(8,128)} %copy.25, f32[512,512]{0,1:T(8,128)S(1)} %maximum_select_fusion), kind=kLoop, calls=%fused_computation.7 | loop fusion | flops 524288 | bytes 3145728 | tf_op jit(solution)/shard_map/mul | solution.py:215
  79.4 41.4 %shard_map.69 = (f32[512,512]{1,0:T(8,128)}, f32[512,512]{1,0:T(8,128)}) custom-call(f32[512,512]{1,0:T(8,128)} %fusion.2.s_ref), custom_call_target="tpu_custom_call" | custom-call | tf_op jit(solution)/shard_map/pallas_call | solution.py:130
  120.8 0.0 copy-start.1
  120.8 10.8 %fusion.7.solved_ref = f32[4096,512]{1,0:T(8,128)S(1)} fusion(f32[4096,512]{1,0:T(8,128)} %shard_map.68, f32[512,512]{1,0:T(8,128)} %get-tuple-element.17), kind=kOutput, calls=%fused_computation.24 | convolution fusion | flops 6442450944 | bytes 17825792 | tf_op jit(solution)/shard_map/dot_general | solution.py:217
  131.7 0.0 copy-start
  131.7 0.0 collective-permute-done.4
  131.7 0.0 copy-done.1
  131.7 5.8 %fusion = f32[896,512]{1,0:T(8,128)} fusion(f32[512,512]{1,0:T(8,128)S(1)} %copy-done.1, f32[896,512]{1,0:T(8,128)S(1)} %broadcast_select_fusion, f32[896,512]{1,0:T(8,128)} %collective-permute-done.4, pred[]{:T(512)S(6)} %eq.32), kind=kOutput, calls=%fused_computation.3 | convolution fusion | flops 1409744896 | bytes 6553601 | tf_op jit(solution)/shard_map/dot_general | solution.py:218
  137.5 0.0 copy-done
  137.5 18.5 %slice_subtract_fusion.base_ref = f32[4096,896]{1,0:T(8,128)} fusion(f32[4096,1408]{1,0:T(8,128)} %bitcast.39, f32[4096,512]{1,0:T(8,128)S(1)} %fusion.7.solved_ref, f32[896,512]{1,0:T(8,128)} %fusion), kind=kOutput, calls=%fused_computation.2 | convolution fusion | flops 11277959168 | bytes 39583744 | tf_op jit(solution)/shard_map/dot_general | solution.py:219
  156.0 0.0 all-to-all-done.1
  156.0 14.2 %shard_map.71 = f32[4096,896]{1,0:T(8,128)} custom-call(s32[256]{0:T(256)} %convert_element_type.24.idx_ref, f32[4096,896]{1,0:T(8,128)} %slice_subtract_fusion.base_ref, f32[256,896]{1,0:T(8,128)} %bitcast.14.add_ref), custom_call_target="tpu_custom_call" | custom-call | tf_op jit(solution)/shard_map/pallas_call | solution.py:154
  170.3 1.2 shard_map.70
  (2 shorter events, 0.1 us)
Async XLA Ops:
  44.0 7.2 %collective-permute-start.3 = (f32[896,512]{1,0:T(8,128)}, f32[896,512]{1,0:T(8,128)}, u32[]{:S(2)}, u32[]{:S(2)}) collective-permute-start(f32[896,512]{1,0:T(8,128)} %slice.62), channel_id=1, source_target_pairs={{0,1},{1,0},{2,3},{3,2},{4,5},{5,4},{6,7},{7,6},{8,9},{9,8},{10,11... | collective-permute-start | bytes 5505032 | tf_op jit(solution)/shard_map/ppermute | solution.py:53
  45.7 3.6 %collective-permute-start = (f32[512,512]{0,1:T(8,128)S(1)}, f32[512,512]{0,1:T(8,128)S(1)}, u32[]{:S(2)}, u32[]{:S(2)}) collective-permute-start(f32[512,512]{0,1:T(8,128)S(1)} %copy.26), channel_id=1, source_target_pairs={{0,1},{1,0},{2,3},{3,2},{4,5},{5,4},{6,7},{7,6},{8,9},{9,8},{10,11... | collective-permute-start | bytes 3145736 | tf_op jit(solution)/shard_map/ppermute | solution.py:30
  49.6 14.9 %collective-permute-start.1 = (f32[256,512]{0,1:T(8,128)S(1)}, f32[256,512]{0,1:T(8,128)}, u32[]{:S(2)}, u32[]{:S(2)}) collective-permute-start(f32[256,512]{0,1:T(8,128)S(1)} %slice_select_fusion), channel_id=1, source_target_pairs={{0,2},{1,3},{2,0},{3,1},{4,6},{5,7},{6,4},{7,5},{8,10},{9,11},{10,... | collective-permute-start | bytes 1572872 | tf_op jit(solution)/shard_map/ppermute | solution.py:37
  53.7 78.0 %collective-permute-start.4 = (f32[896,512]{1,0:T(8,128)S(1)}, f32[896,512]{1,0:T(8,128)}, u32[]{:S(2)}, u32[]{:S(2)}) collective-permute-start(f32[896,512]{1,0:T(8,128)S(1)} %broadcast_select_fusion), channel_id=1, source_target_pairs={{0,2},{1,3},{2,0},{3,1},{4,6},{5,7},{6,4},{7,5},{8,10},{9,11},{10,... | collective-permute-start | bytes 5505032 | tf_op jit(solution)/shard_map/ppermute | solution.py:53
  65.7 8.6 %collective-permute-start.2 = (f32[256,512]{0,1:T(8,128)S(1)}, f32[256,512]{0,1:T(8,128)}, u32[]{:S(2)}, u32[]{:S(2)}) collective-permute-start(f32[256,512]{0,1:T(8,128)S(1)} %broadcast_select_fusion.2), channel_id=1, source_target_pairs={{0,1},{1,0},{2,3},{3,2},{4,5},{5,4},{6,7},{7,6},{8,9},{9,8},{10,11... | collective-permute-start | bytes 1572872 | tf_op jit(solution)/shard_map/ppermute | solution.py:40
  69.9 86.1 %all-to-all-start.1 = ((f32[8,2,16,896]{3,2,1,0:T(8,128)}), f32[8,2,16,896]{3,2,1,0:T(8,128)}, u32[]{:S(2)}, u32[]{:S(2)}) async-start(f32[8,2,16,896]{3,2,1,0:T(8,128)} %bitcast.13), calls=%async_computation.1 | async-start | bytes 1835008 | tf_op jit(solution)/shard_map/all_to_all | solution.py:208
  120.8 10.9 %copy-start.1 = (f32[512,512]{1,0:T(8,128)S(1)}, f32[512,512]{1,0:T(8,128)}, u32[]{:S(2)}) copy-start(f32[512,512]{1,0:T(8,128)} %get-tuple-element.17) | copy-start | bytes 3145732
  131.7 5.8 %copy-start = (f32[4096,512]{1,0:T(8,128)}, f32[4096,512]{1,0:T(8,128)S(1)}, u32[]{:S(2)}) copy-start(f32[4096,512]{1,0:T(8,128)S(1)} %fusion.7.solved_ref) | copy-start | bytes 25165828

commit v13 on v12

--- a/solution.py
+++ b/solution.py
@@ -137,23 +137,28 @@
 
 
 def _block_add_kernel(col0, idx_ref, base_ref, add_ref, out_ref, sem):
-    width = out_ref.shape[1]
-    copy = pltpu.make_async_copy(base_ref.at[:, pl.ds(col0, width)], out_ref, sem)
+    count, width = out_ref.shape
+    copy = pltpu.make_async_copy(base_ref.at[pl.ds(0, count), pl.ds(col0, width)], out_ref, sem)
     copy.start()
     copy.wait()
 
     def accumulate(i, c):
         r = idx_ref[i]
-        out_ref[pl.ds(r, 1), :] = out_ref[pl.ds(r, 1), :] + add_ref[pl.ds(i, 1), :]
+
+        @pl.when(r < count)
+        def _():
+            out_ref[pl.ds(r, 1), :] = out_ref[pl.ds(r, 1), :] + add_ref[pl.ds(i, 1), :]
+
         return c
 
     lax.fori_loop(0, add_ref.shape[0], accumulate, 0)
 
 
-def add_rows(base, col0, width, rows, values):
+def add_rows(base, col0, width, rows, values, count=None):
+    count = base.shape[0] if count is None else count
     return pl.pallas_call(
         functools.partial(_block_add_kernel, col0),
-        out_shape=jax.ShapeDtypeStruct((base.shape[0], width), base.dtype),
+        out_shape=jax.ShapeDtypeStruct((count, width), base.dtype),
         in_specs=[
             pl.BlockSpec(memory_space=pltpu.SMEM),
             pl.BlockSpec(memory_space=pl.ANY),
@@ -210,8 +215,9 @@
     owner_index = panel_owner[0]
     is_owner = lax.axis_index("grp") == owner_index
 
-    pivot_block = broadcast_from(panel_part[:PB], owner_index, "grp")
-    window_rows = broadcast_whole(panel_part[PB:PB + win_cols], owner_index, "grp")
+    top_rows = add_rows(local_rows, 0, PB, flat_rows, got_panel.reshape(-1, PB), count=PB + win_cols)
+    pivot_block = broadcast_whole(top_rows[:PB], owner_index, "grp")
+    window_rows = broadcast_whole(top_rows[PB:], owner_index, "grp")
     symmetric = 0.5 * (pivot_block + pivot_block.T)
     pivot_factor, factor_inverse = factor_and_inverse(symmetric)
     solved = jnp.dot(panel_part, factor_inverse.T, precision=FAST)

time: 172 us -> 175 us (1.017)
  Pallas kernels: 66.8 us -> 78.8 us
  waiting for transfers between devices: 12.7 us -> 5.16 us
    ppermute x3 -> x0, waiting for transfers between devices: 12.7 us -> none  [the longest x1 10.3 us: broadcast_from(): got = lax.ppermute(half, axis, pairs(size, bit))]
    pallas_call x2 -> x3, Pallas kernels: 24.1 us -> 36.1 us  [add_rows(): pl.pallas_call(functools.partial(_block_add_kernel, col0), out_shape=jax....]
    ppermute x2 -> x4, waiting for transfers between devices: 0.01 us -> 5.16 us  [broadcast_whole(): got = lax.ppermute(x, axis, pairs(size, bit))]
    select_n x1 -> x3, other arithmetic: 2.47 us -> 6.98 us  [broadcast_whole(): x = jnp.where(me // bit == owner // bit, x, got)]
    select_n x4 -> x0, other arithmetic: 2.78 us -> none  [the longest x1 1.36 us: broadcast_from(): jnp.where(core == 0, jnp.concatenate([half, other], axis=0), jnp.concaten...]
    ppermute x3 -> x0, starting transfers between devices: 2.23 us -> none  [the longest x1 1.58 us: broadcast_from(): got = lax.ppermute(half, axis, pairs(size, bit))]
    unnamed x6 -> x12, local copies, waits for them, and re-layouts: 0.44 us -> 2.41 us
    ppermute x2 -> x4, starting transfers between devices: 0.57 us -> 2.54 us  [broadcast_whole(): got = lax.ppermute(x, axis, pairs(size, bit))]
  transfers between devices with their start and end apart: 6 -> 5, of which waited for: 2 -> 2; matrix products, arithmetic and copies ran while one was open for 29% -> 27% of each run, Pallas kernels for 24% -> 31%
where the time goes in v13:
time: 175 us; the launch traced here: 174 us
  Pallas kernels  78.8 us (45%)
  matrix products  33.9 us (19%)
  blocking collectives  24.8 us (14%)
  local copies, waits for them, and re-layouts  12.1 us (7%)
  other arithmetic  10.8 us (6%)
  starting transfers between devices  6.27 us (4%)
  waiting for transfers between devices  5.16 us (3%)
  between operations  1.89 us (1%)
    pallas_call x1, Pallas kernels, factor_and_inverse(): pl.pallas_call(_factor_kernel, out_shape=(jax.ShapeDtypeStruct((n, n), jn...  41.4 us
    pallas_call x3, Pallas kernels, add_rows(): pl.pallas_call(functools.partial(_block_add_kernel, col0), out_shape=jax....  36.1 us
    all_to_all x1, blocking collectives, local(): lax.all_to_all(send_panel, 'front', split_axis=0, concat_axis=0, tiled=True)  24.8 us
    dot_general x1, matrix products, local(): schur_part = local_rows[:, PB:] - jnp.dot(solved, window.T, precision=FAST)  18.3 us
    dot_general x1, matrix products, local(): solved = jnp.dot(panel_part, factor_inverse.T, precision=FAST)  10.9 us
    select_n x3, other arithmetic, broadcast_whole(): x = jnp.where(me // bit == owner // bit, x, got)  6.98 us
    ppermute x4, waiting for transfers between devices, broadcast_whole(): got = lax.ppermute(x, axis, pairs(size, bit))  5.16 us
    dot_general x1, matrix products, local(): window = jnp.dot(window_rows, factor_inverse.T, precision=FAST)  4.59 us
  transfers between devices with their start and end apart: 5, of which 2 were waited for; matrix products, arithmetic and copies ran while one was open for 27% of the time, Pallas kernels for 31%

profile of v13, /device:TPU:0, one launch (start us, length us, event | category | flops | bytes accessed | tf_op | source)
XLA Modules:
  0.0 173.6 jit_solution(12601213704153418689)
XLA Ops:
  0.6 0.9 convert_reduce_fusion
  1.5 0.7 fusion.6
  2.2 0.7 convert_bitcast_fusion
  2.9 0.1 copy.27
  3.0 0.9 slice.47
  4.0 0.7 scatter_fusion
  4.6 24.8 %all_to_all.10 = f32[8,2,16,640]{3,2,1,0:T(8,128)S(1)} all-to-all(f32[8,2,16,640]{3,2,1,0:T(8,128)S(1)} %bitcast.45), channel_id=1, replica_groups=mesh['front'=8,'grp'=4] {'front'}, dimensions={0} | all-to-all | bytes 1310720 | tf_op jit(solution)/shard_map/all_to_all | solution.py:208
  29.4 0.4 fusion.4
  29.8 0.7 convert_element_type.24.idx_ref
  30.5 0.9 slice.49
  31.3 8.1 %shard_map.68 = f32[1408,512]{1,0:T(8,128)} custom-call(s32[256]{0:T(256)} %convert_element_type.24.idx_ref, f32[4096,1408]{1,0:T(8,128)} %bitcast.37, f32[256,512]{1,0:T(8,128)} %bitcast.42), custom_call_target="tpu_custom_call" | custom-call | tf_op jit(solution)/shard_map/pallas_call | solution.py:159
  39.5 0.0 slice-start
  39.5 3.0 %slice.52 = f32[896,512]{1,0:T(8,128)} slice(f32[1408,512]{1,0:T(8,128)} %shard_map.68), slice={[512:1408], [0:512]} | slice | bytes 3670016 | tf_op jit(solution)/shard_map/slice | solution.py:220
  42.4 0.0 collective-permute-start.2
  42.4 0.0 slice-done
  42.4 1.3 copy.26
  43.7 0.0 copy-start.1
  43.7 0.5 collective-permute-start
  45.2 2.9 %collective-permute-done = f32[512,512]{0,1:T(8,128)} collective-permute-done((f32[512,512]{0,1:T(8,128)}, f32[512,512]{0,1:T(8,128)}, u32[]{:S(2)}, u32[]{:S(2)}) %collective-permute-start) | collective-permute-done | bytes 1048608 | tf_op jit(solution)/shard_map/ppermute | solution.py:53
  48.1 2.4 %broadcast_select_fusion.1 = f32[512,512]{0,1:T(8,128)} fusion(f32[512,512]{0,1:T(8,128)} %copy.26, f32[512,512]{0,1:T(8,128)} %collective-permute-done, pred[]{:T(512)S(6)} %eq.24), kind=kLoop, calls=%fused_computation.9 | loop fusion | flops 262144 | bytes 3145729 | tf_op jit(solution)/shard_map/jit(_where)/select_n | solution.py:54
  50.5 0.0 copy-start.4
  50.5 1.6 collective-permute-start.1
  52.0 0.0 collective-permute-done.2
  52.0 0.0 copy-done.1
  52.0 3.1 %broadcast_select_fusion = f32[896,512]{1,0:T(8,128)} fusion(f32[896,512]{1,0:T(8,128)} %collective-permute-done.2, pred[]{:T(512)S(6)} %eq.24, f32[1408,512]{1,0:T(8,128)S(1)} %copy-done.1), kind=kLoop, calls=%fused_computation.7 | loop fusion | flops 458752 | bytes 5505025 | tf_op jit(solution)/shard_map/jit(_where)/select_n | solution.py:54
  55.2 0.4 collective-permute-start.3
  55.6 0.0 copy-done.4
  55.7 1.0 broadcast_in_dim.19
  56.7 2.2 %scatter_fusion.1 = f32[16,16,896]{2,1,0:T(8,128)} fusion(f32[16,16,896]{2,1,0:T(8,128)} %broadcast_in_dim.19, s32[4]{0:T(128)S(1)} %fusion.6, f32[4,16,896]{2,1,0:T(8,128)S(1)} %slice.53), kind=kCustom, calls=%fused_computation.1 | custom fusion | bytes 688144 | tf_op jit(solution)/shard_map/scatter | solution.py:19
  58.9 3.7 %all-to-all-start.1 = ((f32[8,2,16,896]{3,2,1,0:T(8,128)}), f32[8,2,16,896]{3,2,1,0:T(8,128)S(1)}, u32[]{:S(2)}, u32[]{:S(2)}) async-start(f32[8,2,16,896]{3,2,1,0:T(8,128)} %bitcast.13), calls=%async_computation.1 | async-start | bytes 1835008 | tf_op jit(solution)/shard_map/all_to_all | solution.py:213
  62.7 11.9 %shard_map.70 = f32[4096,512]{1,0:T(8,128)} custom-call(s32[256]{0:T(256)} %convert_element_type.24.idx_ref, f32[4096,1408]{1,0:T(8,128)} %bitcast.38, f32[256,512]{1,0:T(8,128)} %bitcast.43), custom_call_target="tpu_custom_call" | custom-call | tf_op jit(solution)/shard_map/pallas_call | solution.py:159
  74.5 2.3 %collective-permute-done.1 = f32[512,512]{0,1:T(8,128)} collective-permute-done((f32[512,512]{0,1:T(8,128)}, f32[512,512]{0,1:T(8,128)}, u32[]{:S(2)}, u32[]{:S(2)}) %collective-permute-start.1) | collective-permute-done | bytes 1048608 | tf_op jit(solution)/shard_map/ppermute | solution.py:53
  76.8 1.4 broadcast_select_fusion.2
  78.2 0.3 copy.25
  78.6 1.2 fusion.2.s_ref
  79.8 41.4 %shard_map.69 = (f32[512,512]{1,0:T(8,128)}, f32[512,512]{1,0:T(8,128)}) custom-call(f32[512,512]{1,0:T(8,128)} %fusion.2.s_ref), custom_call_target="tpu_custom_call" | custom-call | tf_op jit(solution)/shard_map/pallas_call | solution.py:130
  121.2 0.0 copy-start.2
  121.2 10.9 %fusion.7.solved_ref = f32[4096,512]{1,0:T(8,128)S(1)} fusion(f32[4096,512]{1,0:T(8,128)} %shard_map.70, f32[512,512]{1,0:T(8,128)} %get-tuple-element.17), kind=kOutput, calls=%fused_computation.22 | convolution fusion | flops 6442450944 | bytes 17825792 | tf_op jit(solution)/shard_map/dot_general | solution.py:223
  132.1 0.0 copy-start
  132.1 0.0 collective-permute-done.3
  132.1 0.0 copy-done.2
  132.2 4.6 %fusion = f32[896,512]{1,0:T(8,128)S(1)} fusion(f32[512,512]{1,0:T(8,128)S(1)} %copy-done.2, f32[896,512]{1,0:T(8,128)} %broadcast_select_fusion, f32[896,512]{1,0:T(8,128)} %collective-permute-done.3, pred[]{:T(512)S(6)} %eq.25), kind=kOutput, calls=%fused_computation.3 | convolution fusion | flops 1409744896 | bytes 6553601 | tf_op jit(solution)/shard_map/dot_general | solution.py:224
  136.8 0.0 copy-done
  136.8 18.3 %slice_subtract_fusion.base_ref = f32[4096,896]{1,0:T(8,128)} fusion(f32[4096,1408]{1,0:T(8,128)} %bitcast.39, f32[4096,512]{1,0:T(8,128)S(1)} %fusion.7.solved_ref, f32[896,512]{1,0:T(8,128)S(1)} %fusion), kind=kOutput, calls=%fused_computation.2 | convolution fusion | flops 11277959168 | bytes 39583744 | tf_op jit(solution)/shard_map/dot_general | solution.py:225
  155.1 0.0 all-to-all-done.1
  155.1 0.0 copy-start.3
  155.1 1.0 copy-done.3
  156.1 16.1 %shard_map.72 = f32[4096,896]{1,0:T(8,128)} custom-call(s32[256]{0:T(256)} %convert_element_type.24.idx_ref, f32[4096,896]{1,0:T(8,128)} %slice_subtract_fusion.base_ref, f32[256,896]{1,0:T(8,128)} %bitcast.44), custom_call_target="tpu_custom_call" | custom-call | tf_op jit(solution)/shard_map/pallas_call | solution.py:159
  172.2 1.2 shard_map.71
  (3 shorter events, 0.1 us)
Async XLA Ops:
  39.5 3.0 %slice-start = ((f32[1408,512]{1,0:T(8,128)}), f32[512,512]{1,0:T(8,128)S(1)}, s32[]{:S(2)}) async-start(f32[1408,512]{1,0:T(8,128)} %shard_map.68), calls=%async_computation.2 | async-start | bytes 2097152 | tf_op jit(solution)/shard_map/slice | solution.py:219
  42.4 9.6 %collective-permute-start.2 = (f32[896,512]{1,0:T(8,128)}, f32[896,512]{1,0:T(8,128)}, u32[]{:S(2)}, u32[]{:S(2)}) collective-permute-start(f32[896,512]{1,0:T(8,128)} %slice.52), channel_id=1, source_target_pairs={{0,1},{1,0},{2,3},{3,2},{4,5},{5,4},{6,7},{7,6},{8,9},{9,8},{10,11... | collective-permute-start | bytes 5505032 | tf_op jit(solution)/shard_map/ppermute | solution.py:53
  43.7 8.3 %copy-start.1 = (f32[1408,512]{1,0:T(8,128)S(1)}, f32[1408,512]{1,0:T(8,128)}, u32[]{:S(2)}) copy-start(f32[1408,512]{1,0:T(8,128)} %shard_map.68) | copy-start | bytes 8650756
  43.7 4.3 %collective-permute-start = (f32[512,512]{0,1:T(8,128)}, f32[512,512]{0,1:T(8,128)}, u32[]{:S(2)}, u32[]{:S(2)}) collective-permute-start(f32[512,512]{0,1:T(8,128)} %copy.26), channel_id=1, source_target_pairs={{0,1},{1,0},{2,3},{3,2},{4,5},{5,4},{6,7},{7,6},{8,9},{9,8},{10,11... | collective-permute-start | bytes 3145736 | tf_op jit(solution)/shard_map/ppermute | solution.py:53
  50.5 5.2 %copy-start.4 = (f32[1,1,4,16,1408]{4,3,2,1,0:T(8,128)S(1)}, f32[1,1,4,16,1408]{4,3,2,1,0:T(8,128)}, u32[]{:S(2)}) copy-start(f32[1,1,4,16,1408]{4,3,2,1,0:T(8,128)} %param.8) | copy-start | bytes 1081348
  50.5 26.3 %collective-permute-start.1 = (f32[512,512]{0,1:T(8,128)}, f32[512,512]{0,1:T(8,128)}, u32[]{:S(2)}, u32[]{:S(2)}) collective-permute-start(f32[512,512]{0,1:T(8,128)} %broadcast_select_fusion.1), channel_id=1, source_target_pairs={{0,2},{1,3},{2,0},{3,1},{4,6},{5,7},{6,4},{7,5},{8,10},{9,11},{10,... | collective-permute-start | bytes 3145736 | tf_op jit(solution)/shard_map/ppermute | solution.py:53
  55.2 77.0 %collective-permute-start.3 = (f32[896,512]{1,0:T(8,128)}, f32[896,512]{1,0:T(8,128)}, u32[]{:S(2)}, u32[]{:S(2)}) collective-permute-start(f32[896,512]{1,0:T(8,128)} %broadcast_select_fusion), channel_id=1, source_target_pairs={{0,2},{1,3},{2,0},{3,1},{4,6},{5,7},{6,4},{7,5},{8,10},{9,11},{10,... | collective-permute-start | bytes 5505032 | tf_op jit(solution)/shard_map/ppermute | solution.py:53
  58.9 96.2 %all-to-all-start.1 = ((f32[8,2,16,896]{3,2,1,0:T(8,128)}), f32[8,2,16,896]{3,2,1,0:T(8,128)S(1)}, u32[]{:S(2)}, u32[]{:S(2)}) async-start(f32[8,2,16,896]{3,2,1,0:T(8,128)} %bitcast.13), calls=%async_computation.1 | async-start | bytes 1835008 | tf_op jit(solution)/shard_map/all_to_all | solution.py:213
  121.2 10.9 %copy-start.2 = (f32[512,512]{1,0:T(8,128)S(1)}, f32[512,512]{1,0:T(8,128)}, u32[]{:S(2)}) copy-start(f32[512,512]{1,0:T(8,128)} %get-tuple-element.17) | copy-start | bytes 3145732
  132.1 4.6 %copy-start = (f32[4096,512]{1,0:T(8,128)}, f32[4096,512]{1,0:T(8,128)S(1)}, u32[]{:S(2)}) copy-start(f32[4096,512]{1,0:T(8,128)S(1)} %fusion.7.solved_ref) | copy-start | bytes 25165828
  155.1 1.0 copy-start.3

commit v14 on v12

--- a/solution.py
+++ b/solution.py
@@ -147,7 +147,7 @@
         out_ref[pl.ds(r, 1), :] = out_ref[pl.ds(r, 1), :] + add_ref[pl.ds(i, 1), :]
         return c
 
-    lax.fori_loop(0, add_ref.shape[0], accumulate, 0)
+    lax.fori_loop(0, add_ref.shape[0], accumulate, 0, unroll=8)
 
 
 def add_rows(base, col0, width, rows, values):

time: 172 us -> 171 us (level)
  matrix products: 35.2 us -> 33 us
    dot_general x1, matrix products: 5.79 us -> 3.64 us  [local(): window = jnp.dot(window_rows, factor_inverse.T, precision=FAST)]
  transfers between devices with their start and end apart: 6 -> 6, of which waited for: 2 -> 2; matrix products, arithmetic and copies ran while one was open for 29% -> 27% of each run, Pallas kernels for 24% -> 24%
where the time goes in v14:
time: 171 us; the launch traced here: 169 us
  Pallas kernels  67.1 us (39%)
  matrix products  33 us (19%)
  blocking collectives  24.8 us (15%)
  local copies, waits for them, and re-layouts  13.5 us (8%)
  waiting for transfers between devices  12.7 us (7%)
  other arithmetic  8.7 us (5%)
  starting transfers between devices  7.76 us (5%)
    pallas_call x1, Pallas kernels, factor_and_inverse(): pl.pallas_call(_factor_kernel, out_shape=(jax.ShapeDtypeStruct((n, n), jn...  41.4 us
    all_to_all x1, blocking collectives, local(): lax.all_to_all(send_panel, 'front', split_axis=0, concat_axis=0, tiled=True)  24.8 us
    pallas_call x2, Pallas kernels, add_rows(): pl.pallas_call(functools.partial(_block_add_kernel, col0), out_shape=jax....  23.5 us
    dot_general x1, matrix products, local(): schur_part = local_rows[:, PB:] - jnp.dot(solved, window.T, precision=FAST)  18.5 us
    dot_general x1, matrix products, local(): solved = jnp.dot(panel_part, factor_inverse.T, precision=FAST)  10.8 us
    ppermute x1, waiting for transfers between devices, broadcast_from(): got = lax.ppermute(half, axis, pairs(size, bit))  10.3 us
    all_to_all x1, starting transfers between devices, local(): lax.all_to_all(send_trail, 'front', split_axis=0, concat_axis=0, tiled=True)  4.4 us
    dot_general x1, matrix products, local(): window = jnp.dot(window_rows, factor_inverse.T, precision=FAST)  3.64 us
  transfers between devices with their start and end apart: 6, of which 2 were waited for; matrix products, arithmetic and copies ran while one was open for 27% of the time, Pallas kernels for 24%

profile of v14, /device:TPU:0, one launch (start us, length us, event | category | flops | bytes accessed | tf_op | source)
XLA Modules:
  0.0 169.2 jit_solution(12119279197403415101)
XLA Ops:
  0.6 0.9 convert_reduce_fusion
  1.5 0.7 fusion.6
  2.2 0.7 convert_bitcast_fusion
  2.9 0.1 copy.27
  3.0 0.9 slice.55
  4.0 0.7 scatter_fusion
  4.6 24.8 %all_to_all.10 = f32[8,2,16,640]{3,2,1,0:T(8,128)S(1)} all-to-all(f32[8,2,16,640]{3,2,1,0:T(8,128)S(1)} %bitcast.41), channel_id=1, replica_groups=mesh['front'=8,'grp'=4] {'front'}, dimensions={0} | all-to-all | bytes 1310720 | tf_op jit(solution)/shard_map/all_to_all | solution.py:203
  29.4 0.4 fusion.4
  29.8 0.7 convert_element_type.24.idx_ref
  30.4 0.9 slice.57
  31.3 9.6 %shard_map.68 = f32[4096,512]{1,0:T(8,128)} custom-call(s32[256]{0:T(256)} %convert_element_type.24.idx_ref, f32[4096,1408]{1,0:T(8,128)} %bitcast.38, f32[256,512]{1,0:T(8,128)} %bitcast.42), custom_call_target="tpu_custom_call" | custom-call | tf_op jit(solution)/shard_map/pallas_call | solution.py:154
  40.9 2.9 %slice.62 = f32[896,512]{1,0:T(8,128)} slice(f32[4096,512]{1,0:T(8,128)} %shard_map.68), slice={[512:1408], [0:512]} | slice | bytes 3670016 | tf_op jit(solution)/shard_map/slice | solution.py:214
  43.8 0.0 collective-permute-start.3
  43.8 1.3 slice.58
  45.1 0.3 copy.26
  45.5 0.6 collective-permute-start
  46.7 2.4 %collective-permute-done = f32[512,512]{0,1:T(8,128)S(1)} collective-permute-done((f32[512,512]{0,1:T(8,128)S(1)}, f32[512,512]{0,1:T(8,128)S(1)}, u32[]{:S(2)}, u32[]{:S(2)}) %collective-permute-start) | collective-permute-done | bytes 1048608 | tf_op jit(solution)/shard_map/ppermute | solution.py:30
  49.1 0.2 broadcast_select_fusion.1
  49.3 0.1 slice_select_fusion
  49.4 1.5 collective-permute-start.1
  50.9 0.0 collective-permute-done.3
  50.9 1.9 %broadcast_select_fusion = f32[896,512]{1,0:T(8,128)S(1)} fusion(f32[896,512]{1,0:T(8,128)} %collective-permute-done.3, pred[]{:T(512)S(6)} %eq.30, f32[4096,512]{1,0:T(8,128)} %shard_map.68), kind=kLoop, calls=%fused_computation.8 | loop fusion | flops 458752 | bytes 5505025 | tf_op jit(solution)/shard_map/jit(_where)/select_n | solution.py:54
  52.8 1.2 collective-permute-start.4
  54.0 10.3 %collective-permute-done.1 = f32[256,512]{0,1:T(8,128)} collective-permute-done((f32[256,512]{0,1:T(8,128)S(1)}, f32[256,512]{0,1:T(8,128)}, u32[]{:S(2)}, u32[]{:S(2)}) %collective-permute-start.1) | collective-permute-done | bytes 524320 | tf_op jit(solution)/shard_map/ppermute | solution.py:37
  64.3 0.1 broadcast_select_fusion.2
  64.4 0.1 collective-permute-start.2
  64.5 1.0 slice.63
  65.5 1.0 broadcast_in_dim.19
  66.5 2.2 %scatter_fusion.1 = f32[16,16,896]{2,1,0:T(8,128)} fusion(f32[16,16,896]{2,1,0:T(8,128)} %broadcast_in_dim.19, s32[4]{0:T(128)S(1)} %fusion.6, f32[4,16,896]{2,1,0:T(8,128)S(1)} %slice.63), kind=kCustom, calls=%fused_computation.1 | custom fusion | bytes 688144 | tf_op jit(solution)/shard_map/scatter | solution.py:19
  68.7 4.4 %all-to-all-start.1 = ((f32[8,2,16,896]{3,2,1,0:T(8,128)}), f32[8,2,16,896]{3,2,1,0:T(8,128)}, u32[]{:S(2)}, u32[]{:S(2)}) async-start(f32[8,2,16,896]{3,2,1,0:T(8,128)} %bitcast.13), calls=%async_computation.1 | async-start | bytes 1835008 | tf_op jit(solution)/shard_map/all_to_all | solution.py:208
  73.1 0.0 collective-permute-done.2
  73.1 1.4 maximum_select_fusion
  74.5 1.3 copy.25
  75.8 2.4 %fusion.2.s_ref = f32[512,512]{1,0:T(8,128)} fusion(f32[512,512]{1,0:T(8,128)} %copy.25, f32[512,512]{0,1:T(8,128)S(1)} %maximum_select_fusion), kind=kLoop, calls=%fused_computation.7 | loop fusion | flops 524288 | bytes 3145728 | tf_op jit(solution)/shard_map/mul | solution.py:215
  78.2 41.4 %shard_map.69 = (f32[512,512]{1,0:T(8,128)}, f32[512,512]{1,0:T(8,128)}) custom-call(f32[512,512]{1,0:T(8,128)} %fusion.2.s_ref), custom_call_target="tpu_custom_call" | custom-call | tf_op jit(solution)/shard_map/pallas_call | solution.py:130
  119.6 0.0 copy-start.1
  119.6 10.8 %fusion.7.solved_ref = f32[4096,512]{1,0:T(8,128)S(1)} fusion(f32[4096,512]{1,0:T(8,128)} %shard_map.68, f32[512,512]{1,0:T(8,128)} %get-tuple-element.17), kind=kOutput, calls=%fused_computation.24 | convolution fusion | flops 6442450944 | bytes 17825792 | tf_op jit(solution)/shard_map/dot_general | solution.py:217
  130.4 0.0 copy-start
  130.5 0.0 collective-permute-done.4
  130.5 0.0 copy-done.1
  130.5 3.6 %fusion = f32[896,512]{1,0:T(8,128)} fusion(f32[512,512]{1,0:T(8,128)S(1)} %copy-done.1, f32[896,512]{1,0:T(8,128)S(1)} %broadcast_select_fusion, f32[896,512]{1,0:T(8,128)} %collective-permute-done.4, pred[]{:T(512)S(6)} %eq.32), kind=kOutput, calls=%fused_computation.3 | convolution fusion | flops 1409744896 | bytes 6553601 | tf_op jit(solution)/shard_map/dot_general | solution.py:218
  134.1 0.3 copy-done
  134.4 18.5 %slice_subtract_fusion.base_ref = f32[4096,896]{1,0:T(8,128)} fusion(f32[4096,1408]{1,0:T(8,128)} %bitcast.39, f32[4096,512]{1,0:T(8,128)S(1)} %fusion.7.solved_ref, f32[896,512]{1,0:T(8,128)} %fusion), kind=kOutput, calls=%fused_computation.2 | convolution fusion | flops 11277959168 | bytes 39583744 | tf_op jit(solution)/shard_map/dot_general | solution.py:219
  152.9 0.0 all-to-all-done.1
  152.9 13.9 %shard_map.71 = f32[4096,896]{1,0:T(8,128)} custom-call(s32[256]{0:T(256)} %convert_element_type.24.idx_ref, f32[4096,896]{1,0:T(8,128)} %slice_subtract_fusion.base_ref, f32[256,896]{1,0:T(8,128)} %bitcast.14.add_ref), custom_call_target="tpu_custom_call" | custom-call | tf_op jit(solution)/shard_map/pallas_call | solution.py:154
  166.8 2.2 %shard_map.70 = f32[4096,512]{1,0:T(8,128)} custom-call(s32[1]{0:T(128)} %bitcast.1.flag_ref, f32[512,512]{1,0:T(8,128)} %get-tuple-element.16.factor_ref, f32[4096,512]{1,0:T(8,128)} %copy-done), custom_call_target="tpu_custom_call", output_to_operand_aliasing={{}: (2, {})} | custom-call | tf_op jit(solution)/shard_map/pallas_call | solution.py:176
  (2 shorter events, 0.1 us)
Async XLA Ops:
  43.8 7.1 %collective-permute-start.3 = (f32[896,512]{1,0:T(8,128)}, f32[896,512]{1,0:T(8,128)}, u32[]{:S(2)}, u32[]{:S(2)}) collective-permute-start(f32[896,512]{1,0:T(8,128)} %slice.62), channel_id=1, source_target_pairs={{0,1},{1,0},{2,3},{3,2},{4,5},{5,4},{6,7},{7,6},{8,9},{9,8},{10,11... | collective-permute-start | bytes 5505032 | tf_op jit(solution)/shard_map/ppermute | solution.py:53
  45.5 3.6 %collective-permute-start = (f32[512,512]{0,1:T(8,128)S(1)}, f32[512,512]{0,1:T(8,128)S(1)}, u32[]{:S(2)}, u32[]{:S(2)}) collective-permute-start(f32[512,512]{0,1:T(8,128)S(1)} %copy.26), channel_id=1, source_target_pairs={{0,1},{1,0},{2,3},{3,2},{4,5},{5,4},{6,7},{7,6},{8,9},{9,8},{10,11... | collective-permute-start | bytes 3145736 | tf_op jit(solution)/shard_map/ppermute | solution.py:30
  49.4 14.9 %collective-permute-start.1 = (f32[256,512]{0,1:T(8,128)S(1)}, f32[256,512]{0,1:T(8,128)}, u32[]{:S(2)}, u32[]{:S(2)}) collective-permute-start(f32[256,512]{0,1:T(8,128)S(1)} %slice_select_fusion), channel_id=1, source_target_pairs={{0,2},{1,3},{2,0},{3,1},{4,6},{5,7},{6,4},{7,5},{8,10},{9,11},{10,... | collective-permute-start | bytes 1572872 | tf_op jit(solution)/shard_map/ppermute | solution.py:37
  52.8 77.6 %collective-permute-start.4 = (f32[896,512]{1,0:T(8,128)S(1)}, f32[896,512]{1,0:T(8,128)}, u32[]{:S(2)}, u32[]{:S(2)}) collective-permute-start(f32[896,512]{1,0:T(8,128)S(1)} %broadcast_select_fusion), channel_id=1, source_target_pairs={{0,2},{1,3},{2,0},{3,1},{4,6},{5,7},{6,4},{7,5},{8,10},{9,11},{10,... | collective-permute-start | bytes 5505032 | tf_op jit(solution)/shard_map/ppermute | solution.py:53
  64.4 8.6 %collective-permute-start.2 = (f32[256,512]{0,1:T(8,128)S(1)}, f32[256,512]{0,1:T(8,128)}, u32[]{:S(2)}, u32[]{:S(2)}) collective-permute-start(f32[256,512]{0,1:T(8,128)S(1)} %broadcast_select_fusion.2), channel_id=1, source_target_pairs={{0,1},{1,0},{2,3},{3,2},{4,5},{5,4},{6,7},{7,6},{8,9},{9,8},{10,11... | collective-permute-start | bytes 1572872 | tf_op jit(solution)/shard_map/ppermute | solution.py:40
  68.7 84.3 %all-to-all-start.1 = ((f32[8,2,16,896]{3,2,1,0:T(8,128)}), f32[8,2,16,896]{3,2,1,0:T(8,128)}, u32[]{:S(2)}, u32[]{:S(2)}) async-start(f32[8,2,16,896]{3,2,1,0:T(8,128)} %bitcast.13), calls=%async_computation.1 | async-start | bytes 1835008 | tf_op jit(solution)/shard_map/all_to_all | solution.py:208
  119.6 10.9 %copy-start.1 = (f32[512,512]{1,0:T(8,128)S(1)}, f32[512,512]{1,0:T(8,128)}, u32[]{:S(2)}) copy-start(f32[512,512]{1,0:T(8,128)} %get-tuple-element.17) | copy-start | bytes 3145732
  130.4 4.0 %copy-start = (f32[4096,512]{1,0:T(8,128)}, f32[4096,512]{1,0:T(8,128)S(1)}, u32[]{:S(2)}) copy-start(f32[4096,512]{1,0:T(8,128)S(1)} %fusion.7.solved_ref) | copy-start | bytes 25165828

commit v15 on v14

--- a/solution.py
+++ b/solution.py
@@ -10,6 +10,7 @@
 PB = 512
 CAP = 2
 BLK = 128
+PARTS = 4
 EXACT = lax.Precision.HIGHEST
 FAST = lax.Precision.HIGH
 
@@ -136,11 +137,19 @@
     )(sym)
 
 
-def _block_add_kernel(col0, idx_ref, base_ref, add_ref, out_ref, sem):
-    width = out_ref.shape[1]
-    copy = pltpu.make_async_copy(base_ref.at[:, pl.ds(col0, width)], out_ref, sem)
-    copy.start()
-    copy.wait()
+def _block_add_kernel(col0, idx_ref, base_ref, add_ref, out_ref, sems):
+    rows, width = out_ref.shape
+    part = rows // PARTS
+    copies = [
+        pltpu.make_async_copy(
+            base_ref.at[pl.ds(p * part, part), pl.ds(col0, width)], out_ref.at[pl.ds(p * part, part)], sems.at[p]
+        )
+        for p in range(PARTS)
+    ]
+    for copy in copies:
+        copy.start()
+    for copy in copies:
+        copy.wait()
 
     def accumulate(i, c):
         r = idx_ref[i]
@@ -160,7 +169,7 @@
             pl.BlockSpec(memory_space=pltpu.VMEM),
         ],
         out_specs=pl.BlockSpec(memory_space=pltpu.VMEM),
-        scratch_shapes=[pltpu.SemaphoreType.DMA(())],
+        scratch_shapes=[pltpu.SemaphoreType.DMA((PARTS,))],
     )(rows, base, values)
 
 

time: 171 us -> 171 us (level)
  no operation moved by 1% of the time
where the time goes in v15:
time: 171 us; the launch traced here: 169 us
  Pallas kernels  67.4 us (39%)
  matrix products  33 us (19%)
  blocking collectives  24.8 us (15%)
  local copies, waits for them, and re-layouts  13.5 us (8%)
  waiting for transfers between devices  12.7 us (7%)
  other arithmetic  8.7 us (5%)
  starting transfers between devices  7.76 us (5%)
    pallas_call x1, Pallas kernels, factor_and_inverse(): pl.pallas_call(_factor_kernel, out_shape=(jax.ShapeDtypeStruct((n, n), jn...  41.4 us
    all_to_all x1, blocking collectives, local(): lax.all_to_all(send_panel, 'front', split_axis=0, concat_axis=0, tiled=True)  24.8 us
    pallas_call x2, Pallas kernels, add_rows(): pl.pallas_call(functools.partial(_block_add_kernel, col0), out_shape=jax....  23.8 us
    dot_general x1, matrix products, local(): schur_part = local_rows[:, PB:] - jnp.dot(solved, window.T, precision=FAST)  18.5 us
    dot_general x1, matrix products, local(): solved = jnp.dot(panel_part, factor_inverse.T, precision=FAST)  10.8 us
    ppermute x1, waiting for transfers between devices, broadcast_from(): got = lax.ppermute(half, axis, pairs(size, bit))  10.3 us
    all_to_all x1, starting transfers between devices, local(): lax.all_to_all(send_trail, 'front', split_axis=0, concat_axis=0, tiled=True)  4.4 us
    dot_general x1, matrix products, local(): window = jnp.dot(window_rows, factor_inverse.T, precision=FAST)  3.64 us
  transfers between devices with their start and end apart: 6, of which 2 were waited for; matrix products, arithmetic and copies ran while one was open for 27% of the time, Pallas kernels for 24%

profile of v15, /device:TPU:0, one launch (start us, length us, event | category | flops | bytes accessed | tf_op | source)
XLA Modules:
  0.0 169.4 jit_solution(1612462473977680865)
XLA Ops:
  0.6 0.9 convert_reduce_fusion
  1.5 0.7 fusion.6
  2.2 0.7 convert_bitcast_fusion
  2.9 0.1 copy.27
  3.0 0.9 slice.55
  4.0 0.7 scatter_fusion
  4.6 24.8 %all_to_all.10 = f32[8,2,16,640]{3,2,1,0:T(8,128)S(1)} all-to-all(f32[8,2,16,640]{3,2,1,0:T(8,128)S(1)} %bitcast.41), channel_id=1, replica_groups=mesh['front'=8,'grp'=4] {'front'}, dimensions={0} | all-to-all | bytes 1310720 | tf_op jit(solution)/shard_map/all_to_all | solution.py:212
  29.4 0.4 fusion.4
  29.8 0.7 convert_element_type.24.idx_ref
  30.4 0.9 slice.57
  31.3 9.7 %shard_map.68 = f32[4096,512]{1,0:T(8,128)} custom-call(s32[256]{0:T(256)} %convert_element_type.24.idx_ref, f32[4096,1408]{1,0:T(8,128)} %bitcast.38, f32[256,512]{1,0:T(8,128)} %bitcast.42), custom_call_target="tpu_custom_call" | custom-call | tf_op jit(solution)/shard_map/pallas_call | solution.py:163
  41.0 2.9 %slice.62 = f32[896,512]{1,0:T(8,128)} slice(f32[4096,512]{1,0:T(8,128)} %shard_map.68), slice={[512:1408], [0:512]} | slice | bytes 3670016 | tf_op jit(solution)/shard_map/slice | solution.py:223
  43.9 0.0 collective-permute-start.3
  43.9 1.3 slice.58
  45.2 0.3 copy.26
  45.5 0.6 collective-permute-start
  46.8 2.4 %collective-permute-done = f32[512,512]{0,1:T(8,128)S(1)} collective-permute-done((f32[512,512]{0,1:T(8,128)S(1)}, f32[512,512]{0,1:T(8,128)S(1)}, u32[]{:S(2)}, u32[]{:S(2)}) %collective-permute-start) | collective-permute-done | bytes 1048608 | tf_op jit(solution)/shard_map/ppermute | solution.py:31
  49.2 0.2 broadcast_select_fusion.1
  49.4 0.1 slice_select_fusion
  49.5 1.4 collective-permute-start.1
  50.9 0.0 collective-permute-done.3
  50.9 1.9 %broadcast_select_fusion = f32[896,512]{1,0:T(8,128)S(1)} fusion(f32[896,512]{1,0:T(8,128)} %collective-permute-done.3, pred[]{:T(512)S(6)} %eq.30, f32[4096,512]{1,0:T(8,128)} %shard_map.68), kind=kLoop, calls=%fused_computation.8 | loop fusion | flops 458752 | bytes 5505025 | tf_op jit(solution)/shard_map/jit(_where)/select_n | solution.py:55
  52.8 1.3 collective-permute-start.4
  54.1 10.3 %collective-permute-done.1 = f32[256,512]{0,1:T(8,128)} collective-permute-done((f32[256,512]{0,1:T(8,128)S(1)}, f32[256,512]{0,1:T(8,128)}, u32[]{:S(2)}, u32[]{:S(2)}) %collective-permute-start.1) | collective-permute-done | bytes 524320 | tf_op jit(solution)/shard_map/ppermute | solution.py:38
  64.4 0.1 broadcast_select_fusion.2
  64.5 0.1 collective-permute-start.2
  64.6 1.0 slice.63
  65.6 1.0 broadcast_in_dim.19
  66.6 2.2 %scatter_fusion.1 = f32[16,16,896]{2,1,0:T(8,128)} fusion(f32[16,16,896]{2,1,0:T(8,128)} %broadcast_in_dim.19, s32[4]{0:T(128)S(1)} %fusion.6, f32[4,16,896]{2,1,0:T(8,128)S(1)} %slice.63), kind=kCustom, calls=%fused_computation.1 | custom fusion | bytes 688144 | tf_op jit(solution)/shard_map/scatter | solution.py:20
  68.7 4.4 %all-to-all-start.1 = ((f32[8,2,16,896]{3,2,1,0:T(8,128)}), f32[8,2,16,896]{3,2,1,0:T(8,128)}, u32[]{:S(2)}, u32[]{:S(2)}) async-start(f32[8,2,16,896]{3,2,1,0:T(8,128)} %bitcast.13), calls=%async_computation.1 | async-start | bytes 1835008 | tf_op jit(solution)/shard_map/all_to_all | solution.py:217
  73.1 0.0 collective-permute-done.2
  73.1 1.4 maximum_select_fusion
  74.5 1.3 copy.25
  75.8 2.4 %fusion.2.s_ref = f32[512,512]{1,0:T(8,128)} fusion(f32[512,512]{1,0:T(8,128)} %copy.25, f32[512,512]{0,1:T(8,128)S(1)} %maximum_select_fusion), kind=kLoop, calls=%fused_computation.7 | loop fusion | flops 524288 | bytes 3145728 | tf_op jit(solution)/shard_map/mul | solution.py:224
  78.2 41.4 %shard_map.69 = (f32[512,512]{1,0:T(8,128)}, f32[512,512]{1,0:T(8,128)}) custom-call(f32[512,512]{1,0:T(8,128)} %fusion.2.s_ref), custom_call_target="tpu_custom_call" | custom-call | tf_op jit(solution)/shard_map/pallas_call | solution.py:131
  119.6 0.0 copy-start.1
  119.6 10.8 %fusion.7.solved_ref = f32[4096,512]{1,0:T(8,128)S(1)} fusion(f32[4096,512]{1,0:T(8,128)} %shard_map.68, f32[512,512]{1,0:T(8,128)} %get-tuple-element.17), kind=kOutput, calls=%fused_computation.24 | convolution fusion | flops 6442450944 | bytes 17825792 | tf_op jit(solution)/shard_map/dot_general | solution.py:226
  130.5 0.0 copy-start
  130.5 0.0 collective-permute-done.4
  130.5 0.0 copy-done.1
  130.5 3.6 %fusion = f32[896,512]{1,0:T(8,128)} fusion(f32[512,512]{1,0:T(8,128)S(1)} %copy-done.1, f32[896,512]{1,0:T(8,128)S(1)} %broadcast_select_fusion, f32[896,512]{1,0:T(8,128)} %collective-permute-done.4, pred[]{:T(512)S(6)} %eq.32), kind=kOutput, calls=%fused_computation.3 | convolution fusion | flops 1409744896 | bytes 6553601 | tf_op jit(solution)/shard_map/dot_general | solution.py:227
  134.2 0.3 copy-done
  134.4 18.5 %slice_subtract_fusion.base_ref = f32[4096,896]{1,0:T(8,128)} fusion(f32[4096,1408]{1,0:T(8,128)} %bitcast.39, f32[4096,512]{1,0:T(8,128)S(1)} %fusion.7.solved_ref, f32[896,512]{1,0:T(8,128)} %fusion), kind=kOutput, calls=%fused_computation.2 | convolution fusion | flops 11277959168 | bytes 39583744 | tf_op jit(solution)/shard_map/dot_general | solution.py:228
  153.0 0.0 all-to-all-done.1
  153.0 14.0 %shard_map.71 = f32[4096,896]{1,0:T(8,128)} custom-call(s32[256]{0:T(256)} %convert_element_type.24.idx_ref, f32[4096,896]{1,0:T(8,128)} %slice_subtract_fusion.base_ref, f32[256,896]{1,0:T(8,128)} %bitcast.14.add_ref), custom_call_target="tpu_custom_call" | custom-call | tf_op jit(solution)/shard_map/pallas_call | solution.py:163
  167.0 2.2 %shard_map.70 = f32[4096,512]{1,0:T(8,128)} custom-call(s32[1]{0:T(128)} %bitcast.1.flag_ref, f32[512,512]{1,0:T(8,128)} %get-tuple-element.16.factor_ref, f32[4096,512]{1,0:T(8,128)} %copy-done), custom_call_target="tpu_custom_call", output_to_operand_aliasing={{}: (2, {})} | custom-call | tf_op jit(solution)/shard_map/pallas_call | solution.py:185
  (2 shorter events, 0.1 us)
Async XLA Ops:
  43.9 7.0 %collective-permute-start.3 = (f32[896,512]{1,0:T(8,128)}, f32[896,512]{1,0:T(8,128)}, u32[]{:S(2)}, u32[]{:S(2)}) collective-permute-start(f32[896,512]{1,0:T(8,128)} %slice.62), channel_id=1, source_target_pairs={{0,1},{1,0},{2,3},{3,2},{4,5},{5,4},{6,7},{7,6},{8,9},{9,8},{10,11... | collective-permute-start | bytes 5505032 | tf_op jit(solution)/shard_map/ppermute | solution.py:54
  45.5 3.6 %collective-permute-start = (f32[512,512]{0,1:T(8,128)S(1)}, f32[512,512]{0,1:T(8,128)S(1)}, u32[]{:S(2)}, u32[]{:S(2)}) collective-permute-start(f32[512,512]{0,1:T(8,128)S(1)} %copy.26), channel_id=1, source_target_pairs={{0,1},{1,0},{2,3},{3,2},{4,5},{5,4},{6,7},{7,6},{8,9},{9,8},{10,11... | collective-permute-start | bytes 3145736 | tf_op jit(solution)/shard_map/ppermute | solution.py:31
  49.5 14.9 %collective-permute-start.1 = (f32[256,512]{0,1:T(8,128)S(1)}, f32[256,512]{0,1:T(8,128)}, u32[]{:S(2)}, u32[]{:S(2)}) collective-permute-start(f32[256,512]{0,1:T(8,128)S(1)} %slice_select_fusion), channel_id=1, source_target_pairs={{0,2},{1,3},{2,0},{3,1},{4,6},{5,7},{6,4},{7,5},{8,10},{9,11},{10,... | collective-permute-start | bytes 1572872 | tf_op jit(solution)/shard_map/ppermute | solution.py:38
  52.8 77.7 %collective-permute-start.4 = (f32[896,512]{1,0:T(8,128)S(1)}, f32[896,512]{1,0:T(8,128)}, u32[]{:S(2)}, u32[]{:S(2)}) collective-permute-start(f32[896,512]{1,0:T(8,128)S(1)} %broadcast_select_fusion), channel_id=1, source_target_pairs={{0,2},{1,3},{2,0},{3,1},{4,6},{5,7},{6,4},{7,5},{8,10},{9,11},{10,... | collective-permute-start | bytes 5505032 | tf_op jit(solution)/shard_map/ppermute | solution.py:54
  64.5 8.6 %collective-permute-start.2 = (f32[256,512]{0,1:T(8,128)S(1)}, f32[256,512]{0,1:T(8,128)}, u32[]{:S(2)}, u32[]{:S(2)}) collective-permute-start(f32[256,512]{0,1:T(8,128)S(1)} %broadcast_select_fusion.2), channel_id=1, source_target_pairs={{0,1},{1,0},{2,3},{3,2},{4,5},{5,4},{6,7},{7,6},{8,9},{9,8},{10,11... | collective-permute-start | bytes 1572872 | tf_op jit(solution)/shard_map/ppermute | solution.py:41
  68.7 84.3 %all-to-all-start.1 = ((f32[8,2,16,896]{3,2,1,0:T(8,128)}), f32[8,2,16,896]{3,2,1,0:T(8,128)}, u32[]{:S(2)}, u32[]{:S(2)}) async-start(f32[8,2,16,896]{3,2,1,0:T(8,128)} %bitcast.13), calls=%async_computation.1 | async-start | bytes 1835008 | tf_op jit(solution)/shard_map/all_to_all | solution.py:217
  119.6 10.9 %copy-start.1 = (f32[512,512]{1,0:T(8,128)S(1)}, f32[512,512]{1,0:T(8,128)}, u32[]{:S(2)}) copy-start(f32[512,512]{1,0:T(8,128)} %get-tuple-element.17) | copy-start | bytes 3145732
  130.5 4.0 %copy-start = (f32[4096,512]{1,0:T(8,128)}, f32[4096,512]{1,0:T(8,128)S(1)}, u32[]{:S(2)}) copy-start(f32[4096,512]{1,0:T(8,128)S(1)} %fusion.7.solved_ref) | copy-start | bytes 25165828

commit v16 on v14

--- a/solution.py
+++ b/solution.py
@@ -67,7 +67,8 @@
 def _factor_kernel(s_ref, l_ref, inv_ref, w_ref, d_ref, dt_ref, di_ref):
     n = s_ref.shape[0]
     nb = n // BLK
-    w_ref[...] = s_ref[...]
+    pivot = s_ref[...]
+    w_ref[...] = 0.5 * (pivot + pivot.T)
     l_ref[...] = jnp.zeros_like(l_ref)
     inv_ref[...] = jnp.zeros_like(inv_ref)
     sub = lax.broadcasted_iota(jnp.int32, (BLK, BLK), 0)
@@ -212,8 +213,7 @@
 
     pivot_block = broadcast_from(panel_part[:PB], owner_index, "grp")
     window_rows = broadcast_whole(panel_part[PB:PB + win_cols], owner_index, "grp")
-    symmetric = 0.5 * (pivot_block + pivot_block.T)
-    pivot_factor, factor_inverse = factor_and_inverse(symmetric)
+    pivot_factor, factor_inverse = factor_and_inverse(pivot_block)
     solved = jnp.dot(panel_part, factor_inverse.T, precision=FAST)
     window = jnp.dot(window_rows, factor_inverse.T, precision=FAST)
     schur_part = local_rows[:, PB:] - jnp.dot(solved, window.T, precision=FAST)

time: 171 us -> 168 us (0.982)
  local copies, waits for them, and re-layouts: 13.5 us -> 10.6 us
    mul x1 -> x0, other arithmetic: 2.41 us -> none  [local(): symmetric = 0.5 * (pivot_block + pivot_block.T)]
  transfers between devices with their start and end apart: 6 -> 6, of which waited for: 2 -> 2; matrix products, arithmetic and copies ran while one was open for 27% -> 26% of each run, Pallas kernels for 24% -> 25%
where the time goes in v16:
time: 168 us; the launch traced here: 166 us
  Pallas kernels  66.9 us (40%)
  matrix products  33 us (20%)
  blocking collectives  24.8 us (15%)
  waiting for transfers between devices  13.1 us (8%)
  local copies, waits for them, and re-layouts  10.6 us (6%)
  starting transfers between devices  8.3 us (5%)
  other arithmetic  7.3 us (4%)
    pallas_call x1, Pallas kernels, factor_and_inverse(): pl.pallas_call(_factor_kernel, out_shape=(jax.ShapeDtypeStruct((n, n), jn...  41.6 us
    all_to_all x1, blocking collectives, local(): lax.all_to_all(send_panel, 'front', split_axis=0, concat_axis=0, tiled=True)  24.8 us
    pallas_call x2, Pallas kernels, add_rows(): pl.pallas_call(functools.partial(_block_add_kernel, col0), out_shape=jax....  23.1 us
    dot_general x1, matrix products, local(): schur_part = local_rows[:, PB:] - jnp.dot(solved, window.T, precision=FAST)  18.5 us
    dot_general x1, matrix products, local(): solved = jnp.dot(panel_part, factor_inverse.T, precision=FAST)  10.8 us
    ppermute x1, waiting for transfers between devices, broadcast_from(): got = lax.ppermute(half, axis, pairs(size, bit))  10.2 us
    all_to_all x1, starting transfers between devices, local(): lax.all_to_all(send_trail, 'front', split_axis=0, concat_axis=0, tiled=True)  4.84 us
    dot_general x1, matrix products, local(): window = jnp.dot(window_rows, factor_inverse.T, precision=FAST)  3.64 us
  transfers between devices with their start and end apart: 6, of which 2 were waited for; matrix products, arithmetic and copies ran while one was open for 26% of the time, Pallas kernels for 25%

profile of v16, /device:TPU:0, one launch (start us, length us, event | category | flops | bytes accessed | tf_op | source)
XLA Modules:
  0.0 165.6 jit_solution(5946427524068924035)
XLA Ops:
  0.6 0.9 convert_reduce_fusion
  1.5 0.7 fusion.5
  2.2 0.7 convert_bitcast_fusion
  2.9 0.1 copy.16
  3.0 0.9 slice.55
  4.0 0.7 scatter_fusion
  4.6 24.8 %all_to_all.10 = f32[8,2,16,640]{3,2,1,0:T(8,128)S(1)} all-to-all(f32[8,2,16,640]{3,2,1,0:T(8,128)S(1)} %bitcast.37), channel_id=1, replica_groups=mesh['front'=8,'grp'=4] {'front'}, dimensions={0} | all-to-all | bytes 1310720 | tf_op jit(solution)/shard_map/all_to_all | solution.py:204
  29.4 0.4 fusion.3
  29.8 0.7 convert_element_type.24.idx_ref
  30.4 0.9 slice.57
  31.3 9.4 %shard_map.68 = f32[4096,512]{1,0:T(8,128)} custom-call(s32[256]{0:T(256)} %convert_element_type.24.idx_ref, f32[4096,1408]{1,0:T(8,128)} %bitcast.34, f32[256,512]{1,0:T(8,128)} %bitcast.38), custom_call_target="tpu_custom_call" | custom-call | tf_op jit(solution)/shard_map/pallas_call | solution.py:155
  40.7 1.6 slice.62
  42.4 0.1 collective-permute-start.3
  42.5 1.3 slice.58
  43.8 0.6 collective-permute-start
  45.0 2.9 %collective-permute-done = f32[512,512]{1,0:T(8,128)} collective-permute-done((f32[512,512]{1,0:T(8,128)S(1)}, f32[512,512]{1,0:T(8,128)}, u32[]{:S(2)}, u32[]{:S(2)}) %collective-permute-start) | collective-permute-done | bytes 1048608 | tf_op jit(solution)/shard_map/ppermute | solution.py:30
  47.9 1.4 broadcast_select_fusion.1
  49.3 0.1 slice_select_fusion
  49.4 2.1 %collective-permute-start.1 = (f32[256,512]{1,0:T(8,128)S(1)}, f32[256,512]{1,0:T(8,128)}, u32[]{:S(2)}, u32[]{:S(2)}) collective-permute-start(f32[256,512]{1,0:T(8,128)S(1)} %slice_select_fusion), channel_id=1, source_target_pairs={{0,2},{1,3},{2,0},{3,1},{4,6},{5,7},{6,4},{7,5},{8,10},{9,11},{10,... | collective-permute-start | bytes 1572872 | tf_op jit(solution)/shard_map/ppermute | solution.py:37
  51.5 0.0 collective-permute-done.3
  51.5 1.9 %broadcast_select_fusion = f32[896,512]{1,0:T(8,128)S(1)} fusion(f32[896,512]{1,0:T(8,128)} %collective-permute-done.3, pred[]{:T(512)S(6)} %eq.30, f32[4096,512]{1,0:T(8,128)} %shard_map.68), kind=kLoop, calls=%fused_computation.6 | loop fusion | flops 458752 | bytes 5505025 | tf_op jit(solution)/shard_map/jit(_where)/select_n | solution.py:54
  53.4 0.6 collective-permute-start.4
  54.1 10.2 %collective-permute-done.1 = f32[256,512]{1,0:T(8,128)} collective-permute-done((f32[256,512]{1,0:T(8,128)S(1)}, f32[256,512]{1,0:T(8,128)}, u32[]{:S(2)}, u32[]{:S(2)}) %collective-permute-start.1) | collective-permute-done | bytes 524320 | tf_op jit(solution)/shard_map/ppermute | solution.py:37
  64.3 0.1 broadcast_select_fusion.2
  64.5 0.1 collective-permute-start.2
  64.5 1.0 slice.63
  65.5 1.0 broadcast_in_dim.19
  66.5 2.2 %scatter_fusion.1 = f32[16,16,896]{2,1,0:T(8,128)} fusion(f32[16,16,896]{2,1,0:T(8,128)} %broadcast_in_dim.19, s32[4]{0:T(128)S(1)} %fusion.5, f32[4,16,896]{2,1,0:T(8,128)S(1)} %slice.63), kind=kCustom, calls=%fused_computation.1 | custom fusion | bytes 688144 | tf_op jit(solution)/shard_map/scatter | solution.py:19
  68.7 4.8 %all-to-all-start.1 = ((f32[8,2,16,896]{3,2,1,0:T(8,128)}), f32[8,2,16,896]{3,2,1,0:T(8,128)}, u32[]{:S(2)}, u32[]{:S(2)}) async-start(f32[8,2,16,896]{3,2,1,0:T(8,128)} %bitcast.12), calls=%async_computation.1 | async-start | bytes 1835008 | tf_op jit(solution)/shard_map/all_to_all | solution.py:209
  73.5 0.0 collective-permute-done.2
  73.5 1.1 maximum_select_fusion.s_ref
  74.6 41.6 %shard_map.69 = (f32[512,512]{1,0:T(8,128)}, f32[512,512]{1,0:T(8,128)}) custom-call(f32[512,512]{1,0:T(8,128)} %maximum_select_fusion.s_ref), custom_call_target="tpu_custom_call" | custom-call | tf_op jit(solution)/shard_map/pallas_call | solution.py:131
  116.2 0.0 copy-start.1
  116.2 10.8 %fusion.6.solved_ref = f32[4096,512]{1,0:T(8,128)S(1)} fusion(f32[4096,512]{1,0:T(8,128)} %shard_map.68, f32[512,512]{1,0:T(8,128)} %get-tuple-element.17), kind=kOutput, calls=%fused_computation.22 | convolution fusion | flops 6442450944 | bytes 17825792 | tf_op jit(solution)/shard_map/dot_general | solution.py:217
  127.1 0.0 copy-start
  127.1 0.0 collective-permute-done.4
  127.1 0.0 copy-done.1
  127.1 3.6 %fusion = f32[896,512]{1,0:T(8,128)} fusion(f32[512,512]{1,0:T(8,128)S(1)} %copy-done.1, f32[896,512]{1,0:T(8,128)S(1)} %broadcast_select_fusion, f32[896,512]{1,0:T(8,128)} %collective-permute-done.4, pred[]{:T(512)S(6)} %eq.32), kind=kOutput, calls=%fused_computation.3 | convolution fusion | flops 1409744896 | bytes 6553601 | tf_op jit(solution)/shard_map/dot_general | solution.py:218
  130.8 0.3 copy-done
  131.0 18.5 %slice_subtract_fusion.base_ref = f32[4096,896]{1,0:T(8,128)} fusion(f32[4096,1408]{1,0:T(8,128)} %bitcast.35, f32[4096,512]{1,0:T(8,128)S(1)} %fusion.6.solved_ref, f32[896,512]{1,0:T(8,128)} %fusion), kind=kOutput, calls=%fused_computation.2 | convolution fusion | flops 11277959168 | bytes 39583744 | tf_op jit(solution)/shard_map/dot_general | solution.py:219
  149.6 0.0 all-to-all-done.1
  149.6 13.7 %shard_map.71 = f32[4096,896]{1,0:T(8,128)} custom-call(s32[256]{0:T(256)} %convert_element_type.24.idx_ref, f32[4096,896]{1,0:T(8,128)} %slice_subtract_fusion.base_ref, f32[256,896]{1,0:T(8,128)} %bitcast.13.add_ref), custom_call_target="tpu_custom_call" | custom-call | tf_op jit(solution)/shard_map/pallas_call | solution.py:155
  163.3 2.2 %shard_map.70 = f32[4096,512]{1,0:T(8,128)} custom-call(s32[1]{0:T(128)} %bitcast.1.flag_ref, f32[512,512]{1,0:T(8,128)} %get-tuple-element.16.factor_ref, f32[4096,512]{1,0:T(8,128)} %copy-done), custom_call_target="tpu_custom_call", output_to_operand_aliasing={{}: (2, {})} | custom-call | tf_op jit(solution)/shard_map/pallas_call | solution.py:177
  (2 shorter events, 0.1 us)
Async XLA Ops:
  42.4 9.1 %collective-permute-start.3 = (f32[896,512]{1,0:T(8,128)S(1)}, f32[896,512]{1,0:T(8,128)}, u32[]{:S(2)}, u32[]{:S(2)}) collective-permute-start(f32[896,512]{1,0:T(8,128)S(1)} %slice.62), channel_id=1, source_target_pairs={{0,1},{1,0},{2,3},{3,2},{4,5},{5,4},{6,7},{7,6},{8,9},{9,8},{10,11... | collective-permute-start | bytes 5505032 | tf_op jit(solution)/shard_map/ppermute | solution.py:53
  43.8 4.1 %collective-permute-start = (f32[512,512]{1,0:T(8,128)S(1)}, f32[512,512]{1,0:T(8,128)}, u32[]{:S(2)}, u32[]{:S(2)}) collective-permute-start(f32[512,512]{1,0:T(8,128)S(1)} %slice.58), channel_id=1, source_target_pairs={{0,1},{1,0},{2,3},{3,2},{4,5},{5,4},{6,7},{7,6},{8,9},{9,8},{10,11... | collective-permute-start | bytes 3145736 | tf_op jit(solution)/shard_map/ppermute | solution.py:30
  49.4 14.9 %collective-permute-start.1 = (f32[256,512]{1,0:T(8,128)S(1)}, f32[256,512]{1,0:T(8,128)}, u32[]{:S(2)}, u32[]{:S(2)}) collective-permute-start(f32[256,512]{1,0:T(8,128)S(1)} %slice_select_fusion), channel_id=1, source_target_pairs={{0,2},{1,3},{2,0},{3,1},{4,6},{5,7},{6,4},{7,5},{8,10},{9,11},{10,... | collective-permute-start | bytes 1572872 | tf_op jit(solution)/shard_map/ppermute | solution.py:37
  53.4 73.7 %collective-permute-start.4 = (f32[896,512]{1,0:T(8,128)S(1)}, f32[896,512]{1,0:T(8,128)}, u32[]{:S(2)}, u32[]{:S(2)}) collective-permute-start(f32[896,512]{1,0:T(8,128)S(1)} %broadcast_select_fusion), channel_id=1, source_target_pairs={{0,2},{1,3},{2,0},{3,1},{4,6},{5,7},{6,4},{7,5},{8,10},{9,11},{10,... | collective-permute-start | bytes 5505032 | tf_op jit(solution)/shard_map/ppermute | solution.py:53
  64.5 9.1 %collective-permute-start.2 = (f32[256,512]{1,0:T(8,128)S(1)}, f32[256,512]{1,0:T(8,128)S(1)}, u32[]{:S(2)}, u32[]{:S(2)}) collective-permute-start(f32[256,512]{1,0:T(8,128)S(1)} %broadcast_select_fusion.2), channel_id=1, source_target_pairs={{0,1},{1,0},{2,3},{3,2},{4,5},{5,4},{6,7},{7,6},{8,9},{9,8},{10,11... | collective-permute-start | bytes 1572872 | tf_op jit(solution)/shard_map/ppermute | solution.py:40
  68.7 80.9 %all-to-all-start.1 = ((f32[8,2,16,896]{3,2,1,0:T(8,128)}), f32[8,2,16,896]{3,2,1,0:T(8,128)}, u32[]{:S(2)}, u32[]{:S(2)}) async-start(f32[8,2,16,896]{3,2,1,0:T(8,128)} %bitcast.12), calls=%async_computation.1 | async-start | bytes 1835008 | tf_op jit(solution)/shard_map/all_to_all | solution.py:209
  116.2 10.9 %copy-start.1 = (f32[512,512]{1,0:T(8,128)S(1)}, f32[512,512]{1,0:T(8,128)}, u32[]{:S(2)}) copy-start(f32[512,512]{1,0:T(8,128)} %get-tuple-element.17) | copy-start | bytes 3145732
  127.1 4.0 %copy-start = (f32[4096,512]{1,0:T(8,128)}, f32[4096,512]{1,0:T(8,128)S(1)}, u32[]{:S(2)}) copy-start(f32[4096,512]{1,0:T(8,128)S(1)} %fusion.6.solved_ref) | copy-start | bytes 25165828

commit v17 on v16

--- a/solution.py
+++ b/solution.py
@@ -45,6 +45,23 @@
     )
 
 
+def broadcast_halves(x, owner, axis):
+    size = lax.axis_size(axis)
+    me = lax.axis_index(axis)
+    got = lax.ppermute(x, axis, pairs(size, 1))
+    x = jnp.where(me == owner, x, got)
+    half_rows = x.shape[0] // 2
+    core = me % 2
+    half = jnp.where(core == 0, x[:half_rows], x[half_rows:])
+    bit = 2
+    while bit < size:
+        got = lax.ppermute(half, axis, pairs(size, bit))
+        half = jnp.where(me // bit == owner // bit, half, got)
+        bit *= 2
+    other = lax.ppermute(half, axis, pairs(size, 1))
+    return half, other, (core == 0).astype(jnp.int32).reshape(1)
+
+
 def broadcast_whole(x, owner, axis):
     size = lax.axis_size(axis)
     me = lax.axis_index(axis)
@@ -64,10 +81,13 @@
     return lax.dot_general(a, b, (((1,), (1,)), ((), ())), precision=EXACT, preferred_element_type=jnp.float32)
 
 
-def _factor_kernel(s_ref, l_ref, inv_ref, w_ref, d_ref, dt_ref, di_ref):
-    n = s_ref.shape[0]
+def _factor_kernel(first_ref, mine_ref, other_ref, l_ref, inv_ref, w_ref, d_ref, dt_ref, di_ref):
+    n = l_ref.shape[0]
     nb = n // BLK
-    pivot = s_ref[...]
+    first = first_ref[0] == 1
+    mine = mine_ref[...]
+    other = other_ref[...]
+    pivot = jnp.concatenate([jnp.where(first, mine, other), jnp.where(first, other, mine)], axis=0)
     w_ref[...] = 0.5 * (pivot + pivot.T)
     l_ref[...] = jnp.zeros_like(l_ref)
     inv_ref[...] = jnp.zeros_like(inv_ref)
@@ -126,15 +146,15 @@
             inv_ref[i * BLK:(i + 1) * BLK, j * BLK:(j + 1) * BLK] = -_mm(inv_diag[i], acc)
 
 
-def factor_and_inverse(sym):
-    n = sym.shape[0]
+def factor_and_inverse(mine, other, first):
+    n = mine.shape[1]
     return pl.pallas_call(
         _factor_kernel,
         out_shape=(jax.ShapeDtypeStruct((n, n), jnp.float32), jax.ShapeDtypeStruct((n, n), jnp.float32)),
-        in_specs=[pl.BlockSpec(memory_space=pltpu.VMEM)],
+        in_specs=[pl.BlockSpec(memory_space=pltpu.SMEM)] + [pl.BlockSpec(memory_space=pltpu.VMEM)] * 2,
         out_specs=(pl.BlockSpec(memory_space=pltpu.VMEM), pl.BlockSpec(memory_space=pltpu.VMEM)),
         scratch_shapes=[pltpu.VMEM((n, n), jnp.float32)] + [pltpu.VMEM((BLK, BLK), jnp.float32)] * 3,
-    )(sym)
+    )(first, mine, other)
 
 
 def _block_add_kernel(col0, idx_ref, base_ref, add_ref, out_ref, sem):
@@ -211,9 +231,9 @@
     owner_index = panel_owner[0]
     is_owner = lax.axis_index("grp") == owner_index
 
-    pivot_block = broadcast_from(panel_part[:PB], owner_index, "grp")
+    pivot_mine, pivot_other, pivot_first = broadcast_halves(panel_part[:PB], owner_index, "grp")
     window_rows = broadcast_whole(panel_part[PB:PB + win_cols], owner_index, "grp")
-    pivot_factor, factor_inverse = factor_and_inverse(pivot_block)
+    pivot_factor, factor_inverse = factor_and_inverse(pivot_mine, pivot_other, pivot_first)
     solved = jnp.dot(panel_part, factor_inverse.T, precision=FAST)
     window = jnp.dot(window_rows, factor_inverse.T, precision=FAST)
     schur_part = local_rows[:, PB:] - jnp.dot(solved, window.T, precision=FAST)

time: 168 us -> 168 us (level); the launches traced: 166 us -> 167 us
  matrix products: 33 us -> 35.3 us
    dot_general x1, matrix products: 3.64 us -> 5.79 us  [local(): window = jnp.dot(window_rows, factor_inverse.T, precision=FAST)]
  transfers between devices with their start and end apart: 6 -> 6, of which waited for: 2 -> 2; matrix products, arithmetic and copies ran while one was open for 26% -> 28% of each run, Pallas kernels for 25% -> 25%
where the time goes in v17:
time: 168 us; the launch traced here: 167 us
  Pallas kernels  66 us (39%)
  matrix products  35.3 us (21%)
  blocking collectives  24.8 us (15%)
  waiting for transfers between devices  13.2 us (8%)
  local copies, waits for them, and re-layouts  11.2 us (7%)
  other arithmetic  8.12 us (5%)
  starting transfers between devices  7.26 us (4%)
    pallas_call x1, Pallas kernels, factor_and_inverse(): pl.pallas_call(_factor_kernel, out_shape=(jax.ShapeDtypeStruct((n, n), jn...  41.5 us
    all_to_all x1, blocking collectives, local(): lax.all_to_all(send_panel, 'front', split_axis=0, concat_axis=0, tiled=True)  24.8 us
    pallas_call x2, Pallas kernels, add_rows(): pl.pallas_call(functools.partial(_block_add_kernel, col0), out_shape=jax....  23.2 us
    dot_general x1, matrix products, local(): schur_part = local_rows[:, PB:] - jnp.dot(solved, window.T, precision=FAST)  18.5 us
    dot_general x1, matrix products, local(): solved = jnp.dot(panel_part, factor_inverse.T, precision=FAST)  11 us
    ppermute x1, waiting for transfers between devices, broadcast_halves(): got = lax.ppermute(half, axis, pairs(size, bit))  10.3 us
    dot_general x1, matrix products, local(): window = jnp.dot(window_rows, factor_inverse.T, precision=FAST)  5.79 us
    all_to_all x1, starting transfers between devices, local(): lax.all_to_all(send_trail, 'front', split_axis=0, concat_axis=0, tiled=True)  4.41 us
  transfers between devices with their start and end apart: 6, of which 2 were waited for; matrix products, arithmetic and copies ran while one was open for 28% of the time, Pallas kernels for 25%

profile of v17, /device:TPU:0, one launch (start us, length us, event | category | flops | bytes accessed | tf_op | source)
XLA Modules:
  0.0 167.5 jit_solution(1546798276487042343)
XLA Ops:
  0.6 0.9 convert_reduce_fusion
  1.5 0.7 fusion.5
  2.2 0.7 convert_bitcast_fusion
  2.9 0.1 copy.16
  3.0 0.9 slice.55
  4.0 0.7 scatter_fusion
  4.6 24.8 %all_to_all.10 = f32[8,2,16,640]{3,2,1,0:T(8,128)S(1)} all-to-all(f32[8,2,16,640]{3,2,1,0:T(8,128)S(1)} %bitcast.38), channel_id=1, replica_groups=mesh['front'=8,'grp'=4] {'front'}, dimensions={0} | all-to-all | bytes 1310720 | tf_op jit(solution)/shard_map/all_to_all | solution.py:224
  29.4 0.4 fusion.3
  29.8 0.7 convert_element_type.25.idx_ref
  30.4 0.9 slice.57
  31.3 9.5 %shard_map.68 = f32[4096,512]{1,0:T(8,128)} custom-call(s32[256]{0:T(256)} %convert_element_type.25.idx_ref, f32[4096,1408]{1,0:T(8,128)} %bitcast.35, f32[256,512]{1,0:T(8,128)} %bitcast.39), custom_call_target="tpu_custom_call" | custom-call | tf_op jit(solution)/shard_map/pallas_call | solution.py:175
  40.8 1.6 slice.62
  42.4 0.1 collective-permute-start.3
  42.5 1.3 slice.58
  43.8 0.6 collective-permute-start
  45.0 2.9 %collective-permute-done = f32[512,512]{1,0:T(8,128)} collective-permute-done((f32[512,512]{1,0:T(8,128)S(1)}, f32[512,512]{1,0:T(8,128)}, u32[]{:S(2)}, u32[]{:S(2)}) %collective-permute-start) | collective-permute-done | bytes 1048608 | tf_op jit(solution)/shard_map/ppermute | solution.py:51
  47.9 1.8 %broadcast_select_fusion.1 = f32[512,512]{1,0:T(8,128)S(1)} fusion(f32[512,512]{1,0:T(8,128)} %collective-permute-done, pred[]{:T(512)S(6)} %eq.30, f32[4096,512]{1,0:T(8,128)} %shard_map.68), kind=kLoop, calls=%fused_computation.8 | loop fusion | flops 262144 | bytes 3145729 | tf_op jit(solution)/shard_map/jit(_where)/select_n | solution.py:52
  49.6 0.1 slice_select_fusion
  49.7 1.6 collective-permute-start.1
  51.4 0.0 collective-permute-done.3
  51.4 2.5 %broadcast_select_fusion = f32[896,512]{1,0:T(8,128)S(1)} fusion(f32[896,512]{1,0:T(8,128)} %collective-permute-done.3, pred[]{:T(512)S(6)} %eq.30, f32[4096,512]{1,0:T(8,128)} %shard_map.68), kind=kLoop, calls=%fused_computation.5 | loop fusion | flops 458752 | bytes 5505025 | tf_op jit(solution)/shard_map/jit(_where)/select_n | solution.py:71
  53.9 0.5 collective-permute-start.4
  54.4 10.3 %collective-permute-done.1 = f32[256,512]{1,0:T(8,128)} collective-permute-done((f32[256,512]{1,0:T(8,128)S(1)}, f32[256,512]{1,0:T(8,128)}, u32[]{:S(2)}, u32[]{:S(2)}) %collective-permute-start.1) | collective-permute-done | bytes 524320 | tf_op jit(solution)/shard_map/ppermute | solution.py:58
  64.7 1.2 broadcast_select_fusion.2.mine_ref
  65.9 0.0 copy-start.2
  65.9 0.1 collective-permute-start.2
  66.0 1.1 slice.63
  67.0 1.0 broadcast_in_dim.19
  68.0 2.2 %scatter_fusion.1 = f32[16,16,896]{2,1,0:T(8,128)} fusion(f32[16,16,896]{2,1,0:T(8,128)} %broadcast_in_dim.19, s32[4]{0:T(128)S(1)} %fusion.5, f32[4,16,896]{2,1,0:T(8,128)S(1)} %slice.63), kind=kCustom, calls=%fused_computation.1 | custom fusion | bytes 688144 | tf_op jit(solution)/shard_map/scatter | solution.py:19
  70.2 4.4 %all-to-all-start.1 = ((f32[8,2,16,896]{3,2,1,0:T(8,128)}), f32[8,2,16,896]{3,2,1,0:T(8,128)}, u32[]{:S(2)}, u32[]{:S(2)}) async-start(f32[8,2,16,896]{3,2,1,0:T(8,128)} %bitcast.13), calls=%async_computation.1 | async-start | bytes 1835008 | tf_op jit(solution)/shard_map/all_to_all | solution.py:229
  74.6 0.0 collective-permute-done.2.other_ref
  74.7 0.0 copy-start.3
  74.7 0.0 copy-done.2
  74.7 0.8 copy-done.3
  75.5 41.5 %shard_map.69 = (f32[512,512]{1,0:T(8,128)}, f32[512,512]{1,0:T(8,128)}) custom-call(s32[1]{0:T(128)} %bitcast.2.first_ref, f32[256,512]{1,0:T(8,128)} %copy-done.2, f32[256,512]{1,0:T(8,128)} %copy-done.3), custom_call_target="tpu_custom_call" | custom-call | tf_op jit(solution)/shard_map/pallas_call | solution.py:151
  117.0 0.0 copy-start.1
  117.0 11.0 %fusion.6.solved_ref = f32[4096,512]{1,0:T(8,128)S(1)} fusion(f32[4096,512]{1,0:T(8,128)} %shard_map.68, f32[512,512]{1,0:T(8,128)} %get-tuple-element.17), kind=kOutput, calls=%fused_computation.21 | convolution fusion | flops 6442450944 | bytes 17825792 | tf_op jit(solution)/shard_map/dot_general | solution.py:237
  128.0 0.0 copy-start
  128.0 0.0 collective-permute-done.4
  128.0 0.0 copy-done.1
  128.0 5.8 %fusion = f32[896,512]{1,0:T(8,128)} fusion(f32[512,512]{1,0:T(8,128)S(1)} %copy-done.1, f32[896,512]{1,0:T(8,128)S(1)} %broadcast_select_fusion, f32[896,512]{1,0:T(8,128)} %collective-permute-done.4, pred[]{:T(512)S(6)} %eq.32), kind=kOutput, calls=%fused_computation.3 | convolution fusion | flops 1409744896 | bytes 6553601 | tf_op jit(solution)/shard_map/dot_general | solution.py:238
  133.8 0.0 copy-done
  133.8 18.5 %slice_subtract_fusion.base_ref = f32[4096,896]{1,0:T(8,128)} fusion(f32[4096,1408]{1,0:T(8,128)} %bitcast.36, f32[4096,512]{1,0:T(8,128)S(1)} %fusion.6.solved_ref, f32[896,512]{1,0:T(8,128)} %fusion), kind=kOutput, calls=%fused_computation.2 | convolution fusion | flops 11277959168 | bytes 39583744 | tf_op jit(solution)/shard_map/dot_general | solution.py:239
  152.3 0.0 all-to-all-done.1
  152.3 13.7 %shard_map.71 = f32[4096,896]{1,0:T(8,128)} custom-call(s32[256]{0:T(256)} %convert_element_type.25.idx_ref, f32[4096,896]{1,0:T(8,128)} %slice_subtract_fusion.base_ref, f32[256,896]{1,0:T(8,128)} %bitcast.14.add_ref), custom_call_target="tpu_custom_call" | custom-call | tf_op jit(solution)/shard_map/pallas_call | solution.py:175
  166.1 1.2 shard_map.70
  (2 shorter events, 0.1 us)
Async XLA Ops:
  42.4 9.0 %collective-permute-start.3 = (f32[896,512]{1,0:T(8,128)S(1)}, f32[896,512]{1,0:T(8,128)}, u32[]{:S(2)}, u32[]{:S(2)}) collective-permute-start(f32[896,512]{1,0:T(8,128)S(1)} %slice.62), channel_id=1, source_target_pairs={{0,1},{1,0},{2,3},{3,2},{4,5},{5,4},{6,7},{7,6},{8,9},{9,8},{10,11... | collective-permute-start | bytes 5505032 | tf_op jit(solution)/shard_map/ppermute | solution.py:70
  43.8 4.1 %collective-permute-start = (f32[512,512]{1,0:T(8,128)S(1)}, f32[512,512]{1,0:T(8,128)}, u32[]{:S(2)}, u32[]{:S(2)}) collective-permute-start(f32[512,512]{1,0:T(8,128)S(1)} %slice.58), channel_id=1, source_target_pairs={{0,1},{1,0},{2,3},{3,2},{4,5},{5,4},{6,7},{7,6},{8,9},{9,8},{10,11... | collective-permute-start | bytes 3145736 | tf_op jit(solution)/shard_map/ppermute | solution.py:51
  49.7 14.9 %collective-permute-start.1 = (f32[256,512]{1,0:T(8,128)S(1)}, f32[256,512]{1,0:T(8,128)}, u32[]{:S(2)}, u32[]{:S(2)}) collective-permute-start(f32[256,512]{1,0:T(8,128)S(1)} %slice_select_fusion), channel_id=1, source_target_pairs={{0,2},{1,3},{2,0},{3,1},{4,6},{5,7},{6,4},{7,5},{8,10},{9,11},{10,... | collective-permute-start | bytes 1572872 | tf_op jit(solution)/shard_map/ppermute | solution.py:58
  53.9 74.2 %collective-permute-start.4 = (f32[896,512]{1,0:T(8,128)S(1)}, f32[896,512]{1,0:T(8,128)}, u32[]{:S(2)}, u32[]{:S(2)}) collective-permute-start(f32[896,512]{1,0:T(8,128)S(1)} %broadcast_select_fusion), channel_id=1, source_target_pairs={{0,2},{1,3},{2,0},{3,1},{4,6},{5,7},{6,4},{7,5},{8,10},{9,11},{10,... | collective-permute-start | bytes 5505032 | tf_op jit(solution)/shard_map/ppermute | solution.py:70
  65.9 8.8 %copy-start.2 = (f32[256,512]{1,0:T(8,128)}, f32[256,512]{1,0:T(8,128)S(1)}, u32[]{:S(2)}) copy-start(f32[256,512]{1,0:T(8,128)S(1)} %broadcast_select_fusion.2.mine_ref) | copy-start | bytes 1572868
  65.9 8.8 %collective-permute-start.2 = (f32[256,512]{1,0:T(8,128)S(1)}, f32[256,512]{1,0:T(8,128)S(1)}, u32[]{:S(2)}, u32[]{:S(2)}) collective-permute-start(f32[256,512]{1,0:T(8,128)S(1)} %broadcast_select_fusion.2.mine_ref), channel_id=1, source_target_pairs={{0,1},{1,0},{2,3},{3,2},{4,5},{5,4},{6,7},{7,6},{8,9},{9,8},{10,11... | collective-permute-start | bytes 1572872 | tf_op jit(solution)/shard_map/ppermute | solution.py:61
  70.2 82.1 %all-to-all-start.1 = ((f32[8,2,16,896]{3,2,1,0:T(8,128)}), f32[8,2,16,896]{3,2,1,0:T(8,128)}, u32[]{:S(2)}, u32[]{:S(2)}) async-start(f32[8,2,16,896]{3,2,1,0:T(8,128)} %bitcast.13), calls=%async_computation.1 | async-start | bytes 1835008 | tf_op jit(solution)/shard_map/all_to_all | solution.py:229
  74.7 0.8 copy-start.3
  117.0 11.0 %copy-start.1 = (f32[512,512]{1,0:T(8,128)S(1)}, f32[512,512]{1,0:T(8,128)}, u32[]{:S(2)}) copy-start(f32[512,512]{1,0:T(8,128)} %get-tuple-element.17) | copy-start | bytes 3145732
  128.0 5.8 %copy-start = (f32[4096,512]{1,0:T(8,128)}, f32[4096,512]{1,0:T(8,128)S(1)}, u32[]{:S(2)}) copy-start(f32[4096,512]{1,0:T(8,128)S(1)} %fusion.6.solved_ref) | copy-start | bytes 25165828
